TPU v7x, 256 devices: a whole 4x4x8 slice. The times are simulated.
256 devices in a mesh: seq: 32 (over y, x, z_lo), tensor: 8 (over z_hi, core).
Axes of the slice: x: 4, y: 4, z: 8 (z_hi: 4, z_lo: 2; z = z_hi * 2 + z_lo), core: 2. Of those that a mesh axis runs over, the one named last changes fastest.
Arguments:
- residual: bfloat16 [4096, 2048], P('seq', 'tensor'), may hold values from -10 to 10
- queries: bfloat16 [4096, 2048], P('seq', 'tensor'), may hold values from -5 to 5
- new_keys: bfloat16 [4096, 2048], P('seq', 'tensor'), may hold values from -5 to 5
- new_values: bfloat16 [4096, 2048], P('seq', 'tensor'), may hold values from -6 to 6
- cache_keys: bfloat16 [8, 16384, 2048], P(None, 'seq', 'tensor'), may hold values from -5 to 5
- cache_values: bfloat16 [8, 16384, 2048], P(None, 'seq', 'tensor'), may hold values from -6 to 6
- cache_lengths: int32 [8], replicated, may hold values from 1 to 16384, 23552 in all
- out_proj: bfloat16 [2048, 2048], P('tensor'), may hold values from -0.125 to 0.125
- norm_gain: float32 [2048], P('tensor'), may hold values from 0.5 to 1.5
- router: bfloat16 [2048, 64], P('tensor'), may hold values from -0.3984375 to 0.3984375
- expert_ids: int32 [4096, 6], P('seq'), may hold values from 0 to 63, all different within a row; in each aligned block of 128 rows (0 to 127, 128 to 255, ...) at most 16 rows name the same one
- expert_gate_up: bfloat16 [64, 2048, 2, 1408], P('seq', None, None, 'tensor'), may hold values from -0.125 to 0.125
- expert_down: bfloat16 [64, 1408, 2048], P('seq', 'tensor'), may hold values from -0.15625 to 0.15625
- shared_gate_up: bfloat16 [2048, 2, 1408], P(None, None, 'tensor'), may hold values from -0.125 to 0.125
- shared_down: bfloat16 [1408, 2048], P('tensor'), may hold values from -0.15625 to 0.15625
Outputs:
- layer_out: bfloat16 [4096, 2048], P('seq', 'tensor')
Inputs may be any that keep to these rules, and one draw needn't show every extreme that they name: Request r's cached tokens are positions 0 to cache_lengths[r] - 1 of its row of 16384 cache positions; the lengths sum to 16384 + 7 * (1024) and the longest equals 16384. `expert_ids`: each row names 6 different experts. Among the 128 rows of one index of seq no expert is named by more than 16 rows, and this bound is reached.
All inputs are finite; a program needn't handle non-finite values.
Results may differ from a plain program's by a relative error of at most 0.025.
Values may be sent and summed in bfloat16 or wider, within the bound.
No kernel may reach another device: no remote copies, remote signals or barrier semaphores. Data moves between devices by JAX's collectives and lax.ppermute only.
A program may use at most 128 MiB of HBM per device.

v0:
```python
import math

import jax
import jax.numpy as jnp
from jax import lax
from jax.sharding import PartitionSpec as P

D = 2048
HD = 128
NEW = 512


negative = -1e30
epsilon = 1e-06


def block_partial(scores, visible, values):
    masked = jnp.where(visible, scores, negative)
    block_max = jnp.max(masked, -1)
    shifted = jnp.where(visible, scores, block_max[..., None]) - block_max[..., None]
    weights = jnp.where(visible, jnp.exp(shifted), 0.0)
    block_sum = jnp.sum(weights, -1)
    block_out = jnp.einsum(
        "hqk,khd->qhd", weights.astype(jnp.bfloat16), values, preferred_element_type=jnp.float32
    )
    return (block_max, block_sum, block_out)


def shards(
    residual,
    queries,
    new_keys,
    new_values,
    cache_keys,
    cache_values,
    cache_lengths,
    out_proj,
    norm_gain,
    router,
    expert_ids,
    expert_gate_up,
    expert_down,
    shared_gate_up,
    shared_down,
):
    seq_count = lax.axis_size("seq")
    tensor_count = lax.axis_size("tensor")
    seq_index = lax.axis_index("seq")
    tok_dev = queries.shape[0]
    heads_local = queries.shape[1] // HD
    requests = tok_dev * seq_count // NEW
    clen_dev = cache_keys.shape[1]
    tokens = tok_dev * seq_count
    width_local = residual.shape[1]
    experts = router.shape[1]
    exp_dev = expert_gate_up.shape[0]
    topk = expert_ids.shape[1]
    scaling = 1.0 / math.sqrt(HD)
    every_query = lax.all_gather(queries, "seq", axis=0, tiled=True)
    grouped = every_query.reshape(requests, NEW, heads_local, HD)
    first_place = seq_index * clen_dev

    def cached_part(request):
        query_block, key_block, value_block, length = request
        scores = (
            jnp.einsum("qhd,khd->hqk", query_block, key_block, preferred_element_type=jnp.float32)
            * scaling
        )
        visible = (first_place + lax.iota(jnp.int32, clen_dev) < length)[None, None, :]
        return block_partial(scores, visible, value_block)

    max_cached, sum_cached, out_cached = lax.map(
        cached_part,
        (
            grouped,
            cache_keys.reshape(requests, clen_dev, heads_local, HD),
            cache_values.reshape(requests, clen_dev, heads_local, HD),
            cache_lengths,
        ),
    )
    max_cached = jnp.transpose(max_cached, (0, 2, 1))
    sum_cached = jnp.transpose(sum_cached, (0, 2, 1))
    own_start = seq_index * tok_dev
    own_request = own_start // NEW
    offset = own_start % NEW
    own_queries = lax.dynamic_index_in_dim(grouped, own_request, 0, keepdims=False)
    new_scores = (
        jnp.einsum(
            "qhd,khd->hqk",
            own_queries,
            new_keys.reshape(tok_dev, heads_local, HD),
            preferred_element_type=jnp.float32,
        )
        * scaling
    )
    visible_new = (
        lax.iota(jnp.int32, NEW)[:, None] >= offset + lax.iota(jnp.int32, tok_dev)[None, :]
    )[None]
    max_new, sum_new, out_new = block_partial(
        new_scores, visible_new, new_values.reshape(tok_dev, heads_local, HD)
    )
    chosen_request = (lax.iota(jnp.int32, requests) == own_request)[:, None, None]
    max_placed = jnp.where(chosen_request, jnp.transpose(max_new)[None], negative)
    sum_placed = jnp.where(chosen_request, jnp.transpose(sum_new)[None], 0.0)
    out_placed = jnp.where(chosen_request[..., None], out_new[None], 0.0)
    local_max = jnp.maximum(max_cached, max_placed)
    factor_cached = jnp.exp(max_cached - local_max)
    factor_new = jnp.exp(max_placed - local_max)
    local_sum = sum_cached * factor_cached + sum_placed * factor_new
    local_out = out_cached * factor_cached[..., None] + out_placed * factor_new[..., None]
    flat_max = local_max.reshape(tokens, heads_local)
    row_max = lax.pmax(flat_max.astype(jnp.bfloat16), "seq").astype(flat_max.dtype)
    factors = jnp.exp(flat_max - row_max)
    weighted, row_sum = (
        lax.psum_scatter(
            (local_out.reshape(tokens, heads_local, HD) * factors[..., None]).astype(jnp.bfloat16),
            "seq",
            scatter_dimension=0,
            tiled=True,
        ).astype(jnp.float32),
        lax.psum_scatter(
            (local_sum.reshape(tokens, heads_local) * factors).astype(jnp.bfloat16),
            "seq",
            scatter_dimension=0,
            tiled=True,
        ).astype(jnp.float32),
    )
    attended = (
        (weighted / row_sum[..., None]).astype(jnp.bfloat16).reshape(tok_dev, heads_local * HD)
    )
    projected = jnp.dot(attended, out_proj, preferred_element_type=jnp.float32)
    attn_out = lax.psum_scatter(
        projected.astype(jnp.bfloat16), "tensor", scatter_dimension=1, tiled=True
    ).astype(jnp.float32)
    stream = residual.astype(jnp.float32) + attn_out
    square_total = lax.psum(jnp.sum(stream * stream, 1), "tensor")
    inverse_rms = lax.rsqrt(square_total / D + epsilon)
    normed = (stream * inverse_rms[:, None] * norm_gain).astype(jnp.bfloat16)
    logits = lax.psum(
        jnp.dot(normed, router, preferred_element_type=jnp.float32).astype(jnp.bfloat16), "tensor"
    ).astype(jnp.float32)
    matches = expert_ids[:, :, None] == lax.iota(jnp.int32, experts)[None, None, :]
    selected = jnp.sum(jnp.where(matches, logits[:, None, :], 0.0), 2)
    sigmoids = jax.nn.sigmoid(selected)
    gates = sigmoids / jnp.sum(sigmoids, 1, keepdims=True)
    normed_full = lax.all_gather(normed, "tensor", axis=1, tiled=True)
    shared_pair = jnp.einsum(
        "td,dcf->tcf", normed_full, shared_gate_up, preferred_element_type=jnp.float32
    )
    shared_act = (jax.nn.silu(shared_pair[:, 0]) * shared_pair[:, 1]).astype(jnp.bfloat16)
    shared_term = jnp.dot(shared_act, shared_down, preferred_element_type=jnp.float32)
    shared_out = lax.psum_scatter(
        shared_term.astype(jnp.bfloat16), "tensor", scatter_dimension=1, tiled=True
    ).astype(jnp.float32)
    cap = tensor_count * (
        (4 * tok_dev * topk + 3 * experts * tensor_count - 1) // (3 * experts * tensor_count)
    )
    flat_ids = expert_ids.reshape(-1)
    marks = (flat_ids[:, None] == lax.iota(jnp.int32, experts)[None, :]).astype(jnp.int32)
    earlier = jnp.cumsum(marks, 0) - marks
    rank = jnp.sum(earlier * marks, 1)
    slot_index = flat_ids * cap + rank
    source_rows = (
        jnp.full((experts * cap,), tok_dev, jnp.int32)
        .at[slot_index]
        .set(lax.iota(jnp.int32, flat_ids.shape[0]) // topk)
    )
    padded_local = jnp.concatenate([normed, jnp.zeros((1, width_local), jnp.bfloat16)], 0)
    outgoing = padded_local[source_rows].reshape(seq_count, exp_dev, cap, width_local)
    incoming = lax.all_to_all(outgoing, "seq", split_axis=0, concat_axis=0, tiled=True)
    routed_rows = lax.all_gather(incoming, "tensor", axis=3, tiled=True)
    expert_pair = jnp.einsum(
        "secd,edjf->secjf", routed_rows, expert_gate_up, preferred_element_type=jnp.float32
    )
    expert_act = (jax.nn.silu(expert_pair[..., 0, :]) * expert_pair[..., 1, :]).astype(jnp.bfloat16)
    expert_term = jnp.einsum(
        "secf,efd->secd", expert_act, expert_down, preferred_element_type=jnp.float32
    )
    expert_total = lax.psum_scatter(
        expert_term.astype(jnp.bfloat16), "tensor", scatter_dimension=3, tiled=True
    )
    returned = lax.all_to_all(expert_total, "seq", split_axis=0, concat_axis=0, tiled=True)
    picked = returned.reshape(experts * cap, width_local)[slot_index].reshape(
        tok_dev, topk, width_local
    )
    mixture = jnp.sum(gates[..., None] * picked.astype(jnp.float32), 1)
    return (stream + shared_out + mixture).astype(jnp.bfloat16)


def solution(mesh):
    in_specs = (
        P("seq", "tensor"),
        P("seq", "tensor"),
        P("seq", "tensor"),
        P("seq", "tensor"),
        P(None, "seq", "tensor"),
        P(None, "seq", "tensor"),
        P(),
        P("tensor", None),
        P("tensor"),
        P("tensor", None),
        P("seq", None),
        P("seq", None, None, "tensor"),
        P("seq", "tensor", None),
        P(None, None, "tensor"),
        P("tensor", None),
    )
    out_specs = P("seq", "tensor")
    return jax.shard_map(shards, mesh=mesh, in_specs=in_specs, out_specs=out_specs, check_vma=False)
```

profile of v0, /device:TPU:65, one launch (start us, length us, event | category | flops | bytes accessed | tf_op | source)
XLA Modules:
  0.0 1000.6 jit_solution(4869210231114567954)
XLA Ops:
  7.3 4.0 copy.98
  11.3 3.9 copy.99
  15.4 132.9 %all-gather.3.cloned.1.call-done = bf16[4096,256]{1,0:T(8,128)(2,1)} async-done(((bf16[128,256]{1,0:T(8,128)(2,1)}), bf16[4096,256]{1,0:T(8,128)(2,1)}) %all-gather.3.cloned.1.call-update) | async-done | bytes 2097168 | tf_op jit(solution)/shard_map/all_gather | solution.py:59
  148.3 4.0 reshape.198
  152.3 77.6 %while.15 = (s32[]{:T(128)}, f32[8,2,512]{2,1,0:T(2,128)S(1)}, f32[8,2,512]{2,1,0:T(2,128)}, f32[8,512,2,128]{3,1,0,2:T(8,128)}, s32[]{:T(128)}, /*index=5*/s32[...) while((s32[]{:T(128)}, f32[8,2,512]{2,1,0:T(2,128)S(1)}, ...), condition=%wide.region_3.4_spmd.clone, body=%wide.region_0.3_spmd.sunk.clone | while | flops 275250176 | bytes 10258573 | solution.py:72
  154.7 1.5 select_reduce_fusion.5
  157.4 2.5 convolution_bitcast_fusion.4
  164.5 1.5 select_reduce_fusion.5
  167.1 2.5 convolution_bitcast_fusion.4
  174.2 1.5 select_reduce_fusion.5
  176.8 2.5 convolution_bitcast_fusion.4
  183.9 1.5 select_reduce_fusion.5
  186.5 2.5 convolution_bitcast_fusion.4
  193.6 1.5 select_reduce_fusion.5
  196.2 2.5 convolution_bitcast_fusion.4
  203.3 1.5 select_reduce_fusion.5
  205.9 2.5 convolution_bitcast_fusion.4
  213.0 1.5 select_reduce_fusion.5
  215.6 2.5 convolution_bitcast_fusion.4
  222.7 1.5 select_reduce_fusion.5
  225.3 2.5 convolution_bitcast_fusion.4
  233.5 130.5 %pmax.7 = bf16[4096,2]{0,1:T(2,128)(2,1)} all-reduce(bf16[4096,2]{0,1:T(2,128)(2,1)S(1)} %convert_element_type.81), channel_id=1, replica_groups=mesh['seq'=32,'tensor'=8] {'seq'}, use_global_device_ids=true, to_apply=%region_5.6 | all-reduce | flops 8192 | bytes 32768 | tf_op jit(solution)/shard_map/pmax | solution.py:112
  366.2 4.5 multiply_add_fusion
  370.8 2.5 fusion.17
  374.3 179.3 %reduce-scatter.16.cloned.1.call-done = bf16[128,2]{1,0:T(8,128)(2,1)} async-done(((bf16[4096,2]{1,0:T(8,128)(2,1)}), bf16[128,2]{1,0:T(8,128)(2,1)}) %reduce-scatter.16.cloned.1.call-update) | async-done | bytes 528
  554.5 166.6 %reduce-scatter.8.cloned.1.call-done = bf16[128,2,128]{2,0,1:T(8,128)(2,1)} async-done(((bf16[4096,2,128]{2,0,1:T(8,128)(2,1)}), bf16[128,2,128]{2,0,1:T(8,128)(2,1)}) %reduce-scatter.8.cloned.1.call-update) | async-done | bytes 65552 | tf_op jit(solution)/shard_map/reduce_scatter | solution.py:115
  722.1 2.4 convolution_convert_fusion.1
  724.8 1.8 reduce-window.6
  727.1 3.4 scatter_custom_fusion
  730.5 51.2 %reduce-scatter.10.cloned.1.call-done = bf16[128,256]{1,0:T(8,128)(2,1)} async-done(((bf16[128,2048]{1,0:T(8,128)(2,1)}), bf16[128,256]{1,0:T(8,128)(2,1)}) %reduce-scatter.10.cloned.1.call-update) | async-done | bytes 65552 | tf_op jit(solution)/shard_map/reduce_scatter | solution.py:132
  782.7 13.7 %psum.14 = f32[128]{0:T(128)S(1)} all-reduce(f32[128]{0:T(128)S(1)} %multiply_reduce_fusion.1), channel_id=1, replica_groups=mesh['seq'=32,'tensor'=8] {'tensor'}, use_global_device_ids=true, to_apply=%region_11.12 | all-reduce | flops 128 | bytes 1024 | tf_op jit(solution)/shard_map/psum | solution.py:136
  797.4 3.9 gather_fusion
  801.3 19.3 %all_to_all.10 = bf16[32,2,16,256]{3,2,1,0:T(8,128)(2,1)S(1)} all-to-all(bf16[32,2,16,256]{3,2,1,0:T(8,128)(2,1)S(1)} %bitcast.174), channel_id=1, replica_groups=mesh['seq'=32,'tensor'=8] {'seq'}, dimensions={0} | all-to-all | bytes 1048576 | tf_op jit(solution)/shard_map/all_to_all | solution.py:170
  821.7 53.9 %all-gather.5.cloned.1.call-done = bf16[32,2,16,2048]{3,2,0,1:T(8,128)(2,1)} async-done(((bf16[32,2,16,256]{3,2,0,1:T(8,128)(2,1)}), bf16[32,2,16,2048]{3,2,0,1:T(8,128)(2,1)}) %all-gather.5.cloned.1.call-update) | async-done | bytes 4194320 | tf_op jit(solution)/shard_map/all_gather | solution.py:171
  875.6 4.6 fusion.19
  880.2 3.2 convert_bitcast_fusion
  883.5 15.6 %all_gather.10 = bf16[128,2048]{1,0:T(8,128)(2,1)S(1)} all-gather(bf16[128,256]{1,0:T(8,128)(2,1)S(1)} %multiply_convert_fusion), channel_id=1, replica_groups=mesh['seq'=32,'tensor'=8] {'tensor'}, dimensions={1}, use_global_device_ids=true | all-gather | bytes 589824 | tf_op jit(solution)/shard_map/all_gather | solution.py:146
  899.1 2.6 fusion.62
  901.7 39.3 %reduce-scatter.14.cloned.1.call-done = bf16[32,2,16,256]{3,2,0,1:T(8,128)(2,1)} async-done(((bf16[32,2,16,2048]{3,2,0,1:T(8,128)(2,1)}), bf16[32,2,16,256]{3,2,0,1:T(8,128)(2,1)}) %reduce-scatter.14.cloned.1.call-update) | async-done | bytes 524304 | tf_op jit(solution)/shard_map/reduce_scatter | solution.py:179
  940.9 1.9 copy.118
  942.8 6.9 all-to-all-start.1
  949.8 2.4 convolution_convert_fusion
  952.3 26.9 %psum.15 = bf16[128,64]{0,1:T(8,128)(2,1)S(1)} all-reduce(bf16[128,64]{0,1:T(8,128)(2,1)S(1)} %convolution_convert_fusion.2), channel_id=1, replica_groups=mesh['seq'=32,'tensor'=8] {'tensor'}, use_global_device_ids=true, to_apply=%region_13.14 | all-reduce | flops 8192 | bytes 32768 | tf_op jit(solution)/shard_map/psum | solution.py:139
  979.5 3.3 gather_fusion.1
  982.7 2.1 reshape.167
  984.8 1.6 multiply_reduce_fusion
  986.5 5.8 reduce-scatter.12.cloned.1.call-done
  992.3 1.5 add_convert_fusion
  (142 shorter events, 59.3 us)
Async XLA Ops:
  6.5 869.0 %copy-start = (bf16[2,2048,2,176]{1,3,2,0:T(8,128)(2,1)S(1)}, bf16[2,2048,2,176]{1,3,2,0:T(8,128)(2,1)}, u32[]{:S(2)}) copy-start(bf16[2,2048,2,176]{1,3,2,0:T(8,128)(2,1)} %param.28) | copy-start | bytes 8650756
  6.5 141.8 %all-gather.3.cloned.1.call-start = ((), (), s32[]{:S(2)}) async-start(), calls=%async_computation.7 | async-start | bytes 2162688 | tf_op jit(solution)/shard_map/all_gather | solution.py:59
  7.3 546.4 %reduce-scatter.16.cloned.1.call-start = ((), (), s32[]{:S(2)}) async-start(), calls=%async_computation.13 | async-start | bytes 1081344
  15.3 217.1 %copy-start.8 = (pred[8]{0:T(512)(128)(4,1)}, pred[8]{0:T(512)(128)(4,1)S(1)}, u32[]{:S(2)}) copy-start(pred[8]{0:T(512)(128)(4,1)S(1)} %iota_compare_fusion.4) | copy-start | bytes 28
  15.4 136.9 %copy-start.12 = (s32[8]{0:T(128)S(1)}, s32[8]{0:T(128)}, u32[]{:S(2)}) copy-start(s32[8]{0:T(128)} %param.23) | copy-start | bytes 100
  229.9 2.4 copy-start.7
  229.9 3.2 copy-start.4
  364.8 1.5 copy-start.9
  366.2 354.9 %reduce-scatter.8.cloned.1.call-start = ((), (), s32[]{:S(2)}) async-start(), calls=%async_computation.8 | async-start | bytes 2162688 | tf_op jit(solution)/shard_map/reduce_scatter | solution.py:115
  373.3 0.7 copy-start.5
  373.3 408.5 %copy-start.1 = (bf16[128,256]{1,0:T(8,128)(2,1)S(1)}, bf16[128,256]{1,0:T(8,128)(2,1)}, u32[]{:S(2)}) copy-start(bf16[128,256]{1,0:T(8,128)(2,1)} %param.17) | copy-start | bytes 196612
  373.3 423.1 %copy-start.10 = (f32[256]{0:T(256)S(1)}, f32[256]{0:T(256)}, u32[]{:S(2)}) copy-start(f32[256]{0:T(256)} %param.25) | copy-start | bytes 3076
  373.3 408.4 %reduce-scatter.10.cloned.1.call-start = ((), (), s32[]{:S(2)}) async-start(), calls=%async_computation.9 | async-start | bytes 589824 | tf_op jit(solution)/shard_map/reduce_scatter | solution.py:132
  724.5 151.1 %all-gather.5.cloned.1.call-start = ((), (), s32[]{:S(2)}) async-start(), calls=%async_computation.11 | async-start | bytes 4718592 | tf_op jit(solution)/shard_map/all_gather | solution.py:171
  821.5 119.5 %reduce-scatter.14.cloned.1.call-start = ((), (), s32[]{:S(2)}) async-start(), calls=%async_computation.12 | async-start | bytes 4718592 | tf_op jit(solution)/shard_map/reduce_scatter | solution.py:179
  875.6 4.7 copy-start.11
  901.7 50.5 %copy-start.6 = (bf16[256,64]{0,1:T(8,128)(2,1)S(1)}, bf16[256,64]{0,1:T(8,128)(2,1)}, u32[]{:S(2)}) copy-start(bf16[256,64]{0,1:T(8,128)(2,1)} %param.26) | copy-start | bytes 98308
  942.8 36.6 %all-to-all-start.1 = ((bf16[32,2,16,256]{3,2,1,0:T(8,128)(2,1)}), bf16[32,2,16,256]{3,2,1,0:T(8,128)(2,1)S(1)}, u32[]{:S(2)}, u32[]{:S(2)}) async-start(bf16[32,2,16,256]{3,2,1,0:T(8,128)(2,1)} %copy.118), calls=%async_computation.5 | async-start | bytes 1048576 | tf_op jit(solution)/shard_map/all_to_all | solution.py:182
  949.7 42.6 %reduce-scatter.12.cloned.1.call-start = ((), (), s32[]{:S(2)}) async-start(), calls=%async_computation.10 | async-start | bytes 589824 | tf_op jit(solution)/shard_map/reduce_scatter | solution.py:152
  982.7 9.6 copy-start.2
  982.7 9.6 copy-start.3
Sparse Core Ops, SparseCore 0:
  9.1 139.1 all-gather.2
  366.3 187.2 reduce-scatter.15
  556.2 164.8 reduce-scatter.7
  724.6 57.1 reduce-scatter.9
  821.6 53.9 all-gather.4
  883.6 57.3 reduce-scatter.13
  953.0 39.2 reduce-scatter.11
where the time goes:
time: 1000 us
  waiting for transfers between devices  630 us (63%)
  blocking collectives  206 us (21%)
  local copies, waits for them, and re-layouts  68.2 us (7%)
  matrix products  48.5 us (5%)
  other arithmetic  26.8 us (3%)
  between operations  13.8 us (1%)
    unnamed x8, waiting for transfers between devices  180 us
    reduce_scatter x1, waiting for transfers between devices, shards(): lax.psum_scatter((local_out.reshape(tokens, heads_local, HD) * factors[.....  167 us
    all_gather x1, waiting for transfers between devices, shards(): every_query = lax.all_gather(queries, 'seq', axis=0, tiled=True)  133 us
    pmax x1, blocking collectives, shards(): lax.pmax(flat_max.astype(jnp.bfloat16), 'seq').astype(flat_max.dtype)  130 us
    all_gather x1, waiting for transfers between devices, shards(): routed_rows = lax.all_gather(incoming, 'tensor', axis=3, tiled=True)  53.9 us
    reduce_scatter x1, waiting for transfers between devices, shards(): lax.psum_scatter(projected.astype(jnp.bfloat16), 'tensor', scatter_dimens...  51.2 us
    reduce_scatter x1, waiting for transfers between devices, shards(): lax.psum_scatter(expert_term.astype(jnp.bfloat16), 'tensor', scatter_dime...  39.3 us
    psum x1, blocking collectives, shards(): lax.psum(jnp.dot(normed, router, preferred_element_type=jnp.float32).asty...  26.9 us
  transfers between devices with their start and end apart: 8, of which 7 were waited for; matrix products, arithmetic and copies ran while one was open for 3% of the time, Pallas kernels for 0%

commit v1 on v0

--- a/solution.py
+++ b/solution.py
@@ -56,7 +56,8 @@
     exp_dev = expert_gate_up.shape[0]
     topk = expert_ids.shape[1]
     scaling = 1.0 / math.sqrt(HD)
-    every_query = lax.all_gather(queries, "seq", axis=0, tiled=True)
+    spread = jnp.broadcast_to(queries[None], (seq_count,) + queries.shape)
+    every_query = lax.all_to_all(spread, "seq", 0, 0, tiled=True).reshape(tokens, width_local)
     grouped = every_query.reshape(requests, NEW, heads_local, HD)
     first_place = seq_index * clen_dev
 
@@ -108,23 +109,23 @@
     factor_new = jnp.exp(max_placed - local_max)
     local_sum = sum_cached * factor_cached + sum_placed * factor_new
     local_out = out_cached * factor_cached[..., None] + out_placed * factor_new[..., None]
-    flat_max = local_max.reshape(tokens, heads_local)
-    row_max = lax.pmax(flat_max.astype(jnp.bfloat16), "seq").astype(flat_max.dtype)
-    factors = jnp.exp(flat_max - row_max)
-    weighted, row_sum = (
-        lax.psum_scatter(
-            (local_out.reshape(tokens, heads_local, HD) * factors[..., None]).astype(jnp.bfloat16),
-            "seq",
-            scatter_dimension=0,
-            tiled=True,
-        ).astype(jnp.float32),
-        lax.psum_scatter(
-            (local_sum.reshape(tokens, heads_local) * factors).astype(jnp.bfloat16),
-            "seq",
-            scatter_dimension=0,
-            tiled=True,
-        ).astype(jnp.float32),
-    )
+    flat_max = local_max.reshape(seq_count, tok_dev, heads_local)
+    flat_sum = local_sum.reshape(seq_count, tok_dev, heads_local)
+    stats = lax.all_to_all(
+        jnp.stack([flat_max, flat_sum], -1), "seq", 0, 0, tiled=True
+    )
+    parts_out = lax.all_to_all(
+        local_out.reshape(seq_count, tok_dev, heads_local, HD).astype(jnp.bfloat16),
+        "seq",
+        0,
+        0,
+        tiled=True,
+    ).astype(jnp.float32)
+    part_max = stats[..., 0]
+    row_max = jnp.max(part_max, 0)
+    factors = jnp.exp(part_max - row_max[None])
+    row_sum = jnp.sum(stats[..., 1] * factors, 0)
+    weighted = jnp.sum(parts_out * factors[..., None], 0)
     attended = (
         (weighted / row_sum[..., None]).astype(jnp.bfloat16).reshape(tok_dev, heads_local * HD)
     )

time: 1000 us -> 463 us (0.46)
  waiting for transfers between devices: 630 us -> 180 us
  blocking collectives: 206 us -> 75.6 us
  local copies, waits for them, and re-layouts: 68.2 us -> 89.1 us
  starting transfers between devices: 7.29 us -> 25.3 us
    unnamed x8 -> x4, waiting for transfers between devices: 180 us -> 0.07 us
    reduce_scatter x1 -> x0, waiting for transfers between devices: 167 us -> none  [shards(): lax.psum_scatter((local_out.reshape(tokens, heads_local, HD) * factors[.....]
    all_gather x1 -> x0, waiting for transfers between devices: 133 us -> none  [shards(): every_query = lax.all_gather(queries, 'seq', axis=0, tiled=True)]
    pmax x1 -> x0, blocking collectives: 130 us -> none  [shards(): lax.pmax(flat_max.astype(jnp.bfloat16), 'seq').astype(flat_max.dtype)]
    all_to_all x0 -> x3, waiting for transfers between devices: none -> 46.6 us  [the longest x1 25.2 us: shards(): lax.all_to_all(local_out.reshape(seq_count, tok_dev, heads_local, HD).ast...]
    all_to_all x0 -> x3, starting transfers between devices: none -> 19.2 us  [the longest x1 8.52 us: shards(): lax.all_to_all(spread, 'seq', 0, 0, tiled=True).reshape(tokens, width_local)]
    dynamic_update_slice x24 -> x48, local copies, waits for them, and re-layouts: 21.4 us -> 38.8 us  [shards(): lax.map(cached_part, (grouped, cache_keys.reshape(requests, clen_dev, hea...]
    reduce_scatter x1, waiting for transfers between devices: 51.2 us -> 33.9 us  [shards(): lax.psum_scatter(projected.astype(jnp.bfloat16), 'tensor', scatter_dimens...]
  transfers between devices with their start and end apart: 8 -> 8, of which waited for: 7 -> 7; matrix products, arithmetic and copies ran while one was open for 3% -> 7% of each run, Pallas kernels for 0% -> 0%
where the time goes in v1:
time: 463 us; the launch traced here: 459 us
  waiting for transfers between devices  180 us (39%)
  local copies, waits for them, and re-layouts  89.1 us (19%)
  blocking collectives  75.6 us (16%)
  matrix products  50.8 us (11%)
  starting transfers between devices  25.3 us (5%)
  other arithmetic  24.3 us (5%)
  between operations  13.5 us (3%)
    all_gather x1, waiting for transfers between devices, shards(): routed_rows = lax.all_gather(incoming, 'tensor', axis=3, tiled=True)  54.1 us
    reduce_scatter x1, waiting for transfers between devices, shards(): lax.psum_scatter(expert_term.astype(jnp.bfloat16), 'tensor', scatter_dime...  39.9 us
    dynamic_update_slice x48, local copies, waits for them, and re-layouts, shards(): lax.map(cached_part, (grouped, cache_keys.reshape(requests, clen_dev, hea...  38.8 us
    reduce_scatter x1, waiting for transfers between devices, shards(): lax.psum_scatter(projected.astype(jnp.bfloat16), 'tensor', scatter_dimens...  33.9 us
    psum x1, blocking collectives, shards(): lax.psum(jnp.dot(normed, router, preferred_element_type=jnp.float32).asty...  26.8 us
    all_to_all x1, waiting for transfers between devices, shards(): lax.all_to_all(local_out.reshape(seq_count, tok_dev, heads_local, HD).ast...  25.2 us
    dot_general x9, matrix products, block_partial(): jnp.einsum('hqk,khd->qhd', weights.astype(jnp.bfloat16), values, preferre...  21.8 us
    all_to_all x1, waiting for transfers between devices, shards(): lax.all_to_all(spread, 'seq', 0, 0, tiled=True).reshape(tokens, width_local)  20.2 us
  transfers between devices with their start and end apart: 8, of which 7 were waited for; matrix products, arithmetic and copies ran while one was open for 7% of the time, Pallas kernels for 0%

profile of v1, /device:TPU:65, one launch (start us, length us, event | category | flops | bytes accessed | tf_op | source)
XLA Modules:
  0.0 459.4 jit_solution(8734745967000259575)
XLA Ops:
  7.6 1.8 broadcast_in_dim.180
  9.4 8.5 %all-to-all-start = ((bf16[32,128,256]{1,2,0:T(8,128)(2,1)}), bf16[32,128,256]{1,2,0:T(8,128)(2,1)}, u32[]{:S(2)}, u32[]{:S(2)}) async-start(bf16[32,128,256]{1,2,0:T(8,128)(2,1)} %broadcast_in_dim.180), calls=%async_computation | async-start | bytes 4194304 | tf_op jit(solution)/shard_map/all_to_all | solution.py:60
  18.0 3.9 copy.147
  22.0 3.9 copy.148
  26.0 20.2 %all-to-all-done = bf16[32,128,256]{1,2,0:T(8,128)(2,1)} async-done(((bf16[32,128,256]{1,2,0:T(8,128)(2,1)}), bf16[32,128,256]{1,2,0:T(8,128)(2,1)}, u32[]{:S(2)}, u32[]{:S(2)}) %all-to-all-start) | async-done | bytes 2097184 | tf_op jit(solution)/shard_map/all_to_all | solution.py:60
  46.2 4.2 copy.146
  50.4 4.4 reshape_reshape.3
  54.8 4.6 copy.150
  59.4 2.1 constant_dynamic-slice_fusion
  63.9 2.0 convolution_bitcast_fusion.1
  65.9 84.8 %while.15 = (s32[]{:T(128)}, f32[8,2,512]{2,0,1:T(8,128)}, f32[8,2,512]{2,0,1:T(8,128)}, f32[8,512,2,128]{3,1,0,2:T(8,128)}, s32[]{:T(128)}, /*index=5*/s32[8]{0...) while((s32[]{:T(128)}, f32[8,2,512]{2,0,1:T(8,128)}, ...), condition=%wide.region_3.4_spmd.clone, body=%wide.region_0.3_spmd.sunk.clone | while | flops 275250176 | bytes 9751689 | solution.py:73
  69.1 2.5 convolution_bitcast_fusion.4
  79.7 2.5 convolution_bitcast_fusion.4
  90.3 2.5 convolution_bitcast_fusion.4
  100.9 2.5 convolution_bitcast_fusion.4
  111.5 2.5 convolution_bitcast_fusion.4
  120.0 1.6 select_reduce_fusion.5
  122.1 2.5 convolution_bitcast_fusion.4
  130.6 1.6 select_reduce_fusion.5
  132.7 2.5 convolution_bitcast_fusion.4
  141.2 1.6 select_reduce_fusion.5
  143.3 2.5 convolution_bitcast_fusion.4
  152.3 3.9 all-to-all-start.2
  156.2 4.5 add_convert_fusion
  163.4 6.7 %all-to-all-start.1 = ((bf16[32,128,2,128]{3,1,2,0:T(8,128)(2,1)}), bf16[32,128,2,128]{3,1,2,0:T(8,128)(2,1)}, u32[]{:S(2)}, u32[]{:S(2)}) async-start(bf16[32,128,2,128]{3,1,2,0:T(8,128)(2,1)} %copy.158), calls=%async_computation.1 | async-start | bytes 4194304 | tf_op jit(solution)/shard_map/all_to_all | solution.py:117
  170.8 25.2 %all-to-all-done.1 = bf16[32,128,2,128]{3,1,2,0:T(8,128)(2,1)} async-done(((bf16[32,128,2,128]{3,1,2,0:T(8,128)(2,1)}), bf16[32,128,2,128]{3,1,2,0:T(8,128)(2,1)}, u32[]{:S(2)}, u32[]{:S(2)}) %all-to-all-start.1) | async-done | bytes 2097184 | tf_op jit(solution)/shard_map/all_to_all | solution.py:117
  196.0 2.5 multiply_reduce_fusion
  198.7 2.4 convolution_convert_fusion.1
  201.6 1.8 reduce-window.6
  203.9 3.4 scatter_custom_fusion
  207.3 33.9 %reduce-scatter.4.cloned.1.call-done = bf16[128,256]{1,0:T(8,128)(2,1)} async-done(((bf16[128,2048]{1,0:T(8,128)(2,1)}), bf16[128,256]{1,0:T(8,128)(2,1)}) %reduce-scatter.4.cloned.1.call-update) | async-done | bytes 65552 | tf_op jit(solution)/shard_map/reduce_scatter | solution.py:133
  242.2 13.7 %psum.14 = f32[128]{0:T(128)S(1)} all-reduce(f32[128]{0:T(128)S(1)} %multiply_reduce_fusion.2), channel_id=1, replica_groups=mesh['seq'=32,'tensor'=8] {'tensor'}, use_global_device_ids=true, to_apply=%region_11.12 | all-reduce | flops 128 | bytes 1024 | tf_op jit(solution)/shard_map/psum | solution.py:137
  256.8 3.9 gather_fusion
  260.8 19.4 %all_to_all.25 = bf16[32,2,16,256]{3,2,1,0:T(8,128)(2,1)S(1)} all-to-all(bf16[32,2,16,256]{3,2,1,0:T(8,128)(2,1)S(1)} %bitcast.199), channel_id=1, replica_groups=mesh['seq'=32,'tensor'=8] {'seq'}, dimensions={0} | all-to-all | bytes 1048576 | tf_op jit(solution)/shard_map/all_to_all | solution.py:171
  281.1 54.1 %all-gather.2.cloned.1.call-done = bf16[32,2,16,2048]{3,2,0,1:T(8,128)(2,1)} async-done(((bf16[32,2,16,256]{3,2,0,1:T(8,128)(2,1)}), bf16[32,2,16,2048]{3,2,0,1:T(8,128)(2,1)}) %all-gather.2.cloned.1.call-update) | async-done | bytes 4194320 | tf_op jit(solution)/shard_map/all_gather | solution.py:172
  335.2 4.6 %fusion.20 = f32[32,2,16,2,176]{4,2,3,0,1:T(8,128)S(1)} fusion(bf16[2,2048,2,176]{1,3,2,0:T(8,128)(2,1)S(1)} %copy-done, bf16[32,2,16,2048]{3,2,0,1:T(8,128)(2,1)} %all-gather.2.cloned.1.call-done), kind=kOutput, calls=%fused_computation.32 | convolution fusion | flops 1476395008 | bytes 8519680 | tf_op jit(solution)/shard_map/secd,edjf->secjf/dot_general | solution.py:173
  339.8 3.2 convert_bitcast_fusion
  343.1 15.6 %all_gather.6 = bf16[128,2048]{1,0:T(8,128)(2,1)S(1)} all-gather(bf16[128,256]{1,0:T(8,128)(2,1)S(1)} %multiply_convert_fusion), channel_id=1, replica_groups=mesh['seq'=32,'tensor'=8] {'tensor'}, dimensions={1}, use_global_device_ids=true | all-gather | bytes 589824 | tf_op jit(solution)/shard_map/all_gather | solution.py:147
  358.7 2.6 fusion.69
  361.3 39.9 %reduce-scatter.8.cloned.1.call-done = bf16[32,2,16,256]{3,2,0,1:T(8,128)(2,1)} async-done(((bf16[32,2,16,2048]{3,2,0,1:T(8,128)(2,1)}), bf16[32,2,16,256]{3,2,0,1:T(8,128)(2,1)}) %reduce-scatter.8.cloned.1.call-update) | async-done | bytes 524304 | tf_op jit(solution)/shard_map/reduce_scatter | solution.py:180
  401.1 1.9 copy.172
  403.0 5.8 %all-to-all-start.4 = ((bf16[32,2,16,256]{3,2,1,0:T(8,128)(2,1)}), bf16[32,2,16,256]{3,2,1,0:T(8,128)(2,1)S(1)}, u32[]{:S(2)}, u32[]{:S(2)}) async-start(bf16[32,2,16,256]{3,2,1,0:T(8,128)(2,1)} %copy.172), calls=%async_computation.7 | async-start | bytes 1048576 | tf_op jit(solution)/shard_map/all_to_all | solution.py:183
  408.9 2.4 convolution_convert_fusion
  411.4 26.8 %psum.15 = bf16[128,64]{0,1:T(8,128)(2,1)S(1)} all-reduce(bf16[128,64]{0,1:T(8,128)(2,1)S(1)} %convolution_convert_fusion.2), channel_id=1, replica_groups=mesh['seq'=32,'tensor'=8] {'tensor'}, use_global_device_ids=true, to_apply=%region_13.14 | all-reduce | flops 8192 | bytes 32768 | tf_op jit(solution)/shard_map/psum | solution.py:140
  438.5 3.3 gather_fusion.1
  441.7 2.1 reshape.155
  443.9 1.6 multiply_reduce_fusion.1
  445.5 5.9 %reduce-scatter.6.cloned.1.call-done = bf16[128,256]{1,0:T(8,128)(2,1)} async-done(((bf16[128,2048]{1,0:T(8,128)(2,1)}), bf16[128,256]{1,0:T(8,128)(2,1)}) %reduce-scatter.6.cloned.1.call-update) | async-done | bytes 65552 | tf_op jit(solution)/shard_map/reduce_scatter | solution.py:153
  (154 shorter events, 74.2 us)
Async XLA Ops:
  6.5 328.6 %copy-start = (bf16[2,2048,2,176]{1,3,2,0:T(8,128)(2,1)S(1)}, bf16[2,2048,2,176]{1,3,2,0:T(8,128)(2,1)}, u32[]{:S(2)}) copy-start(bf16[2,2048,2,176]{1,3,2,0:T(8,128)(2,1)} %param.28) | copy-start | bytes 8650756
  9.4 36.8 %all-to-all-start = ((bf16[32,128,256]{1,2,0:T(8,128)(2,1)}), bf16[32,128,256]{1,2,0:T(8,128)(2,1)}, u32[]{:S(2)}, u32[]{:S(2)}) async-start(bf16[32,128,256]{1,2,0:T(8,128)(2,1)} %broadcast_in_dim.180), calls=%async_computation | async-start | bytes 4194304 | tf_op jit(solution)/shard_map/all_to_all | solution.py:60
  54.8 7.7 %copy-start.4 = (bf16[128,256]{1,0:T(8,128)(2,1)S(1)}, bf16[128,256]{1,0:T(8,128)(2,1)}, u32[]{:S(2)}) copy-start(bf16[128,256]{1,0:T(8,128)(2,1)} %param.19) | copy-start | bytes 196612
  59.4 6.5 %copy-start.9 = (s32[8]{0:T(128)S(1)}, s32[8]{0:T(128)}, u32[]{:S(2)}) copy-start(s32[8]{0:T(128)} %param.23) | copy-start | bytes 100
  152.3 11.1 %all-to-all-start.2 = ((f32[32,128,2,2]{1,2,3,0:T(2,128)}), f32[32,128,2,2]{1,2,3,0:T(2,128)S(1)}, u32[]{:S(2)}, u32[]{:S(2)}) async-start(f32[32,128,2,2]{1,2,3,0:T(2,128)} %copy.160), calls=%async_computation.2 | async-start | bytes 131072 | tf_op jit(solution)/shard_map/all_to_all | solution.py:114
  162.2 8.1 %copy-start.5 = (s32[128,6]{0,1:T(8,128)S(1)}, s32[128,6]{0,1:T(8,128)}, u32[]{:S(2)}) copy-start(s32[128,6]{0,1:T(8,128)} %param.27) | copy-start | bytes 9220
  163.4 32.5 %all-to-all-start.1 = ((bf16[32,128,2,128]{3,1,2,0:T(8,128)(2,1)}), bf16[32,128,2,128]{3,1,2,0:T(8,128)(2,1)}, u32[]{:S(2)}, u32[]{:S(2)}) async-start(bf16[32,128,2,128]{3,1,2,0:T(8,128)(2,1)} %copy.158), calls=%async_computation.1 | async-start | bytes 4194304 | tf_op jit(solution)/shard_map/all_to_all | solution.py:117
  170.2 71.1 %reduce-scatter.4.cloned.1.call-start = ((), (), s32[]{:S(2)}) async-start(), calls=%async_computation.8 | async-start | bytes 589824 | tf_op jit(solution)/shard_map/reduce_scatter | solution.py:133
  198.4 42.8 %copy-start.1 = (bf16[128,256]{1,0:T(8,128)(2,1)S(1)}, bf16[128,256]{1,0:T(8,128)(2,1)}, u32[]{:S(2)}) copy-start(bf16[128,256]{1,0:T(8,128)(2,1)} %param.17) | copy-start | bytes 196612
  198.5 57.4 %copy-start.7 = (f32[256]{0:T(256)S(1)}, f32[256]{0:T(256)}, u32[]{:S(2)}) copy-start(f32[256]{0:T(256)} %param.25) | copy-start | bytes 3076
  201.1 134.1 %all-gather.2.cloned.1.call-start = ((), (), s32[]{:S(2)}) async-start(), calls=%async_computation.10 | async-start | bytes 4718592 | tf_op jit(solution)/shard_map/all_gather | solution.py:172
  281.1 120.1 %reduce-scatter.8.cloned.1.call-start = ((), (), s32[]{:S(2)}) async-start(), calls=%async_computation.11 | async-start | bytes 4718592 | tf_op jit(solution)/shard_map/reduce_scatter | solution.py:180
  335.2 4.6 %copy-start.8 = (bf16[2,176,2048]{2,1,0:T(8,128)(2,1)S(1)}, bf16[2,176,2048]{2,1,0:T(8,128)(2,1)}, u32[]{:S(2)}) copy-start(bf16[2,176,2048]{2,1,0:T(8,128)(2,1)} %param.29) | copy-start | bytes 4325380
  361.3 50.0 %copy-start.6 = (bf16[256,64]{0,1:T(8,128)(2,1)S(1)}, bf16[256,64]{0,1:T(8,128)(2,1)}, u32[]{:S(2)}) copy-start(bf16[256,64]{0,1:T(8,128)(2,1)} %param.26) | copy-start | bytes 98308
  403.0 35.4 %all-to-all-start.4 = ((bf16[32,2,16,256]{3,2,1,0:T(8,128)(2,1)}), bf16[32,2,16,256]{3,2,1,0:T(8,128)(2,1)S(1)}, u32[]{:S(2)}, u32[]{:S(2)}) async-start(bf16[32,2,16,256]{3,2,1,0:T(8,128)(2,1)} %copy.172), calls=%async_computation.7 | async-start | bytes 1048576 | tf_op jit(solution)/shard_map/all_to_all | solution.py:183
  408.8 42.6 %reduce-scatter.6.cloned.1.call-start = ((), (), s32[]{:S(2)}) async-start(), calls=%async_computation.9 | async-start | bytes 589824 | tf_op jit(solution)/shard_map/reduce_scatter | solution.py:153
  441.7 9.7 %copy-start.2 = (bf16[128,256]{1,0:T(8,128)(2,1)S(1)}, bf16[128,256]{1,0:T(8,128)(2,1)}, u32[]{:S(2)}) copy-start(bf16[128,256]{1,0:T(8,128)(2,1)} %param.17) | copy-start | bytes 196612
  441.7 9.7 %copy-start.3 = (bf16[128,256]{1,0:T(8,128)(2,1)S(1)}, bf16[128,256]{1,0:T(8,128)(2,1)}, u32[]{:S(2)}) copy-start(bf16[128,256]{1,0:T(8,128)(2,1)} %reduce-scatter.4.cloned.1.call-done) | copy-start | bytes 196612
Sparse Core Ops, SparseCore 0:
  201.2 39.9 reduce-scatter.3
  281.2 53.9 all-gather.1
  343.2 57.9 reduce-scatter.7
  411.8 39.4 reduce-scatter.5

commit v2 on v1

--- a/solution.py
+++ b/solution.py
@@ -61,23 +61,29 @@
     grouped = every_query.reshape(requests, NEW, heads_local, HD)
     first_place = seq_index * clen_dev
 
-    def cached_part(request):
-        query_block, key_block, value_block, length = request
-        scores = (
-            jnp.einsum("qhd,khd->hqk", query_block, key_block, preferred_element_type=jnp.float32)
-            * scaling
-        )
-        visible = (first_place + lax.iota(jnp.int32, clen_dev) < length)[None, None, :]
-        return block_partial(scores, visible, value_block)
-
-    max_cached, sum_cached, out_cached = lax.map(
-        cached_part,
-        (
+    cached_scores = (
+        jnp.einsum(
+            "rqhd,rkhd->rhqk",
             grouped,
             cache_keys.reshape(requests, clen_dev, heads_local, HD),
-            cache_values.reshape(requests, clen_dev, heads_local, HD),
-            cache_lengths,
-        ),
+            preferred_element_type=jnp.float32,
+        )
+        * scaling
+    )
+    cached_visible = (
+        first_place + lax.iota(jnp.int32, clen_dev)[None, :] < cache_lengths[:, None]
+    )[:, None, None, :]
+    masked = jnp.where(cached_visible, cached_scores, negative)
+    max_cached = jnp.max(masked, -1)
+    cached_weights = jnp.where(
+        cached_visible, jnp.exp(cached_scores - max_cached[..., None]), 0.0
+    )
+    sum_cached = jnp.sum(cached_weights, -1)
+    out_cached = jnp.einsum(
+        "rhqk,rkhd->rqhd",
+        cached_weights.astype(jnp.bfloat16),
+        cache_values.reshape(requests, clen_dev, heads_local, HD),
+        preferred_element_type=jnp.float32,
     )
     max_cached = jnp.transpose(max_cached, (0, 2, 1))
     sum_cached = jnp.transpose(sum_cached, (0, 2, 1))

time: 463 us -> 392 us (0.85)
  local copies, waits for them, and re-layouts: 89.1 us -> 38.5 us
  matrix products: 50.8 us -> 35.9 us
  other arithmetic: 24.3 us -> 16.5 us
    dynamic_update_slice x48 -> x0, local copies, waits for them, and re-layouts: 38.8 us -> none  [shards(): lax.map(cached_part, (grouped, cache_keys.reshape(requests, clen_dev, hea...]
    dot_general x9 -> x1, matrix products: 21.8 us -> 1.15 us  [block_partial(): jnp.einsum('hqk,khd->qhd', weights.astype(jnp.bfloat16), values, preferre...]
    all_to_all x1, waiting for transfers between devices: 20.2 us -> 28 us  [shards(): lax.all_to_all(spread, 'seq', 0, 0, tiled=True).reshape(tokens, width_local)]
    unnamed x24, local copies, waits for them, and re-layouts: 9.13 us -> 3.39 us
    dot_general x8 -> x2, matrix products: 12.5 us -> 16.9 us  [the longest x1 9.95 us: shards(): jnp.einsum('rhqk,rkhd->rqhd', cached_weights.astype(jnp.bfloat16), cache_...]
  transfers between devices with their start and end apart: 8 -> 8, of which waited for: 7 -> 6; matrix products, arithmetic and copies ran while one was open for 7% -> 9% of each run, Pallas kernels for 0% -> 0%
where the time goes in v2:
time: 392 us; the launch traced here: 390 us
  waiting for transfers between devices  183 us (47%)
  blocking collectives  76.2 us (19%)
  local copies, waits for them, and re-layouts  38.5 us (10%)
  matrix products  35.9 us (9%)
  starting transfers between devices  26.7 us (7%)
  other arithmetic  16.5 us (4%)
  between operations  13.5 us (3%)
    all_gather x1, waiting for transfers between devices, shards(): routed_rows = lax.all_gather(incoming, 'tensor', axis=3, tiled=True)  54.1 us
    reduce_scatter x1, waiting for transfers between devices, shards(): lax.psum_scatter(expert_term.astype(jnp.bfloat16), 'tensor', scatter_dime...  39.6 us
    reduce_scatter x1, waiting for transfers between devices, shards(): lax.psum_scatter(projected.astype(jnp.bfloat16), 'tensor', scatter_dimens...  34 us
    all_to_all x1, waiting for transfers between devices, shards(): lax.all_to_all(spread, 'seq', 0, 0, tiled=True).reshape(tokens, width_local)  28 us
    psum x1, blocking collectives, shards(): lax.psum(jnp.dot(normed, router, preferred_element_type=jnp.float32).asty...  27.3 us
    all_to_all x1, waiting for transfers between devices, shards(): lax.all_to_all(local_out.reshape(seq_count, tok_dev, heads_local, HD).ast...  25 us
    all_to_all x1, blocking collectives, shards(): lax.all_to_all(outgoing, 'seq', split_axis=0, concat_axis=0, tiled=True)  19.5 us
    all_gather x1, blocking collectives, shards(): normed_full = lax.all_gather(normed, 'tensor', axis=1, tiled=True)  15.6 us
  transfers between devices with their start and end apart: 8, of which 6 were waited for; matrix products, arithmetic and copies ran while one was open for 9% of the time, Pallas kernels for 0%

profile of v2, /device:TPU:65, one launch (start us, length us, event | category | flops | bytes accessed | tf_op | source)
XLA Modules:
  0.0 389.9 jit_solution(1350715949676768086)
XLA Ops:
  6.5 1.1 copy.129
  7.7 1.8 broadcast_in_dim.155
  9.4 8.5 %all-to-all-start = ((bf16[32,128,256]{1,2,0:T(8,128)(2,1)}), bf16[32,128,256]{1,2,0:T(8,128)(2,1)}, u32[]{:S(2)}, u32[]{:S(2)}) async-start(bf16[32,128,256]{1,2,0:T(8,128)(2,1)} %broadcast_in_dim.155), calls=%async_computation | async-start | bytes 4194304 | tf_op jit(solution)/shard_map/all_to_all | solution.py:60
  18.2 28.0 %all-to-all-done = bf16[32,128,256]{1,2,0:T(8,128)(2,1)} async-done(((bf16[32,128,256]{1,2,0:T(8,128)(2,1)}), bf16[32,128,256]{1,2,0:T(8,128)(2,1)}, u32[]{:S(2)}, u32[]{:S(2)}) %all-to-all-start) | async-done | bytes 2097184 | tf_op jit(solution)/shard_map/all_to_all | solution.py:60
  46.2 4.2 %copy.130 = bf16[32,128,256]{1,0,2:T(8,128)(2,1)} copy(bf16[32,128,256]{1,2,0:T(8,128)(2,1)} %all-to-all-done) | data formatting | bytes 4194304 | tf_op jit(solution)/shard_map/all_to_all | solution.py:60
  50.5 4.3 %reshape_reshape.3 = bf16[8,512,2,128]{1,0,3,2:T(8,128)(2,1)} reshape(bf16[32,128,256]{1,0,2:T(8,128)(2,1)} %copy.130) | data formatting | bytes 4194304 | tf_op jit(solution)/shard_map/reshape;reshape | solution.py:61
  54.8 2.1 constant_dynamic-slice_fusion
  56.9 1.0 copy.136
  57.9 1.2 select_reduce_fusion.1
  59.3 6.9 %select_reduce_fusion = (f32[8,2,512]{2,1,0:T(2,128)S(1)}, f32[8,2,512,512]{2,3,1,0:T(8,128)S(1)}) fusion(pred[8,512]{1,0:T(8,128)(4,1)S(1)} %broadcast_compare_fusion, bf16[8,512,2,128]{1,0,3,2:T(8,128)(2,1)} %reshape_reshape.3, bf16[8,512,256]{2,1,0:T(8,128)(2,1)} %param.19), kind=kOutput, calls=%fused_computation.4 | convolution fusion | flops 1086316544 | bytes 21008384 | tf_op jit(solution)/shard_map/rqhd,rkhd->rhqk/dot_general | solution.py:65
  66.2 3.6 fusion
  69.8 2.1 copy-done.1
  73.3 0.8 pad_maximum_fusion
  74.7 3.9 %all-to-all-start.2 = ((f32[32,128,2,2]{1,2,3,0:T(2,128)}), f32[32,128,2,2]{1,2,3,0:T(2,128)S(1)}, u32[]{:S(2)}, u32[]{:S(2)}) async-start(f32[32,128,2,2]{1,2,3,0:T(2,128)} %copy.145), calls=%async_computation.2 | async-start | bytes 131072 | tf_op jit(solution)/shard_map/all_to_all | solution.py:120
  78.6 0.8 copy.138
  79.4 0.8 copy.141
  80.2 1.2 convolution_bitcast_fusion
  81.4 10.0 %fusion.11 = bf16[8,512,2,128]{3,1,2,0:T(8,128)(2,1)S(1)} fusion(f32[8,2,512,512]{2,3,1,0:T(8,128)} %copy-done.1, f32[8,2,512]{2,1,0:T(2,128)} %copy-done.5, pred[8,512]{1,0:T(8,128)(4,1)S(1)} %broadcast_compare_fusion, f32[8,512,2]{1,2,0:T(2,128)S(1)} %copy.141, f32[512,2,128]{2,0,1:T(8,128)S(1)} %convolution_bitcast_fusion, f32[8,512,2]{1,2,0:T(2,128)S(1)} %copy.138, ...), kind=kOutput, calls=%fused_computation.16 | convolution fusion | flops 1095761920 | bytes 21598216 | tf_op jit(solution)/shard_map/rhqk,rkhd->rqhd/dot_general | solution.py:82
  91.5 1.4 copy.143
  92.9 8.0 %all-to-all-start.1 = ((bf16[32,128,2,128]{3,1,2,0:T(8,128)(2,1)}), bf16[32,128,2,128]{3,1,2,0:T(8,128)(2,1)}, u32[]{:S(2)}, u32[]{:S(2)}) async-start(bf16[32,128,2,128]{3,1,2,0:T(8,128)(2,1)} %copy.143), calls=%async_computation.1 | async-start | bytes 4194304 | tf_op jit(solution)/shard_map/all_to_all | solution.py:123
  101.6 25.0 %all-to-all-done.1 = bf16[32,128,2,128]{3,1,2,0:T(8,128)(2,1)} async-done(((bf16[32,128,2,128]{3,1,2,0:T(8,128)(2,1)}), bf16[32,128,2,128]{3,1,2,0:T(8,128)(2,1)}, u32[]{:S(2)}, u32[]{:S(2)}) %all-to-all-start.1) | async-done | bytes 2097184 | tf_op jit(solution)/shard_map/all_to_all | solution.py:123
  126.5 2.5 multiply_reduce_fusion
  129.3 2.4 convolution_convert_fusion.1
  131.7 1.8 reduce-window.6
  134.3 3.4 scatter_custom_fusion
  137.7 34.0 %reduce-scatter.4.cloned.1.call-done = bf16[128,256]{1,0:T(8,128)(2,1)} async-done(((bf16[128,2048]{1,0:T(8,128)(2,1)}), bf16[128,256]{1,0:T(8,128)(2,1)}) %reduce-scatter.4.cloned.1.call-update) | async-done | bytes 65552 | tf_op jit(solution)/shard_map/reduce_scatter | solution.py:139
  171.7 0.9 multiply_reduce_fusion.2
  172.6 13.7 %psum.14 = f32[128]{0:T(128)S(1)} all-reduce(f32[128]{0:T(128)S(1)} %multiply_reduce_fusion.2), channel_id=1, replica_groups=mesh['seq'=32,'tensor'=8] {'tensor'}, use_global_device_ids=true, to_apply=%region_9.10 | all-reduce | flops 128 | bytes 1024 | tf_op jit(solution)/shard_map/psum | solution.py:143
  186.3 0.9 multiply_convert_fusion
  187.3 3.9 %gather_fusion = bf16[1024,256]{1,0:T(8,128)(2,1)S(1)} fusion(bf16[129,256]{1,0:T(8,128)(2,1)S(1)} %concatenate.3, s32[1024]{0:T(1024)S(1)} %fusion.60), kind=kCustom, calls=%fused_computation | custom fusion | bytes 1052672 | tf_op jit(solution)/shard_map/gather | solution.py:176
  191.2 19.5 %all_to_all.25 = bf16[32,2,16,256]{3,2,1,0:T(8,128)(2,1)S(1)} all-to-all(bf16[32,2,16,256]{3,2,1,0:T(8,128)(2,1)S(1)} %bitcast.174), channel_id=1, replica_groups=mesh['seq'=32,'tensor'=8] {'seq'}, dimensions={0} | all-to-all | bytes 1048576 | tf_op jit(solution)/shard_map/all_to_all | solution.py:177
  210.7 0.8 copy.155
  211.6 54.1 %all-gather.2.cloned.1.call-done = bf16[32,2,16,2048]{3,2,0,1:T(8,128)(2,1)} async-done(((bf16[32,2,16,256]{3,2,0,1:T(8,128)(2,1)}), bf16[32,2,16,2048]{3,2,0,1:T(8,128)(2,1)}) %all-gather.2.cloned.1.call-update) | async-done | bytes 4194320 | tf_op jit(solution)/shard_map/all_gather | solution.py:178
  265.7 4.6 %fusion.21 = f32[32,2,16,2,176]{4,2,3,0,1:T(8,128)S(1)} fusion(bf16[2,2048,2,176]{1,3,2,0:T(8,128)(2,1)S(1)} %copy-done, bf16[32,2,16,2048]{3,2,0,1:T(8,128)(2,1)} %all-gather.2.cloned.1.call-done), kind=kOutput, calls=%fused_computation.28 | convolution fusion | flops 1476395008 | bytes 8519680 | tf_op jit(solution)/shard_map/secd,edjf->secjf/dot_general | solution.py:179
  270.4 3.2 convert_bitcast_fusion
  273.6 15.6 %all_gather.6 = bf16[128,2048]{1,0:T(8,128)(2,1)S(1)} all-gather(bf16[128,256]{1,0:T(8,128)(2,1)S(1)} %multiply_convert_fusion), channel_id=1, replica_groups=mesh['seq'=32,'tensor'=8] {'tensor'}, dimensions={1}, use_global_device_ids=true | all-gather | bytes 589824 | tf_op jit(solution)/shard_map/all_gather | solution.py:153
  289.2 2.6 fusion.72
  291.8 39.6 %reduce-scatter.8.cloned.1.call-done = bf16[32,2,16,256]{3,2,0,1:T(8,128)(2,1)} async-done(((bf16[32,2,16,2048]{3,2,0,1:T(8,128)(2,1)}), bf16[32,2,16,256]{3,2,0,1:T(8,128)(2,1)}) %reduce-scatter.8.cloned.1.call-update) | async-done | bytes 524304 | tf_op jit(solution)/shard_map/reduce_scatter | solution.py:186
  331.5 1.9 copy.157
  333.4 6.1 %all-to-all-start.4 = ((bf16[32,2,16,256]{3,2,1,0:T(8,128)(2,1)}), bf16[32,2,16,256]{3,2,1,0:T(8,128)(2,1)S(1)}, u32[]{:S(2)}, u32[]{:S(2)}) async-start(bf16[32,2,16,256]{3,2,1,0:T(8,128)(2,1)} %copy.157), calls=%async_computation.7 | async-start | bytes 1048576 | tf_op jit(solution)/shard_map/all_to_all | solution.py:189
  339.5 2.4 convolution_convert_fusion
  342.6 1.5 convolution_convert_fusion.2
  344.1 27.3 %psum.15 = bf16[128,64]{0,1:T(8,128)(2,1)S(1)} all-reduce(bf16[128,64]{0,1:T(8,128)(2,1)} %convolution_convert_fusion.2), channel_id=1, replica_groups=mesh['seq'=32,'tensor'=8] {'tensor'}, use_global_device_ids=true, to_apply=%region_11.12 | all-reduce | flops 8192 | bytes 32768 | tf_op jit(solution)/shard_map/psum | solution.py:146
  372.9 3.4 gather_fusion.1
  376.3 2.1 reshape.178
  378.4 1.6 multiply_reduce_fusion.1
  380.0 1.9 reduce-scatter.6.cloned.1.call-done
  381.9 1.5 add_convert_fusion
  (68 shorter events, 6.4 us)
Async XLA Ops:
  6.5 259.2 %copy-start = (bf16[2,2048,2,176]{1,3,2,0:T(8,128)(2,1)S(1)}, bf16[2,2048,2,176]{1,3,2,0:T(8,128)(2,1)}, u32[]{:S(2)}) copy-start(bf16[2,2048,2,176]{1,3,2,0:T(8,128)(2,1)} %param.26) | copy-start | bytes 8650756
  6.5 11.5 %copy-start.9 = (s32[8]{0:T(128)S(1)}, s32[8]{0:T(128)}, u32[]{:S(2)}) copy-start(s32[8]{0:T(128)} %param.21) | copy-start | bytes 100
  9.4 36.8 %all-to-all-start = ((bf16[32,128,256]{1,2,0:T(8,128)(2,1)}), bf16[32,128,256]{1,2,0:T(8,128)(2,1)}, u32[]{:S(2)}, u32[]{:S(2)}) async-start(bf16[32,128,256]{1,2,0:T(8,128)(2,1)} %broadcast_in_dim.155), calls=%async_computation | async-start | bytes 4194304 | tf_op jit(solution)/shard_map/all_to_all | solution.py:60
  18.2 39.7 %copy-start.6 = (bf16[128,256]{1,0:T(8,128)(2,1)S(1)}, bf16[128,256]{1,0:T(8,128)(2,1)}, u32[]{:S(2)}) copy-start(bf16[128,256]{1,0:T(8,128)(2,1)} %param.17) | copy-start | bytes 196612
  66.2 5.7 %copy-start.1 = (f32[8,2,512,512]{2,3,1,0:T(8,128)}, f32[8,2,512,512]{2,3,1,0:T(8,128)S(1)}, u32[]{:S(2)}) copy-start(f32[8,2,512,512]{2,3,1,0:T(8,128)S(1)} %get-tuple-element.10) | copy-start | bytes 50331652
  66.2 5.7 %copy-start.5 = (f32[8,2,512]{2,1,0:T(2,128)}, f32[8,2,512]{2,1,0:T(2,128)S(1)}, u32[]{:S(2)}) copy-start(f32[8,2,512]{2,1,0:T(2,128)S(1)} %get-tuple-element.9) | copy-start | bytes 98308
  74.7 18.2 %all-to-all-start.2 = ((f32[32,128,2,2]{1,2,3,0:T(2,128)}), f32[32,128,2,2]{1,2,3,0:T(2,128)S(1)}, u32[]{:S(2)}, u32[]{:S(2)}) async-start(f32[32,128,2,2]{1,2,3,0:T(2,128)} %copy.145), calls=%async_computation.2 | async-start | bytes 131072 | tf_op jit(solution)/shard_map/all_to_all | solution.py:120
  91.5 9.6 %copy-start.7 = (s32[128,6]{0,1:T(8,128)S(1)}, s32[128,6]{0,1:T(8,128)}, u32[]{:S(2)}) copy-start(s32[128,6]{0,1:T(8,128)} %param.25) | copy-start | bytes 9220
  92.9 33.6 %all-to-all-start.1 = ((bf16[32,128,2,128]{3,1,2,0:T(8,128)(2,1)}), bf16[32,128,2,128]{3,1,2,0:T(8,128)(2,1)}, u32[]{:S(2)}, u32[]{:S(2)}) async-start(bf16[32,128,2,128]{3,1,2,0:T(8,128)(2,1)} %copy.143), calls=%async_computation.1 | async-start | bytes 4194304 | tf_op jit(solution)/shard_map/all_to_all | solution.py:123
  101.0 70.7 %copy-start.2 = (bf16[128,256]{1,0:T(8,128)(2,1)S(1)}, bf16[128,256]{1,0:T(8,128)(2,1)}, u32[]{:S(2)}) copy-start(bf16[128,256]{1,0:T(8,128)(2,1)} %param.15) | copy-start | bytes 196612
  101.0 85.4 %copy-start.8 = (f32[256]{0:T(256)S(1)}, f32[256]{0:T(256)}, u32[]{:S(2)}) copy-start(f32[256]{0:T(256)} %param.23) | copy-start | bytes 3076
  101.0 70.7 %reduce-scatter.4.cloned.1.call-start = ((), (), s32[]{:S(2)}) async-start(), calls=%async_computation.8 | async-start | bytes 589824 | tf_op jit(solution)/shard_map/reduce_scatter | solution.py:139
  131.7 134.0 %all-gather.2.cloned.1.call-start = ((), (), s32[]{:S(2)}) async-start(), calls=%async_computation.10 | async-start | bytes 4718592 | tf_op jit(solution)/shard_map/all_gather | solution.py:178
  211.6 119.9 %reduce-scatter.8.cloned.1.call-start = ((), (), s32[]{:S(2)}) async-start(), calls=%async_computation.11 | async-start | bytes 4718592 | tf_op jit(solution)/shard_map/reduce_scatter | solution.py:186
  265.7 4.7 %copy-start.10 = (bf16[2,176,2048]{2,1,0:T(8,128)(2,1)S(1)}, bf16[2,176,2048]{2,1,0:T(8,128)(2,1)}, u32[]{:S(2)}) copy-start(bf16[2,176,2048]{2,1,0:T(8,128)(2,1)} %param.27) | copy-start | bytes 4325380
  333.4 39.6 %all-to-all-start.4 = ((bf16[32,2,16,256]{3,2,1,0:T(8,128)(2,1)}), bf16[32,2,16,256]{3,2,1,0:T(8,128)(2,1)S(1)}, u32[]{:S(2)}, u32[]{:S(2)}) async-start(bf16[32,2,16,256]{3,2,1,0:T(8,128)(2,1)} %copy.157), calls=%async_computation.7 | async-start | bytes 1048576 | tf_op jit(solution)/shard_map/all_to_all | solution.py:189
  339.5 42.4 %reduce-scatter.6.cloned.1.call-start = ((), (), s32[]{:S(2)}) async-start(), calls=%async_computation.9 | async-start | bytes 589824 | tf_op jit(solution)/shard_map/reduce_scatter | solution.py:159
  339.5 42.4 %copy-start.3 = (bf16[128,256]{1,0:T(8,128)(2,1)S(1)}, bf16[128,256]{1,0:T(8,128)(2,1)}, u32[]{:S(2)}) copy-start(bf16[128,256]{1,0:T(8,128)(2,1)} %param.15) | copy-start | bytes 196612
  344.1 37.8 %copy-start.4 = (bf16[128,256]{1,0:T(8,128)(2,1)S(1)}, bf16[128,256]{1,0:T(8,128)(2,1)}, u32[]{:S(2)}) copy-start(bf16[128,256]{1,0:T(8,128)(2,1)} %reduce-scatter.4.cloned.1.call-done) | copy-start | bytes 196612
Sparse Core Ops, SparseCore 0:
  131.8 39.8 reduce-scatter.3
  211.7 53.9 all-gather.1
  273.7 57.7 reduce-scatter.7
  342.5 39.3 reduce-scatter.5

commit v3 on v2

--- a/solution.py
+++ b/solution.py
@@ -135,22 +135,28 @@
     attended = (
         (weighted / row_sum[..., None]).astype(jnp.bfloat16).reshape(tok_dev, heads_local * HD)
     )
+    tensor_index = lax.axis_index("tensor")
+    own_slice = (lax.iota(jnp.int32, tensor_count) == tensor_index)[None, :, None]
+
+    def placed(part):
+        return jnp.where(own_slice, part[:, None, :], 0.0).reshape(part.shape[0], -1)
+
+    weights_full = lax.psum(
+        placed(jnp.concatenate([router.astype(jnp.float32).T, norm_gain[None]], 0)), "tensor"
+    )
+    router_full = weights_full[:experts].T.astype(jnp.bfloat16)
+    gain_full = weights_full[experts]
     projected = jnp.dot(attended, out_proj, preferred_element_type=jnp.float32)
-    attn_out = lax.psum_scatter(
-        projected.astype(jnp.bfloat16), "tensor", scatter_dimension=1, tiled=True
-    ).astype(jnp.float32)
-    stream = residual.astype(jnp.float32) + attn_out
-    square_total = lax.psum(jnp.sum(stream * stream, 1), "tensor")
-    inverse_rms = lax.rsqrt(square_total / D + epsilon)
-    normed = (stream * inverse_rms[:, None] * norm_gain).astype(jnp.bfloat16)
-    logits = lax.psum(
-        jnp.dot(normed, router, preferred_element_type=jnp.float32).astype(jnp.bfloat16), "tensor"
-    ).astype(jnp.float32)
+    stream_full = lax.psum(projected + placed(residual.astype(jnp.float32)), "tensor")
+    inverse_rms = lax.rsqrt(jnp.sum(stream_full * stream_full, 1) / D + epsilon)
+    normed_full = (stream_full * inverse_rms[:, None] * gain_full).astype(jnp.bfloat16)
+    stream = lax.dynamic_slice_in_dim(stream_full, tensor_index * width_local, width_local, 1)
+    normed = lax.dynamic_slice_in_dim(normed_full, tensor_index * width_local, width_local, 1)
+    logits = jnp.dot(normed_full, router_full, preferred_element_type=jnp.float32)
     matches = expert_ids[:, :, None] == lax.iota(jnp.int32, experts)[None, None, :]
     selected = jnp.sum(jnp.where(matches, logits[:, None, :], 0.0), 2)
     sigmoids = jax.nn.sigmoid(selected)
     gates = sigmoids / jnp.sum(sigmoids, 1, keepdims=True)
-    normed_full = lax.all_gather(normed, "tensor", axis=1, tiled=True)
     shared_pair = jnp.einsum(
         "td,dcf->tcf", normed_full, shared_gate_up, preferred_element_type=jnp.float32
     )

time: 392 us -> 422 us (1.077)
  waiting for transfers between devices: 183 us -> 267 us
  blocking collectives: 76.2 us -> 17.6 us
    psum x0 -> x1, waiting for transfers between devices: none -> 77.3 us  [shards(): lax.psum(projected + placed(residual.astype(jnp.float32)), 'tensor')]
    psum x2 -> x0, blocking collectives: 41 us -> none  [the longest x1 27.3 us: shards(): lax.psum(jnp.dot(normed, router, preferred_element_type=jnp.float32).asty...]
    reduce_scatter x1 -> x0, waiting for transfers between devices: 34 us -> none  [shards(): lax.psum_scatter(projected.astype(jnp.bfloat16), 'tensor', scatter_dimens...]
    reduce_scatter x1, waiting for transfers between devices: 1.87 us -> 23.4 us  [shards(): lax.psum_scatter(shared_term.astype(jnp.bfloat16), 'tensor', scatter_dime...]
    reduce_scatter x1, waiting for transfers between devices: 39.6 us -> 56.1 us  [shards(): lax.psum_scatter(expert_term.astype(jnp.bfloat16), 'tensor', scatter_dime...]
    all_gather x1 -> x0, blocking collectives: 15.6 us -> none  [shards(): normed_full = lax.all_gather(normed, 'tensor', axis=1, tiled=True)]
    all_to_all x1, waiting for transfers between devices: 0.01 us -> 6.58 us  [shards(): lax.all_to_all(expert_total, 'seq', split_axis=0, concat_axis=0, tiled=True)]
  transfers between devices with their start and end apart: 8 -> 8, of which waited for: 6 -> 7; matrix products, arithmetic and copies ran while one was open for 9% -> 9% of each run, Pallas kernels for 0% -> 0%
where the time goes in v3:
time: 422 us; the launch traced here: 420 us
  waiting for transfers between devices  267 us (63%)
  local copies, waits for them, and re-layouts  41.3 us (10%)
  matrix products  36.4 us (9%)
  starting transfers between devices  27.1 us (6%)
  blocking collectives  17.6 us (4%)
  other arithmetic  17 us (4%)
  between operations  13.6 us (3%)
    psum x1, waiting for transfers between devices, shards(): lax.psum(projected + placed(residual.astype(jnp.float32)), 'tensor')  77.3 us
    reduce_scatter x1, waiting for transfers between devices, shards(): lax.psum_scatter(expert_term.astype(jnp.bfloat16), 'tensor', scatter_dime...  56.1 us
    all_gather x1, waiting for transfers between devices, shards(): routed_rows = lax.all_gather(incoming, 'tensor', axis=3, tiled=True)  53.1 us
    all_to_all x1, waiting for transfers between devices, shards(): lax.all_to_all(spread, 'seq', 0, 0, tiled=True).reshape(tokens, width_local)  28 us
    reduce_scatter x1, waiting for transfers between devices, shards(): lax.psum_scatter(shared_term.astype(jnp.bfloat16), 'tensor', scatter_dime...  23.4 us
    all_to_all x1, waiting for transfers between devices, shards(): lax.all_to_all(local_out.reshape(seq_count, tok_dev, heads_local, HD).ast...  22.9 us
    all_to_all x1, blocking collectives, shards(): lax.all_to_all(outgoing, 'seq', split_axis=0, concat_axis=0, tiled=True)  17.6 us
    dot_general x1, matrix products, shards(): jnp.einsum('rhqk,rkhd->rqhd', cached_weights.astype(jnp.bfloat16), cache_...  9.95 us
  transfers between devices with their start and end apart: 8, of which 7 were waited for; matrix products, arithmetic and copies ran while one was open for 9% of the time, Pallas kernels for 0%

profile of v3, /device:TPU:65, one launch (start us, length us, event | category | flops | bytes accessed | tf_op | source)
XLA Modules:
  0.0 420.5 jit_solution(382911607259244197)
XLA Ops:
  6.5 1.1 copy.129
  7.7 1.8 broadcast_in_dim.208
  9.4 8.5 %all-to-all-start = ((bf16[32,128,256]{1,2,0:T(8,128)(2,1)}), bf16[32,128,256]{1,2,0:T(8,128)(2,1)}, u32[]{:S(2)}, u32[]{:S(2)}) async-start(bf16[32,128,256]{1,2,0:T(8,128)(2,1)} %broadcast_in_dim.208), calls=%async_computation | async-start | bytes 4194304 | tf_op jit(solution)/shard_map/all_to_all | solution.py:60
  18.2 28.0 %all-to-all-done = bf16[32,128,256]{1,2,0:T(8,128)(2,1)} async-done(((bf16[32,128,256]{1,2,0:T(8,128)(2,1)}), bf16[32,128,256]{1,2,0:T(8,128)(2,1)}, u32[]{:S(2)}, u32[]{:S(2)}) %all-to-all-start) | async-done | bytes 2097184 | tf_op jit(solution)/shard_map/all_to_all | solution.py:60
  46.2 4.2 %copy.130 = bf16[32,128,256]{1,0,2:T(8,128)(2,1)} copy(bf16[32,128,256]{1,2,0:T(8,128)(2,1)} %all-to-all-done) | data formatting | bytes 4194304 | tf_op jit(solution)/shard_map/all_to_all | solution.py:60
  50.5 4.3 %reshape_reshape.3 = bf16[8,512,2,128]{1,0,3,2:T(8,128)(2,1)} reshape(bf16[32,128,256]{1,0,2:T(8,128)(2,1)} %copy.130) | data formatting | bytes 4194304 | tf_op jit(solution)/shard_map/reshape;reshape | solution.py:61
  54.8 2.1 constant_dynamic-slice_fusion.1
  56.9 1.0 copy.136
  57.9 1.2 select_reduce_fusion.1
  59.3 6.9 %select_reduce_fusion = (f32[8,2,512]{2,1,0:T(2,128)S(1)}, f32[8,2,512,512]{2,3,1,0:T(8,128)S(1)}) fusion(pred[8,512]{1,0:T(8,128)(4,1)S(1)} %broadcast_compare_fusion, bf16[8,512,2,128]{1,0,3,2:T(8,128)(2,1)} %reshape_reshape.3, bf16[8,512,256]{2,1,0:T(8,128)(2,1)} %param.19), kind=kOutput, calls=%fused_computation.4 | convolution fusion | flops 1086316544 | bytes 21008384 | tf_op jit(solution)/shard_map/rqhd,rkhd->rhqk/dot_general | solution.py:65
  66.2 3.6 fusion
  69.8 2.1 copy-done.1
  74.7 3.9 all-to-all-start.2
  78.6 0.8 copy.138
  79.4 0.8 copy.141
  80.2 1.2 convolution_bitcast_fusion
  81.4 10.0 %fusion.11 = bf16[8,512,2,128]{3,1,2,0:T(8,128)(2,1)S(1)} fusion(f32[8,2,512,512]{2,3,1,0:T(8,128)} %copy-done.1, f32[8,2,512]{2,1,0:T(2,128)} %copy-done.3, pred[8,512]{1,0:T(8,128)(4,1)S(1)} %broadcast_compare_fusion, f32[8,512,2]{1,2,0:T(2,128)S(1)} %copy.141, f32[512,2,128]{2,0,1:T(8,128)S(1)} %convolution_bitcast_fusion, f32[8,512,2]{1,2,0:T(2,128)S(1)} %copy.138, ...), kind=kOutput, calls=%fused_computation.16 | convolution fusion | flops 1095761920 | bytes 21598216 | tf_op jit(solution)/shard_map/rhqk,rkhd->rqhd/dot_general | solution.py:82
  91.5 1.4 copy.143
  92.9 8.0 %all-to-all-start.1 = ((bf16[32,128,2,128]{3,1,2,0:T(8,128)(2,1)}), bf16[32,128,2,128]{3,1,2,0:T(8,128)(2,1)}, u32[]{:S(2)}, u32[]{:S(2)}) async-start(bf16[32,128,2,128]{3,1,2,0:T(8,128)(2,1)} %copy.143), calls=%async_computation.1 | async-start | bytes 4194304 | tf_op jit(solution)/shard_map/all_to_all | solution.py:123
  101.1 1.3 copy.172
  102.8 0.9 broadcast_select_fusion
  103.8 22.9 %all-to-all-done.1 = bf16[32,128,2,128]{3,1,2,0:T(8,128)(2,1)} async-done(((bf16[32,128,2,128]{3,1,2,0:T(8,128)(2,1)}), bf16[32,128,2,128]{3,1,2,0:T(8,128)(2,1)}, u32[]{:S(2)}, u32[]{:S(2)}) %all-to-all-start.1) | async-done | bytes 2097184 | tf_op jit(solution)/shard_map/all_to_all | solution.py:123
  126.7 2.5 multiply_reduce_fusion
  129.4 2.9 convolution_add_fusion
  132.8 1.8 reduce-window.6
  135.3 3.4 scatter_custom_fusion
  138.7 77.3 %all-reduce.4.cloned.1.call-done = (f32[128,2048]{1,0:T(8,128)}, f32[65,2048]{1,0:T(8,128)}) async-done(((f32[128,2048]{1,0:T(8,128)}, f32[65,2048]{1,0:T(8,128)}), (f32[128,2048]{1,0:T(8,128)}, f32[65,2048]{1,0:T(8,128)})) %all-reduce.4.cloned.1.call-update) | async-done | bytes 1581072 | tf_op jit(solution)/shard_map/psum | solution.py:150
  216.1 0.8 slice.47
  216.9 1.4 multiply_reduce_fusion.2
  218.3 1.4 multiply_convert_fusion
  219.7 4.9 %gather_fusion = bf16[1024,256]{1,0:T(8,128)(2,1)} fusion(bf16[129,256]{1,0:T(8,128)(2,1)S(1)} %concatenate.7, s32[1024]{0:T(1024)S(1)} %fusion.61), kind=kCustom, calls=%fused_computation | custom fusion | bytes 1052672 | tf_op jit(solution)/shard_map/gather | solution.py:182
  224.7 17.6 %all_to_all.25 = bf16[32,2,16,256]{3,2,1,0:T(8,128)(2,1)S(1)} all-to-all(bf16[32,2,16,256]{3,2,1,0:T(8,128)(2,1)} %bitcast.186), channel_id=1, replica_groups=mesh['seq'=32,'tensor'=8] {'seq'}, dimensions={0} | all-to-all | bytes 1048576 | tf_op jit(solution)/shard_map/all_to_all | solution.py:183
  242.3 0.8 copy.155
  243.2 53.1 %all-gather.2.cloned.1.call-done = bf16[32,2,16,2048]{3,2,0,1:T(8,128)(2,1)} async-done(((bf16[32,2,16,256]{3,2,0,1:T(8,128)(2,1)}), bf16[32,2,16,2048]{3,2,0,1:T(8,128)(2,1)}) %all-gather.2.cloned.1.call-update) | async-done | bytes 4194320 | tf_op jit(solution)/shard_map/all_gather | solution.py:184
  296.3 4.6 %fusion.21 = f32[32,2,16,2,176]{4,2,3,0,1:T(8,128)S(1)} fusion(bf16[2,2048,2,176]{1,3,2,0:T(8,128)(2,1)S(1)} %copy-done, bf16[32,2,16,2048]{3,2,0,1:T(8,128)(2,1)} %all-gather.2.cloned.1.call-done), kind=kOutput, calls=%fused_computation.28 | convolution fusion | flops 1476395008 | bytes 8519680 | tf_op jit(solution)/shard_map/secd,edjf->secjf/dot_general | solution.py:185
  300.9 3.2 convert_bitcast_fusion
  304.2 2.6 fusion.73
  306.8 56.1 %reduce-scatter.5.cloned.1.call-done = bf16[32,2,16,256]{3,2,0,1:T(8,128)(2,1)} async-done(((bf16[32,2,16,2048]{3,2,0,1:T(8,128)(2,1)}), bf16[32,2,16,256]{3,2,0,1:T(8,128)(2,1)}) %reduce-scatter.5.cloned.1.call-update) | async-done | bytes 524304 | tf_op jit(solution)/shard_map/reduce_scatter | solution.py:192
  362.8 1.9 copy.157
  364.7 6.5 %all-to-all-start.4 = ((bf16[32,2,16,256]{3,2,1,0:T(8,128)(2,1)}), bf16[32,2,16,256]{3,2,1,0:T(8,128)(2,1)S(1)}, u32[]{:S(2)}, u32[]{:S(2)}) async-start(bf16[32,2,16,256]{3,2,1,0:T(8,128)(2,1)} %copy.157), calls=%async_computation.6 | async-start | bytes 1048576 | tf_op jit(solution)/shard_map/all_to_all | solution.py:195
  371.3 2.4 convolution_convert_fusion
  373.7 1.5 fusion.34
  375.4 6.6 %all-to-all-done.4 = bf16[32,2,16,256]{3,2,1,0:T(8,128)(2,1)S(1)} async-done(((bf16[32,2,16,256]{3,2,1,0:T(8,128)(2,1)}), bf16[32,2,16,256]{3,2,1,0:T(8,128)(2,1)S(1)}, u32[]{:S(2)}, u32[]{:S(2)}) %all-to-all-start.4) | async-done | bytes 524320 | tf_op jit(solution)/shard_map/all_to_all | solution.py:195
  382.0 3.3 gather_fusion.1
  385.2 2.1 reshape.193
  387.3 1.6 multiply_reduce_fusion.1
  388.9 23.4 %reduce-scatter.3.cloned.1.call-done = bf16[128,256]{1,0:T(8,128)(2,1)} async-done(((bf16[128,2048]{1,0:T(8,128)(2,1)}), bf16[128,256]{1,0:T(8,128)(2,1)}) %reduce-scatter.3.cloned.1.call-update) | async-done | bytes 65552 | tf_op jit(solution)/shard_map/reduce_scatter | solution.py:165
  412.4 1.6 add_convert_fusion
  (77 shorter events, 5.7 us)
Async XLA Ops:
  6.5 289.8 %copy-start = (bf16[2,2048,2,176]{1,3,2,0:T(8,128)(2,1)S(1)}, bf16[2,2048,2,176]{1,3,2,0:T(8,128)(2,1)}, u32[]{:S(2)}) copy-start(bf16[2,2048,2,176]{1,3,2,0:T(8,128)(2,1)} %param.26) | copy-start | bytes 8650756
  6.5 11.5 %copy-start.9 = (s32[8]{0:T(128)S(1)}, s32[8]{0:T(128)}, u32[]{:S(2)}) copy-start(s32[8]{0:T(128)} %param.21) | copy-start | bytes 100
  9.4 36.8 %all-to-all-start = ((bf16[32,128,256]{1,2,0:T(8,128)(2,1)}), bf16[32,128,256]{1,2,0:T(8,128)(2,1)}, u32[]{:S(2)}, u32[]{:S(2)}) async-start(bf16[32,128,256]{1,2,0:T(8,128)(2,1)} %broadcast_in_dim.208), calls=%async_computation | async-start | bytes 4194304 | tf_op jit(solution)/shard_map/all_to_all | solution.py:60
  18.2 39.7 %copy-start.4 = (bf16[128,256]{1,0:T(8,128)(2,1)S(1)}, bf16[128,256]{1,0:T(8,128)(2,1)}, u32[]{:S(2)}) copy-start(bf16[128,256]{1,0:T(8,128)(2,1)} %param.17) | copy-start | bytes 196612
  66.2 5.7 %copy-start.1 = (f32[8,2,512,512]{2,3,1,0:T(8,128)}, f32[8,2,512,512]{2,3,1,0:T(8,128)S(1)}, u32[]{:S(2)}) copy-start(f32[8,2,512,512]{2,3,1,0:T(8,128)S(1)} %get-tuple-element.12) | copy-start | bytes 50331652
  66.2 5.7 %copy-start.3 = (f32[8,2,512]{2,1,0:T(2,128)}, f32[8,2,512]{2,1,0:T(2,128)S(1)}, u32[]{:S(2)}) copy-start(f32[8,2,512]{2,1,0:T(2,128)S(1)} %get-tuple-element.11) | copy-start | bytes 98308
  74.7 18.2 %all-to-all-start.2 = ((f32[32,128,2,2]{1,2,3,0:T(2,128)}), f32[32,128,2,2]{1,2,3,0:T(2,128)S(1)}, u32[]{:S(2)}, u32[]{:S(2)}) async-start(f32[32,128,2,2]{1,2,3,0:T(2,128)} %copy.145), calls=%async_computation.2 | async-start | bytes 131072 | tf_op jit(solution)/shard_map/all_to_all | solution.py:120
  91.5 9.6 %copy-start.5 = (bf16[128,256]{1,0:T(8,128)(2,1)S(1)}, bf16[128,256]{1,0:T(8,128)(2,1)}, u32[]{:S(2)}) copy-start(bf16[128,256]{1,0:T(8,128)(2,1)} %param.15) | copy-start | bytes 196612
  92.9 9.6 %copy-start.7 = (bf16[256,64]{0,1:T(8,128)(2,1)S(1)}, bf16[256,64]{0,1:T(8,128)(2,1)}, u32[]{:S(2)}) copy-start(bf16[256,64]{0,1:T(8,128)(2,1)} %param.24) | copy-start | bytes 98308
  92.9 9.6 %copy-start.8 = (f32[256]{0:T(256)S(1)}, f32[256]{0:T(256)}, u32[]{:S(2)}) copy-start(f32[256]{0:T(256)} %param.23) | copy-start | bytes 3076
  92.9 33.8 %all-to-all-start.1 = ((bf16[32,128,2,128]{3,1,2,0:T(8,128)(2,1)}), bf16[32,128,2,128]{3,1,2,0:T(8,128)(2,1)}, u32[]{:S(2)}, u32[]{:S(2)}) async-start(bf16[32,128,2,128]{3,1,2,0:T(8,128)(2,1)} %copy.143), calls=%async_computation.1 | async-start | bytes 4194304 | tf_op jit(solution)/shard_map/all_to_all | solution.py:123
  100.9 115.1 %all-reduce.4.cloned.1.call-start = ((), (), s32[]{:S(2)}) async-start(), calls=%async_computation.10 | async-start | bytes 3276800 | tf_op jit(solution)/shard_map/psum | solution.py:150
  102.8 29.6 %copy-start.6 = (s32[128,6]{0,1:T(8,128)S(1)}, s32[128,6]{0,1:T(8,128)}, u32[]{:S(2)}) copy-start(s32[128,6]{0,1:T(8,128)} %param.25) | copy-start | bytes 9220
  132.3 164.0 %all-gather.2.cloned.1.call-start = ((), (), s32[]{:S(2)}) async-start(), calls=%async_computation.8 | async-start | bytes 4718592 | tf_op jit(solution)/shard_map/all_gather | solution.py:184
  219.7 84.5 %copy-start.2 = (bf16[128,2048]{1,0:T(8,128)(2,1)}, bf16[128,2048]{1,0:T(8,128)(2,1)S(1)}, u32[]{:S(2)}) copy-start(bf16[128,2048]{1,0:T(8,128)(2,1)S(1)} %multiply_convert_fusion) | copy-start | bytes 1572868
  243.1 119.7 %reduce-scatter.5.cloned.1.call-start = ((), (), s32[]{:S(2)}) async-start(), calls=%async_computation.9 | async-start | bytes 4718592 | tf_op jit(solution)/shard_map/reduce_scatter | solution.py:192
  296.3 4.6 %copy-start.10 = (bf16[2,176,2048]{2,1,0:T(8,128)(2,1)S(1)}, bf16[2,176,2048]{2,1,0:T(8,128)(2,1)}, u32[]{:S(2)}) copy-start(bf16[2,176,2048]{2,1,0:T(8,128)(2,1)} %param.27) | copy-start | bytes 4325380
  364.7 17.2 %all-to-all-start.4 = ((bf16[32,2,16,256]{3,2,1,0:T(8,128)(2,1)}), bf16[32,2,16,256]{3,2,1,0:T(8,128)(2,1)S(1)}, u32[]{:S(2)}, u32[]{:S(2)}) async-start(bf16[32,2,16,256]{3,2,1,0:T(8,128)(2,1)} %copy.157), calls=%async_computation.6 | async-start | bytes 1048576 | tf_op jit(solution)/shard_map/all_to_all | solution.py:195
  371.2 41.2 %reduce-scatter.3.cloned.1.call-start = ((), (), s32[]{:S(2)}) async-start(), calls=%async_computation.7 | async-start | bytes 589824 | tf_op jit(solution)/shard_map/reduce_scatter | solution.py:165
Sparse Core Ops, SparseCore 0:
  132.4 83.5 all-reduce.3
  243.2 53.0 all-gather.1
  304.3 58.4 reduce-scatter.4
  374.2 38.0 reduce-scatter.2

commit v4 on v2

--- a/solution.py
+++ b/solution.py
@@ -140,17 +140,23 @@
         projected.astype(jnp.bfloat16), "tensor", scatter_dimension=1, tiled=True
     ).astype(jnp.float32)
     stream = residual.astype(jnp.float32) + attn_out
-    square_total = lax.psum(jnp.sum(stream * stream, 1), "tensor")
-    inverse_rms = lax.rsqrt(square_total / D + epsilon)
+    gathered = lax.all_gather(
+        jnp.concatenate([stream, norm_gain[None], router.astype(jnp.float32).T], 0),
+        "tensor",
+        axis=1,
+        tiled=True,
+    )
+    stream_full = gathered[:tok_dev]
+    gain_full = gathered[tok_dev]
+    router_full = gathered[tok_dev + 1 :].T.astype(jnp.bfloat16)
+    inverse_rms = lax.rsqrt(jnp.sum(stream_full * stream_full, 1) / D + epsilon)
+    normed_full = (stream_full * inverse_rms[:, None] * gain_full).astype(jnp.bfloat16)
     normed = (stream * inverse_rms[:, None] * norm_gain).astype(jnp.bfloat16)
-    logits = lax.psum(
-        jnp.dot(normed, router, preferred_element_type=jnp.float32).astype(jnp.bfloat16), "tensor"
-    ).astype(jnp.float32)
+    logits = jnp.dot(normed_full, router_full, preferred_element_type=jnp.float32)
     matches = expert_ids[:, :, None] == lax.iota(jnp.int32, experts)[None, None, :]
     selected = jnp.sum(jnp.where(matches, logits[:, None, :], 0.0), 2)
     sigmoids = jax.nn.sigmoid(selected)
     gates = sigmoids / jnp.sum(sigmoids, 1, keepdims=True)
-    normed_full = lax.all_gather(normed, "tensor", axis=1, tiled=True)
     shared_pair = jnp.einsum(
         "td,dcf->tcf", normed_full, shared_gate_up, preferred_element_type=jnp.float32
     )

time: 392 us -> 410 us (1.046)
  waiting for transfers between devices: 183 us -> 257 us
  blocking collectives: 76.2 us -> 18.3 us
    psum x2 -> x0, blocking collectives: 41 us -> none  [the longest x1 27.3 us: shards(): lax.psum(jnp.dot(normed, router, preferred_element_type=jnp.float32).asty...]
    all_gather x0 -> x1, waiting for transfers between devices: none -> 24.2 us  [shards(): lax.all_gather(jnp.concatenate([stream, norm_gain[None], router.astype(jn...]
    reduce_scatter x1, waiting for transfers between devices: 1.87 us -> 23.4 us  [shards(): lax.psum_scatter(shared_term.astype(jnp.bfloat16), 'tensor', scatter_dime...]
    all_gather x1 -> x0, blocking collectives: 15.6 us -> none  [shards(): normed_full = lax.all_gather(normed, 'tensor', axis=1, tiled=True)]
    reduce_scatter x1, waiting for transfers between devices: 39.6 us -> 54.8 us  [shards(): lax.psum_scatter(expert_term.astype(jnp.bfloat16), 'tensor', scatter_dime...]
    reduce_scatter x1, waiting for transfers between devices: 34 us -> 40.1 us  [shards(): lax.psum_scatter(projected.astype(jnp.bfloat16), 'tensor', scatter_dimens...]
    all_to_all x1, waiting for transfers between devices: 0.01 us -> 5.73 us  [shards(): lax.all_to_all(expert_total, 'seq', split_axis=0, concat_axis=0, tiled=True)]
  transfers between devices with their start and end apart: 8 -> 9, of which waited for: 6 -> 8; matrix products, arithmetic and copies ran while one was open for 9% -> 9% of each run, Pallas kernels for 0% -> 0%
where the time goes in v4:
time: 410 us; the launch traced here: 408 us
  waiting for transfers between devices  257 us (63%)
  local copies, waits for them, and re-layouts  39.7 us (10%)
  matrix products  36.5 us (9%)
  starting transfers between devices  27.2 us (7%)
  blocking collectives  18.3 us (4%)
  other arithmetic  16.4 us (4%)
  between operations  13.6 us (3%)
    all_gather x1, waiting for transfers between devices, shards(): routed_rows = lax.all_gather(incoming, 'tensor', axis=3, tiled=True)  55 us
    reduce_scatter x1, waiting for transfers between devices, shards(): lax.psum_scatter(expert_term.astype(jnp.bfloat16), 'tensor', scatter_dime...  54.8 us
    reduce_scatter x1, waiting for transfers between devices, shards(): lax.psum_scatter(projected.astype(jnp.bfloat16), 'tensor', scatter_dimens...  40.1 us
    all_to_all x1, waiting for transfers between devices, shards(): lax.all_to_all(spread, 'seq', 0, 0, tiled=True).reshape(tokens, width_local)  28 us
    all_to_all x1, waiting for transfers between devices, shards(): lax.all_to_all(local_out.reshape(seq_count, tok_dev, heads_local, HD).ast...  25.4 us
    all_gather x1, waiting for transfers between devices, shards(): lax.all_gather(jnp.concatenate([stream, norm_gain[None], router.astype(jn...  24.2 us
    reduce_scatter x1, waiting for transfers between devices, shards(): lax.psum_scatter(shared_term.astype(jnp.bfloat16), 'tensor', scatter_dime...  23.4 us
    all_to_all x1, blocking collectives, shards(): lax.all_to_all(outgoing, 'seq', split_axis=0, concat_axis=0, tiled=True)  18.3 us
  transfers between devices with their start and end apart: 9, of which 8 were waited for; matrix products, arithmetic and copies ran while one was open for 9% of the time, Pallas kernels for 0%

profile of v4, /device:TPU:65, one launch (start us, length us, event | category | flops | bytes accessed | tf_op | source)
XLA Modules:
  0.0 408.3 jit_solution(718714878647191380)
XLA Ops:
  6.5 1.1 copy.129
  7.7 1.8 broadcast_in_dim.159
  9.4 8.5 %all-to-all-start = ((bf16[32,128,256]{1,2,0:T(8,128)(2,1)}), bf16[32,128,256]{1,2,0:T(8,128)(2,1)}, u32[]{:S(2)}, u32[]{:S(2)}) async-start(bf16[32,128,256]{1,2,0:T(8,128)(2,1)} %broadcast_in_dim.159), calls=%async_computation | async-start | bytes 4194304 | tf_op jit(solution)/shard_map/all_to_all | solution.py:60
  18.2 28.0 %all-to-all-done = bf16[32,128,256]{1,2,0:T(8,128)(2,1)} async-done(((bf16[32,128,256]{1,2,0:T(8,128)(2,1)}), bf16[32,128,256]{1,2,0:T(8,128)(2,1)}, u32[]{:S(2)}, u32[]{:S(2)}) %all-to-all-start) | async-done | bytes 2097184 | tf_op jit(solution)/shard_map/all_to_all | solution.py:60
  46.2 4.2 %copy.130 = bf16[32,128,256]{1,0,2:T(8,128)(2,1)} copy(bf16[32,128,256]{1,2,0:T(8,128)(2,1)} %all-to-all-done) | data formatting | bytes 4194304 | tf_op jit(solution)/shard_map/all_to_all | solution.py:60
  50.5 4.4 %reshape_reshape.3 = bf16[8,512,2,128]{1,0,3,2:T(8,128)(2,1)} reshape(bf16[32,128,256]{1,0,2:T(8,128)(2,1)} %copy.130) | data formatting | bytes 4194304 | tf_op jit(solution)/shard_map/reshape;reshape | solution.py:61
  54.8 2.1 constant_dynamic-slice_fusion
  57.0 1.0 copy.136
  58.0 1.2 select_reduce_fusion.1
  59.3 6.9 %select_reduce_fusion = (f32[8,2,512]{2,1,0:T(2,128)S(1)}, f32[8,2,512,512]{2,3,1,0:T(8,128)S(1)}) fusion(pred[8,512]{1,0:T(8,128)(4,1)S(1)} %broadcast_compare_fusion, bf16[8,512,2,128]{1,0,3,2:T(8,128)(2,1)} %reshape_reshape.3, bf16[8,512,256]{2,1,0:T(8,128)(2,1)} %param.19), kind=kOutput, calls=%fused_computation.4 | convolution fusion | flops 1086316544 | bytes 21008384 | tf_op jit(solution)/shard_map/rqhd,rkhd->rhqk/dot_general | solution.py:65
  66.2 3.6 fusion
  69.8 2.1 copy-done.1
  73.3 0.8 pad_maximum_fusion.1
  74.7 3.9 all-to-all-start.2
  78.6 0.8 copy.138
  79.4 0.8 copy.141
  80.2 1.1 convolution_bitcast_fusion
  81.4 10.0 %fusion.11 = bf16[8,512,2,128]{3,1,2,0:T(8,128)(2,1)S(1)} fusion(f32[8,2,512,512]{2,3,1,0:T(8,128)} %copy-done.1, f32[8,2,512]{2,1,0:T(2,128)} %copy-done.5, pred[8,512]{1,0:T(8,128)(4,1)S(1)} %broadcast_compare_fusion, f32[8,512,2]{1,2,0:T(2,128)S(1)} %copy.141, f32[512,2,128]{2,0,1:T(8,128)S(1)} %convolution_bitcast_fusion, f32[8,512,2]{1,2,0:T(2,128)S(1)} %copy.138, ...), kind=kOutput, calls=%fused_computation.16 | convolution fusion | flops 1095761920 | bytes 21598216 | tf_op jit(solution)/shard_map/rhqk,rkhd->rqhd/dot_general | solution.py:82
  91.5 1.4 copy.143
  92.9 8.0 %all-to-all-start.1 = ((bf16[32,128,2,128]{3,1,2,0:T(8,128)(2,1)}), bf16[32,128,2,128]{3,1,2,0:T(8,128)(2,1)}, u32[]{:S(2)}, u32[]{:S(2)}) async-start(bf16[32,128,2,128]{3,1,2,0:T(8,128)(2,1)} %copy.143), calls=%async_computation.1 | async-start | bytes 4194304 | tf_op jit(solution)/shard_map/all_to_all | solution.py:123
  101.2 25.4 %all-to-all-done.1 = bf16[32,128,2,128]{3,1,2,0:T(8,128)(2,1)} async-done(((bf16[32,128,2,128]{3,1,2,0:T(8,128)(2,1)}), bf16[32,128,2,128]{3,1,2,0:T(8,128)(2,1)}, u32[]{:S(2)}, u32[]{:S(2)}) %all-to-all-start.1) | async-done | bytes 2097184 | tf_op jit(solution)/shard_map/all_to_all | solution.py:123
  126.6 2.5 multiply_reduce_fusion
  129.3 2.4 convolution_convert_fusion.1
  131.8 40.1 %reduce-scatter.4.cloned.1.call-done = bf16[128,256]{1,0:T(8,128)(2,1)} async-done(((bf16[128,2048]{1,0:T(8,128)(2,1)}), bf16[128,256]{1,0:T(8,128)(2,1)}) %reduce-scatter.4.cloned.1.call-update) | async-done | bytes 65552 | tf_op jit(solution)/shard_map/reduce_scatter | solution.py:139
  171.9 0.9 convert_add_fusion
  174.0 1.8 reduce-window.6
  176.6 3.4 scatter_custom_fusion
  180.0 24.2 %all-gather.3.cloned.1.call-done = f32[193,2048]{1,0:T(8,128)} async-done(((f32[193,256]{1,0:T(8,128)}), f32[193,2048]{1,0:T(8,128)}) %all-gather.3.cloned.1.call-update) | async-done | bytes 1581072 | tf_op jit(solution)/shard_map/all_gather | solution.py:143
  204.2 1.4 multiply_reduce_fusion.2
  206.1 3.9 gather_fusion
  210.0 18.3 %all_to_all.25 = bf16[32,2,16,256]{3,2,1,0:T(8,128)(2,1)S(1)} all-to-all(bf16[32,2,16,256]{3,2,1,0:T(8,128)(2,1)S(1)} %bitcast.175), channel_id=1, replica_groups=mesh['seq'=32,'tensor'=8] {'seq'}, dimensions={0} | all-to-all | bytes 1048576 | tf_op jit(solution)/shard_map/all_to_all | solution.py:183
  228.4 0.8 copy.155
  229.3 55.0 %all-gather.5.cloned.1.call-done = bf16[32,2,16,2048]{3,2,0,1:T(8,128)(2,1)} async-done(((bf16[32,2,16,256]{3,2,0,1:T(8,128)(2,1)}), bf16[32,2,16,2048]{3,2,0,1:T(8,128)(2,1)}) %all-gather.5.cloned.1.call-update) | async-done | bytes 4194320 | tf_op jit(solution)/shard_map/all_gather | solution.py:184
  284.2 4.6 %fusion.21 = f32[32,2,16,2,176]{4,2,3,0,1:T(8,128)S(1)} fusion(bf16[2,2048,2,176]{1,3,2,0:T(8,128)(2,1)S(1)} %copy-done, bf16[32,2,16,2048]{3,2,0,1:T(8,128)(2,1)} %all-gather.5.cloned.1.call-done), kind=kOutput, calls=%fused_computation.28 | convolution fusion | flops 1476395008 | bytes 8519680 | tf_op jit(solution)/shard_map/secd,edjf->secjf/dot_general | solution.py:185
  288.9 3.2 convert_bitcast_fusion
  292.1 0.8 slice.52
  293.0 3.0 fusion.71
  296.0 54.8 %reduce-scatter.8.cloned.1.call-done = bf16[32,2,16,256]{3,2,0,1:T(8,128)(2,1)} async-done(((bf16[32,2,16,2048]{3,2,0,1:T(8,128)(2,1)}), bf16[32,2,16,256]{3,2,0,1:T(8,128)(2,1)}) %reduce-scatter.8.cloned.1.call-update) | async-done | bytes 524304 | tf_op jit(solution)/shard_map/reduce_scatter | solution.py:192
  350.8 1.9 copy.157
  352.7 6.5 %all-to-all-start.4 = ((bf16[32,2,16,256]{3,2,1,0:T(8,128)(2,1)}), bf16[32,2,16,256]{3,2,1,0:T(8,128)(2,1)S(1)}, u32[]{:S(2)}, u32[]{:S(2)}) async-start(bf16[32,2,16,256]{3,2,1,0:T(8,128)(2,1)} %copy.157), calls=%async_computation.7 | async-start | bytes 1048576 | tf_op jit(solution)/shard_map/all_to_all | solution.py:195
  359.2 2.4 convolution_convert_fusion
  361.6 1.7 fusion.34
  364.2 5.7 %all-to-all-done.4 = bf16[32,2,16,256]{3,2,1,0:T(8,128)(2,1)S(1)} async-done(((bf16[32,2,16,256]{3,2,1,0:T(8,128)(2,1)}), bf16[32,2,16,256]{3,2,1,0:T(8,128)(2,1)S(1)}, u32[]{:S(2)}, u32[]{:S(2)}) %all-to-all-start.4) | async-done | bytes 524320 | tf_op jit(solution)/shard_map/all_to_all | solution.py:195
  369.9 3.3 gather_fusion.1
  373.2 2.1 reshape.182
  375.3 1.6 multiply_reduce_fusion.1
  376.9 23.4 %reduce-scatter.6.cloned.1.call-done = bf16[128,256]{1,0:T(8,128)(2,1)} async-done(((bf16[128,2048]{1,0:T(8,128)(2,1)}), bf16[128,256]{1,0:T(8,128)(2,1)}) %reduce-scatter.6.cloned.1.call-update) | async-done | bytes 65552 | tf_op jit(solution)/shard_map/reduce_scatter | solution.py:165
  400.3 1.5 add_convert_fusion
  (79 shorter events, 6.4 us)
Async XLA Ops:
  6.5 277.7 %copy-start = (bf16[2,2048,2,176]{1,3,2,0:T(8,128)(2,1)S(1)}, bf16[2,2048,2,176]{1,3,2,0:T(8,128)(2,1)}, u32[]{:S(2)}) copy-start(bf16[2,2048,2,176]{1,3,2,0:T(8,128)(2,1)} %param.26) | copy-start | bytes 8650756
  7.6 10.4 %copy-start.13 = (s32[8]{0:T(128)S(1)}, s32[8]{0:T(128)}, u32[]{:S(2)}) copy-start(s32[8]{0:T(128)} %param.21) | copy-start | bytes 100
  9.4 36.8 %all-to-all-start = ((bf16[32,128,256]{1,2,0:T(8,128)(2,1)}), bf16[32,128,256]{1,2,0:T(8,128)(2,1)}, u32[]{:S(2)}, u32[]{:S(2)}) async-start(bf16[32,128,256]{1,2,0:T(8,128)(2,1)} %broadcast_in_dim.159), calls=%async_computation | async-start | bytes 4194304 | tf_op jit(solution)/shard_map/all_to_all | solution.py:60
  50.5 7.5 %copy-start.6 = (bf16[128,256]{1,0:T(8,128)(2,1)S(1)}, bf16[128,256]{1,0:T(8,128)(2,1)}, u32[]{:S(2)}) copy-start(bf16[128,256]{1,0:T(8,128)(2,1)} %param.17) | copy-start | bytes 196612
  66.2 5.7 %copy-start.1 = (f32[8,2,512,512]{2,3,1,0:T(8,128)}, f32[8,2,512,512]{2,3,1,0:T(8,128)S(1)}, u32[]{:S(2)}) copy-start(f32[8,2,512,512]{2,3,1,0:T(8,128)S(1)} %get-tuple-element.10) | copy-start | bytes 50331652
  66.2 5.7 %copy-start.5 = (f32[8,2,512]{2,1,0:T(2,128)}, f32[8,2,512]{2,1,0:T(2,128)S(1)}, u32[]{:S(2)}) copy-start(f32[8,2,512]{2,1,0:T(2,128)S(1)} %get-tuple-element.9) | copy-start | bytes 98308
  74.7 18.2 %all-to-all-start.2 = ((f32[32,128,2,2]{1,2,3,0:T(2,128)}), f32[32,128,2,2]{1,2,3,0:T(2,128)S(1)}, u32[]{:S(2)}, u32[]{:S(2)}) async-start(f32[32,128,2,2]{1,2,3,0:T(2,128)} %copy.145), calls=%async_computation.2 | async-start | bytes 131072 | tf_op jit(solution)/shard_map/all_to_all | solution.py:120
  92.9 33.6 %all-to-all-start.1 = ((bf16[32,128,2,128]{3,1,2,0:T(8,128)(2,1)}), bf16[32,128,2,128]{3,1,2,0:T(8,128)(2,1)}, u32[]{:S(2)}, u32[]{:S(2)}) async-start(bf16[32,128,2,128]{3,1,2,0:T(8,128)(2,1)} %copy.143), calls=%async_computation.1 | async-start | bytes 4194304 | tf_op jit(solution)/shard_map/all_to_all | solution.py:123
  101.0 30.8 %copy-start.8 = (bf16[256,64]{0,1:T(8,128)(2,1)S(1)}, bf16[256,64]{0,1:T(8,128)(2,1)}, u32[]{:S(2)}) copy-start(bf16[256,64]{0,1:T(8,128)(2,1)} %param.24) | copy-start | bytes 98308
  101.0 70.9 %copy-start.2 = (bf16[128,256]{1,0:T(8,128)(2,1)S(1)}, bf16[128,256]{1,0:T(8,128)(2,1)}, u32[]{:S(2)}) copy-start(bf16[128,256]{1,0:T(8,128)(2,1)} %param.15) | copy-start | bytes 196612
  101.0 71.9 %copy-start.11 = (f32[256]{0:T(256)S(1)}, f32[256]{0:T(256)}, u32[]{:S(2)}) copy-start(f32[256]{0:T(256)} %param.23) | copy-start | bytes 3076
  101.0 70.9 %reduce-scatter.4.cloned.1.call-start = ((), (), s32[]{:S(2)}) async-start(), calls=%async_computation.8 | async-start | bytes 589824 | tf_op jit(solution)/shard_map/reduce_scatter | solution.py:139
  101.1 72.5 %copy-start.7 = (s32[128,6]{0,1:T(8,128)S(1)}, s32[128,6]{0,1:T(8,128)}, u32[]{:S(2)}) copy-start(s32[128,6]{0,1:T(8,128)} %param.25) | copy-start | bytes 9220
  129.2 76.4 %copy-start.12 = (f32[256]{0:T(256)S(1)}, f32[256]{0:T(256)}, u32[]{:S(2)}) copy-start(f32[256]{0:T(256)} %param.23) | copy-start | bytes 3076
  131.7 72.5 %all-gather.3.cloned.1.call-start = ((), (), s32[]{:S(2)}) async-start(), calls=%async_computation.9 | async-start | bytes 1843200 | tf_op jit(solution)/shard_map/all_gather | solution.py:143
  171.9 33.7 %copy-start.4 = (bf16[128,256]{1,0:T(8,128)(2,1)S(1)}, bf16[128,256]{1,0:T(8,128)(2,1)}, u32[]{:S(2)}) copy-start(bf16[128,256]{1,0:T(8,128)(2,1)} %reduce-scatter.4.cloned.1.call-done) | copy-start | bytes 196612
  173.6 110.7 %all-gather.5.cloned.1.call-start = ((), (), s32[]{:S(2)}) async-start(), calls=%async_computation.11 | async-start | bytes 4718592 | tf_op jit(solution)/shard_map/all_gather | solution.py:184
  205.6 0.5 copy-start.9
  229.2 121.6 %reduce-scatter.8.cloned.1.call-start = ((), (), s32[]{:S(2)}) async-start(), calls=%async_computation.12 | async-start | bytes 4718592 | tf_op jit(solution)/shard_map/reduce_scatter | solution.py:192
  284.2 4.6 %copy-start.14 = (bf16[2,176,2048]{2,1,0:T(8,128)(2,1)S(1)}, bf16[2,176,2048]{2,1,0:T(8,128)(2,1)}, u32[]{:S(2)}) copy-start(bf16[2,176,2048]{2,1,0:T(8,128)(2,1)} %param.27) | copy-start | bytes 4325380
  292.1 0.9 copy-start.10
  352.7 17.3 %all-to-all-start.4 = ((bf16[32,2,16,256]{3,2,1,0:T(8,128)(2,1)}), bf16[32,2,16,256]{3,2,1,0:T(8,128)(2,1)S(1)}, u32[]{:S(2)}, u32[]{:S(2)}) async-start(bf16[32,2,16,256]{3,2,1,0:T(8,128)(2,1)} %copy.157), calls=%async_computation.7 | async-start | bytes 1048576 | tf_op jit(solution)/shard_map/all_to_all | solution.py:195
  359.2 41.1 %reduce-scatter.6.cloned.1.call-start = ((), (), s32[]{:S(2)}) async-start(), calls=%async_computation.10 | async-start | bytes 589824 | tf_op jit(solution)/shard_map/reduce_scatter | solution.py:165
  369.9 30.3 %copy-start.3 = (bf16[128,256]{1,0:T(8,128)(2,1)S(1)}, bf16[128,256]{1,0:T(8,128)(2,1)}, u32[]{:S(2)}) copy-start(bf16[128,256]{1,0:T(8,128)(2,1)} %param.15) | copy-start | bytes 196612
Sparse Core Ops, SparseCore 0:
  131.8 40.0 reduce-scatter.3
  173.7 30.3 all-gather.2
  229.3 54.8 all-gather.4
  292.3 58.4 reduce-scatter.7
  362.2 38.0 reduce-scatter.5

commit v5 on v4

--- a/solution.py
+++ b/solution.py
@@ -162,9 +162,8 @@
     )
     shared_act = (jax.nn.silu(shared_pair[:, 0]) * shared_pair[:, 1]).astype(jnp.bfloat16)
     shared_term = jnp.dot(shared_act, shared_down, preferred_element_type=jnp.float32)
-    shared_out = lax.psum_scatter(
-        shared_term.astype(jnp.bfloat16), "tensor", scatter_dimension=1, tiled=True
-    ).astype(jnp.float32)
+    shared_term, normed = lax.optimization_barrier((shared_term.astype(jnp.bfloat16), normed))
+    shared_out = lax.psum_scatter(shared_term, "tensor", scatter_dimension=1, tiled=True)
     cap = tensor_count * (
         (4 * tok_dev * topk + 3 * experts * tensor_count - 1) // (3 * experts * tensor_count)
     )
@@ -181,6 +180,7 @@
     padded_local = jnp.concatenate([normed, jnp.zeros((1, width_local), jnp.bfloat16)], 0)
     outgoing = padded_local[source_rows].reshape(seq_count, exp_dev, cap, width_local)
     incoming = lax.all_to_all(outgoing, "seq", split_axis=0, concat_axis=0, tiled=True)
+    incoming, shared_out = lax.optimization_barrier((incoming, shared_out))
     routed_rows = lax.all_gather(incoming, "tensor", axis=3, tiled=True)
     expert_pair = jnp.einsum(
         "secd,edjf->secjf", routed_rows, expert_gate_up, preferred_element_type=jnp.float32
@@ -197,7 +197,7 @@
         tok_dev, topk, width_local
     )
     mixture = jnp.sum(gates[..., None] * picked.astype(jnp.float32), 1)
-    return (stream + shared_out + mixture).astype(jnp.bfloat16)
+    return (stream + shared_out.astype(jnp.float32) + mixture).astype(jnp.bfloat16)
 
 
 def solution(mesh):

time: 410 us -> 407 us (level)
    reduce_scatter x1, waiting for transfers between devices: 23.4 us -> 13.7 us  [shards(): lax.psum_scatter(shared_term, 'tensor', scatter_dimension=1, tiled=True)]
  transfers between devices with their start and end apart: 9 -> 9, of which waited for: 8 -> 8; matrix products, arithmetic and copies ran while one was open for 9% -> 7% of each run, Pallas kernels for 0% -> 0%
where the time goes in v5:
time: 407 us; the launch traced here: 406 us
  waiting for transfers between devices  253 us (62%)
  local copies, waits for them, and re-layouts  40.4 us (10%)
  matrix products  34.6 us (9%)
  starting transfers between devices  27.2 us (7%)
  blocking collectives  19.7 us (5%)
  other arithmetic  17 us (4%)
  between operations  13.6 us (3%)
    reduce_scatter x1, waiting for transfers between devices, shards(): lax.psum_scatter(expert_term.astype(jnp.bfloat16), 'tensor', scatter_dime...  58.6 us
    all_gather x1, waiting for transfers between devices, shards(): routed_rows = lax.all_gather(incoming, 'tensor', axis=3, tiled=True)  55.6 us
    reduce_scatter x1, waiting for transfers between devices, shards(): lax.psum_scatter(projected.astype(jnp.bfloat16), 'tensor', scatter_dimens...  40 us
    all_to_all x1, waiting for transfers between devices, shards(): lax.all_to_all(spread, 'seq', 0, 0, tiled=True).reshape(tokens, width_local)  28 us
    all_to_all x1, waiting for transfers between devices, shards(): lax.all_to_all(local_out.reshape(seq_count, tok_dev, heads_local, HD).ast...  25.4 us
    all_gather x1, waiting for transfers between devices, shards(): lax.all_gather(jnp.concatenate([stream, norm_gain[None], router.astype(jn...  24.4 us
    all_to_all x1, blocking collectives, shards(): lax.all_to_all(outgoing, 'seq', split_axis=0, concat_axis=0, tiled=True)  19.7 us
    reduce_scatter x1, waiting for transfers between devices, shards(): lax.psum_scatter(shared_term, 'tensor', scatter_dimension=1, tiled=True)  13.7 us
  transfers between devices with their start and end apart: 9, of which 8 were waited for; matrix products, arithmetic and copies ran while one was open for 7% of the time, Pallas kernels for 0%

profile of v5, /device:TPU:65, one launch (start us, length us, event | category | flops | bytes accessed | tf_op | source)
XLA Modules:
  0.0 405.9 jit_solution(16583238352200268941)
XLA Ops:
  6.5 1.1 copy.129
  7.7 1.8 broadcast_in_dim.159
  9.4 8.5 %all-to-all-start = ((bf16[32,128,256]{1,2,0:T(8,128)(2,1)}), bf16[32,128,256]{1,2,0:T(8,128)(2,1)}, u32[]{:S(2)}, u32[]{:S(2)}) async-start(bf16[32,128,256]{1,2,0:T(8,128)(2,1)} %broadcast_in_dim.159), calls=%async_computation | async-start | bytes 4194304 | tf_op jit(solution)/shard_map/all_to_all | solution.py:60
  18.2 28.0 %all-to-all-done = bf16[32,128,256]{1,2,0:T(8,128)(2,1)} async-done(((bf16[32,128,256]{1,2,0:T(8,128)(2,1)}), bf16[32,128,256]{1,2,0:T(8,128)(2,1)}, u32[]{:S(2)}, u32[]{:S(2)}) %all-to-all-start) | async-done | bytes 2097184 | tf_op jit(solution)/shard_map/all_to_all | solution.py:60
  46.2 4.2 %copy.130 = bf16[32,128,256]{1,0,2:T(8,128)(2,1)} copy(bf16[32,128,256]{1,2,0:T(8,128)(2,1)} %all-to-all-done) | data formatting | bytes 4194304 | tf_op jit(solution)/shard_map/all_to_all | solution.py:60
  50.5 4.4 %reshape_reshape.3 = bf16[8,512,2,128]{1,0,3,2:T(8,128)(2,1)} reshape(bf16[32,128,256]{1,0,2:T(8,128)(2,1)} %copy.130) | data formatting | bytes 4194304 | tf_op jit(solution)/shard_map/reshape;reshape | solution.py:61
  54.8 2.1 constant_dynamic-slice_fusion
  57.0 1.0 copy.136
  58.0 1.2 select_reduce_fusion.1
  59.3 6.9 %select_reduce_fusion = (f32[8,2,512]{2,1,0:T(2,128)S(1)}, f32[8,2,512,512]{2,3,1,0:T(8,128)S(1)}) fusion(pred[8,512]{1,0:T(8,128)(4,1)S(1)} %broadcast_compare_fusion, bf16[8,512,2,128]{1,0,3,2:T(8,128)(2,1)} %reshape_reshape.3, bf16[8,512,256]{2,1,0:T(8,128)(2,1)} %param.19), kind=kOutput, calls=%fused_computation.4 | convolution fusion | flops 1086316544 | bytes 21008384 | tf_op jit(solution)/shard_map/rqhd,rkhd->rhqk/dot_general | solution.py:65
  66.2 3.6 fusion
  69.8 2.1 copy-done.1
  73.3 0.8 pad_maximum_fusion.1
  74.7 3.9 all-to-all-start.2
  78.6 0.8 copy.138
  79.4 0.8 copy.141
  80.2 1.1 convolution_bitcast_fusion
  81.4 10.0 %fusion.11 = bf16[8,512,2,128]{3,1,2,0:T(8,128)(2,1)S(1)} fusion(f32[8,2,512,512]{2,3,1,0:T(8,128)} %copy-done.1, f32[8,2,512]{2,1,0:T(2,128)} %copy-done.5, pred[8,512]{1,0:T(8,128)(4,1)S(1)} %broadcast_compare_fusion, f32[8,512,2]{1,2,0:T(2,128)S(1)} %copy.141, f32[512,2,128]{2,0,1:T(8,128)S(1)} %convolution_bitcast_fusion, f32[8,512,2]{1,2,0:T(2,128)S(1)} %copy.138, ...), kind=kOutput, calls=%fused_computation.16 | convolution fusion | flops 1095761920 | bytes 21598216 | tf_op jit(solution)/shard_map/rhqk,rkhd->rqhd/dot_general | solution.py:82
  91.5 1.4 copy.143
  92.9 8.0 %all-to-all-start.1 = ((bf16[32,128,2,128]{3,1,2,0:T(8,128)(2,1)}), bf16[32,128,2,128]{3,1,2,0:T(8,128)(2,1)}, u32[]{:S(2)}, u32[]{:S(2)}) async-start(bf16[32,128,2,128]{3,1,2,0:T(8,128)(2,1)} %copy.143), calls=%async_computation.1 | async-start | bytes 4194304 | tf_op jit(solution)/shard_map/all_to_all | solution.py:123
  101.2 25.4 %all-to-all-done.1 = bf16[32,128,2,128]{3,1,2,0:T(8,128)(2,1)} async-done(((bf16[32,128,2,128]{3,1,2,0:T(8,128)(2,1)}), bf16[32,128,2,128]{3,1,2,0:T(8,128)(2,1)}, u32[]{:S(2)}, u32[]{:S(2)}) %all-to-all-start.1) | async-done | bytes 2097184 | tf_op jit(solution)/shard_map/all_to_all | solution.py:123
  126.6 2.5 multiply_reduce_fusion
  129.3 2.4 convolution_convert_fusion.1
  131.8 40.0 %reduce-scatter.4.cloned.1.call-done = bf16[128,256]{1,0:T(8,128)(2,1)} async-done(((bf16[128,2048]{1,0:T(8,128)(2,1)}), bf16[128,256]{1,0:T(8,128)(2,1)}) %reduce-scatter.4.cloned.1.call-update) | async-done | bytes 65552 | tf_op jit(solution)/shard_map/reduce_scatter | solution.py:139
  171.8 0.9 convert_add_fusion
  173.8 1.8 reduce-window.6
  176.4 3.4 scatter_custom_fusion
  179.8 24.4 %all-gather.3.cloned.1.call-done = f32[193,2048]{1,0:T(8,128)} async-done(((f32[193,256]{1,0:T(8,128)}), f32[193,2048]{1,0:T(8,128)}) %all-gather.3.cloned.1.call-update) | async-done | bytes 1581072 | tf_op jit(solution)/shard_map/all_gather | solution.py:143
  204.2 1.4 multiply_reduce_fusion.2
  205.7 0.8 slice.52
  206.5 2.3 fusion.71
  208.8 1.1 convolution_convert_fusion
  210.2 5.0 %gather_fusion = bf16[1024,256]{1,0:T(8,128)(2,1)} fusion(bf16[129,256]{1,0:T(8,128)(2,1)S(1)} %concatenate.7, s32[1024]{0:T(1024)S(1)} %fusion.61), kind=kCustom, calls=%fused_computation | custom fusion | bytes 1052672 | tf_op jit(solution)/shard_map/gather | solution.py:181
  215.1 19.7 %all_to_all.25 = bf16[32,2,16,256]{3,2,1,0:T(8,128)(2,1)S(1)} all-to-all(bf16[32,2,16,256]{3,2,1,0:T(8,128)(2,1)} %bitcast.175), channel_id=1, replica_groups=mesh['seq'=32,'tensor'=8] {'seq'}, dimensions={0} | all-to-all | bytes 1048576 | tf_op jit(solution)/shard_map/all_to_all | solution.py:182
  234.9 13.7 %reduce-scatter.6.cloned.1.call-done = bf16[128,256]{1,0:T(8,128)(2,1)} async-done(((bf16[128,2048]{1,0:T(8,128)(2,1)}), bf16[128,256]{1,0:T(8,128)(2,1)}) %reduce-scatter.6.cloned.1.call-update) | async-done | bytes 65552 | tf_op jit(solution)/shard_map/reduce_scatter | solution.py:166
  248.6 0.8 copy.155
  249.5 55.6 %all-gather.5.cloned.1.call-done = bf16[32,2,16,2048]{3,2,0,1:T(8,128)(2,1)} async-done(((bf16[32,2,16,256]{3,2,0,1:T(8,128)(2,1)}), bf16[32,2,16,2048]{3,2,0,1:T(8,128)(2,1)}) %all-gather.5.cloned.1.call-update) | async-done | bytes 4194320 | tf_op jit(solution)/shard_map/all_gather | solution.py:184
  305.1 4.6 %fusion.21 = f32[32,2,16,2,176]{4,2,3,0,1:T(8,128)S(1)} fusion(bf16[2,2048,2,176]{1,3,2,0:T(8,128)(2,1)S(1)} %copy-done, bf16[32,2,16,2048]{3,2,0,1:T(8,128)(2,1)} %all-gather.5.cloned.1.call-done), kind=kOutput, calls=%fused_computation.28 | convolution fusion | flops 1476395008 | bytes 8519680 | tf_op jit(solution)/shard_map/secd,edjf->secjf/dot_general | solution.py:185
  309.8 3.2 convert_bitcast_fusion
  313.0 58.6 %reduce-scatter.8.cloned.1.call-done = bf16[32,2,16,256]{3,2,0,1:T(8,128)(2,1)} async-done(((bf16[32,2,16,2048]{3,2,0,1:T(8,128)(2,1)}), bf16[32,2,16,256]{3,2,0,1:T(8,128)(2,1)}) %reduce-scatter.8.cloned.1.call-update) | async-done | bytes 524304 | tf_op jit(solution)/shard_map/reduce_scatter | solution.py:192
  371.6 1.9 copy.157
  373.5 6.5 %all-to-all-start.4 = ((bf16[32,2,16,256]{3,2,1,0:T(8,128)(2,1)}), bf16[32,2,16,256]{3,2,1,0:T(8,128)(2,1)S(1)}, u32[]{:S(2)}, u32[]{:S(2)}) async-start(bf16[32,2,16,256]{3,2,1,0:T(8,128)(2,1)} %copy.157), calls=%async_computation.7 | async-start | bytes 1048576 | tf_op jit(solution)/shard_map/all_to_all | solution.py:195
  380.6 1.8 fusion.34
  383.2 7.5 %all-to-all-done.4 = bf16[32,2,16,256]{3,2,1,0:T(8,128)(2,1)S(1)} async-done(((bf16[32,2,16,256]{3,2,1,0:T(8,128)(2,1)}), bf16[32,2,16,256]{3,2,1,0:T(8,128)(2,1)S(1)}, u32[]{:S(2)}, u32[]{:S(2)}) %all-to-all-start.4) | async-done | bytes 524320 | tf_op jit(solution)/shard_map/all_to_all | solution.py:195
  390.8 3.4 gather_fusion.1
  394.2 2.1 reshape.182
  396.3 1.6 multiply_reduce_fusion.1
  397.9 1.5 add_convert_fusion
  (75 shorter events, 6.5 us)
Async XLA Ops:
  6.5 298.6 %copy-start = (bf16[2,2048,2,176]{1,3,2,0:T(8,128)(2,1)S(1)}, bf16[2,2048,2,176]{1,3,2,0:T(8,128)(2,1)}, u32[]{:S(2)}) copy-start(bf16[2,2048,2,176]{1,3,2,0:T(8,128)(2,1)} %param.26) | copy-start | bytes 8650756
  7.6 10.4 %copy-start.11 = (s32[8]{0:T(128)S(1)}, s32[8]{0:T(128)}, u32[]{:S(2)}) copy-start(s32[8]{0:T(128)} %param.21) | copy-start | bytes 100
  9.4 36.8 %all-to-all-start = ((bf16[32,128,256]{1,2,0:T(8,128)(2,1)}), bf16[32,128,256]{1,2,0:T(8,128)(2,1)}, u32[]{:S(2)}, u32[]{:S(2)}) async-start(bf16[32,128,256]{1,2,0:T(8,128)(2,1)} %broadcast_in_dim.159), calls=%async_computation | async-start | bytes 4194304 | tf_op jit(solution)/shard_map/all_to_all | solution.py:60
  50.5 7.5 %copy-start.6 = (bf16[128,256]{1,0:T(8,128)(2,1)S(1)}, bf16[128,256]{1,0:T(8,128)(2,1)}, u32[]{:S(2)}) copy-start(bf16[128,256]{1,0:T(8,128)(2,1)} %param.17) | copy-start | bytes 196612
  66.2 5.7 %copy-start.1 = (f32[8,2,512,512]{2,3,1,0:T(8,128)}, f32[8,2,512,512]{2,3,1,0:T(8,128)S(1)}, u32[]{:S(2)}) copy-start(f32[8,2,512,512]{2,3,1,0:T(8,128)S(1)} %get-tuple-element.18) | copy-start | bytes 50331652
  66.2 5.7 %copy-start.5 = (f32[8,2,512]{2,1,0:T(2,128)}, f32[8,2,512]{2,1,0:T(2,128)S(1)}, u32[]{:S(2)}) copy-start(f32[8,2,512]{2,1,0:T(2,128)S(1)} %get-tuple-element.17) | copy-start | bytes 98308
  74.7 18.2 %all-to-all-start.2 = ((f32[32,128,2,2]{1,2,3,0:T(2,128)}), f32[32,128,2,2]{1,2,3,0:T(2,128)S(1)}, u32[]{:S(2)}, u32[]{:S(2)}) async-start(f32[32,128,2,2]{1,2,3,0:T(2,128)} %copy.145), calls=%async_computation.2 | async-start | bytes 131072 | tf_op jit(solution)/shard_map/all_to_all | solution.py:120
  92.9 33.6 %all-to-all-start.1 = ((bf16[32,128,2,128]{3,1,2,0:T(8,128)(2,1)}), bf16[32,128,2,128]{3,1,2,0:T(8,128)(2,1)}, u32[]{:S(2)}, u32[]{:S(2)}) async-start(bf16[32,128,2,128]{3,1,2,0:T(8,128)(2,1)} %copy.143), calls=%async_computation.1 | async-start | bytes 4194304 | tf_op jit(solution)/shard_map/all_to_all | solution.py:123
  101.0 30.8 %copy-start.8 = (bf16[256,64]{0,1:T(8,128)(2,1)S(1)}, bf16[256,64]{0,1:T(8,128)(2,1)}, u32[]{:S(2)}) copy-start(bf16[256,64]{0,1:T(8,128)(2,1)} %param.24) | copy-start | bytes 98308
  101.0 70.8 %copy-start.3 = (bf16[128,256]{1,0:T(8,128)(2,1)S(1)}, bf16[128,256]{1,0:T(8,128)(2,1)}, u32[]{:S(2)}) copy-start(bf16[128,256]{1,0:T(8,128)(2,1)} %param.15) | copy-start | bytes 196612
  101.0 71.7 %copy-start.10 = (f32[256]{0:T(256)S(1)}, f32[256]{0:T(256)}, u32[]{:S(2)}) copy-start(f32[256]{0:T(256)} %param.23) | copy-start | bytes 3076
  101.0 70.8 %reduce-scatter.4.cloned.1.call-start = ((), (), s32[]{:S(2)}) async-start(), calls=%async_computation.8 | async-start | bytes 589824 | tf_op jit(solution)/shard_map/reduce_scatter | solution.py:139
  101.1 72.3 %copy-start.7 = (s32[128,6]{0,1:T(8,128)S(1)}, s32[128,6]{0,1:T(8,128)}, u32[]{:S(2)}) copy-start(s32[128,6]{0,1:T(8,128)} %param.25) | copy-start | bytes 9220
  131.7 72.5 %all-gather.3.cloned.1.call-start = ((), (), s32[]{:S(2)}) async-start(), calls=%async_computation.9 | async-start | bytes 1843200 | tf_op jit(solution)/shard_map/all_gather | solution.py:143
  173.4 75.2 %reduce-scatter.6.cloned.1.call-start = ((), (), s32[]{:S(2)}) async-start(), calls=%async_computation.10 | async-start | bytes 589824 | tf_op jit(solution)/shard_map/reduce_scatter | solution.py:166
  175.6 34.3 %copy-start.4 = (bf16[128,256]{1,0:T(8,128)(2,1)S(1)}, bf16[128,256]{1,0:T(8,128)(2,1)}, u32[]{:S(2)}) copy-start(bf16[128,256]{1,0:T(8,128)(2,1)} %reduce-scatter.4.cloned.1.call-done) | copy-start | bytes 196612
  204.2 4.6 %copy-start.2 = (bf16[176,2048]{1,0:T(8,128)(2,1)S(1)}, bf16[176,2048]{1,0:T(8,128)(2,1)}, u32[]{:S(2)}) copy-start(bf16[176,2048]{1,0:T(8,128)(2,1)} %param.29) | copy-start | bytes 2162692
  205.6 4.5 %copy-start.9 = (f32[128]{0:T(128)}, f32[128]{0:T(128)S(1)}, u32[]{:S(2)}) copy-start(f32[128]{0:T(128)S(1)} %add_rsqrt_fusion) | copy-start | bytes 1540
  210.1 95.0 %all-gather.5.cloned.1.call-start = ((), (), s32[]{:S(2)}) async-start(), calls=%async_computation.11 | async-start | bytes 4718592 | tf_op jit(solution)/shard_map/all_gather | solution.py:184
  249.4 122.2 %reduce-scatter.8.cloned.1.call-start = ((), (), s32[]{:S(2)}) async-start(), calls=%async_computation.12 | async-start | bytes 4718592 | tf_op jit(solution)/shard_map/reduce_scatter | solution.py:192
  305.1 4.6 %copy-start.12 = (bf16[2,176,2048]{2,1,0:T(8,128)(2,1)S(1)}, bf16[2,176,2048]{2,1,0:T(8,128)(2,1)}, u32[]{:S(2)}) copy-start(bf16[2,176,2048]{2,1,0:T(8,128)(2,1)} %param.27) | copy-start | bytes 4325380
  373.5 17.3 %all-to-all-start.4 = ((bf16[32,2,16,256]{3,2,1,0:T(8,128)(2,1)}), bf16[32,2,16,256]{3,2,1,0:T(8,128)(2,1)S(1)}, u32[]{:S(2)}, u32[]{:S(2)}) async-start(bf16[32,2,16,256]{3,2,1,0:T(8,128)(2,1)} %copy.157), calls=%async_computation.7 | async-start | bytes 1048576 | tf_op jit(solution)/shard_map/all_to_all | solution.py:195
Sparse Core Ops, SparseCore 0:
  131.8 39.9 reduce-scatter.3
  173.6 30.5 all-gather.2
  210.2 38.3 reduce-scatter.5
  250.3 54.7 all-gather.4
  313.1 58.4 reduce-scatter.7

commit v6 on v5

--- a/solution.py
+++ b/solution.py
@@ -151,7 +151,6 @@
     router_full = gathered[tok_dev + 1 :].T.astype(jnp.bfloat16)
     inverse_rms = lax.rsqrt(jnp.sum(stream_full * stream_full, 1) / D + epsilon)
     normed_full = (stream_full * inverse_rms[:, None] * gain_full).astype(jnp.bfloat16)
-    normed = (stream * inverse_rms[:, None] * norm_gain).astype(jnp.bfloat16)
     logits = jnp.dot(normed_full, router_full, preferred_element_type=jnp.float32)
     matches = expert_ids[:, :, None] == lax.iota(jnp.int32, experts)[None, None, :]
     selected = jnp.sum(jnp.where(matches, logits[:, None, :], 0.0), 2)
@@ -162,7 +161,9 @@
     )
     shared_act = (jax.nn.silu(shared_pair[:, 0]) * shared_pair[:, 1]).astype(jnp.bfloat16)
     shared_term = jnp.dot(shared_act, shared_down, preferred_element_type=jnp.float32)
-    shared_term, normed = lax.optimization_barrier((shared_term.astype(jnp.bfloat16), normed))
+    shared_term, normed_full = lax.optimization_barrier(
+        (shared_term.astype(jnp.bfloat16), normed_full)
+    )
     shared_out = lax.psum_scatter(shared_term, "tensor", scatter_dimension=1, tiled=True)
     cap = tensor_count * (
         (4 * tok_dev * topk + 3 * experts * tensor_count - 1) // (3 * experts * tensor_count)
@@ -177,11 +178,10 @@
         .at[slot_index]
         .set(lax.iota(jnp.int32, flat_ids.shape[0]) // topk)
     )
-    padded_local = jnp.concatenate([normed, jnp.zeros((1, width_local), jnp.bfloat16)], 0)
-    outgoing = padded_local[source_rows].reshape(seq_count, exp_dev, cap, width_local)
-    incoming = lax.all_to_all(outgoing, "seq", split_axis=0, concat_axis=0, tiled=True)
-    incoming, shared_out = lax.optimization_barrier((incoming, shared_out))
-    routed_rows = lax.all_gather(incoming, "tensor", axis=3, tiled=True)
+    padded_full = jnp.concatenate([normed_full, jnp.zeros((1, D), jnp.bfloat16)], 0)
+    outgoing = padded_full[source_rows].reshape(seq_count, exp_dev, cap, D)
+    routed_rows = lax.all_to_all(outgoing, "seq", split_axis=0, concat_axis=0, tiled=True)
+    routed_rows, shared_out = lax.optimization_barrier((routed_rows, shared_out))
     expert_pair = jnp.einsum(
         "secd,edjf->secjf", routed_rows, expert_gate_up, preferred_element_type=jnp.float32
     )

time: 407 us -> 392 us (0.963)
  blocking collectives: 19.7 us -> 0 us
  starting transfers between devices: 27.2 us -> 34.4 us
    all_gather x1 -> x0, waiting for transfers between devices: 55.6 us -> none  [shards(): routed_rows = lax.all_gather(incoming, 'tensor', axis=3, tiled=True)]
    reduce_scatter x1, waiting for transfers between devices: 13.7 us -> 43.2 us  [shards(): lax.psum_scatter(shared_term, 'tensor', scatter_dimension=1, tiled=True)]
    all_to_all x1 -> x0, blocking collectives: 19.7 us -> none  [shards(): lax.all_to_all(outgoing, 'seq', split_axis=0, concat_axis=0, tiled=True)]
    all_to_all x0 -> x1, waiting for transfers between devices: none -> 14.3 us  [shards(): lax.all_to_all(outgoing, 'seq', split_axis=0, concat_axis=0, tiled=True)]
    all_to_all x0 -> x1, starting transfers between devices: none -> 7.18 us  [shards(): lax.all_to_all(outgoing, 'seq', split_axis=0, concat_axis=0, tiled=True)]
    reduce_scatter x1, waiting for transfers between devices: 58.6 us -> 63.6 us  [shards(): lax.psum_scatter(expert_term.astype(jnp.bfloat16), 'tensor', scatter_dime...]
  transfers between devices with their start and end apart: 9 -> 9, of which waited for: 8 -> 8; matrix products, arithmetic and copies ran while one was open for 7% -> 6% of each run, Pallas kernels for 0% -> 0%
where the time goes in v6:
time: 392 us; the launch traced here: 390 us
  waiting for transfers between devices  249 us (64%)
  local copies, waits for them, and re-layouts  41.7 us (11%)
  starting transfers between devices  34.4 us (9%)
  matrix products  34 us (9%)
  other arithmetic  17.7 us (5%)
  between operations  13.6 us (3%)
    reduce_scatter x1, waiting for transfers between devices, shards(): lax.psum_scatter(expert_term.astype(jnp.bfloat16), 'tensor', scatter_dime...  63.6 us
    reduce_scatter x1, waiting for transfers between devices, shards(): lax.psum_scatter(shared_term, 'tensor', scatter_dimension=1, tiled=True)  43.2 us
    reduce_scatter x1, waiting for transfers between devices, shards(): lax.psum_scatter(projected.astype(jnp.bfloat16), 'tensor', scatter_dimens...  40 us
    all_to_all x1, waiting for transfers between devices, shards(): lax.all_to_all(spread, 'seq', 0, 0, tiled=True).reshape(tokens, width_local)  28 us
    all_to_all x1, waiting for transfers between devices, shards(): lax.all_to_all(local_out.reshape(seq_count, tok_dev, heads_local, HD).ast...  25.6 us
    all_gather x1, waiting for transfers between devices, shards(): lax.all_gather(jnp.concatenate([stream, norm_gain[None], router.astype(jn...  24.5 us
    all_to_all x1, waiting for transfers between devices, shards(): lax.all_to_all(outgoing, 'seq', split_axis=0, concat_axis=0, tiled=True)  14.3 us
    dot_general x1, matrix products, shards(): jnp.einsum('rhqk,rkhd->rqhd', cached_weights.astype(jnp.bfloat16), cache_...  9.95 us
  transfers between devices with their start and end apart: 9, of which 8 were waited for; matrix products, arithmetic and copies ran while one was open for 6% of the time, Pallas kernels for 0%

profile of v6, /device:TPU:65, one launch (start us, length us, event | category | flops | bytes accessed | tf_op | source)
XLA Modules:
  0.0 390.3 jit_solution(6215445025625532631)
XLA Ops:
  6.5 1.1 copy.130
  7.7 1.8 broadcast_in_dim.157
  9.4 8.5 %all-to-all-start = ((bf16[32,128,256]{1,2,0:T(8,128)(2,1)}), bf16[32,128,256]{1,2,0:T(8,128)(2,1)}, u32[]{:S(2)}, u32[]{:S(2)}) async-start(bf16[32,128,256]{1,2,0:T(8,128)(2,1)} %broadcast_in_dim.157), calls=%async_computation | async-start | bytes 4194304 | tf_op jit(solution)/shard_map/all_to_all | solution.py:60
  18.2 28.0 %all-to-all-done = bf16[32,128,256]{1,2,0:T(8,128)(2,1)} async-done(((bf16[32,128,256]{1,2,0:T(8,128)(2,1)}), bf16[32,128,256]{1,2,0:T(8,128)(2,1)}, u32[]{:S(2)}, u32[]{:S(2)}) %all-to-all-start) | async-done | bytes 2097184 | tf_op jit(solution)/shard_map/all_to_all | solution.py:60
  46.2 4.2 %copy.131 = bf16[32,128,256]{1,0,2:T(8,128)(2,1)} copy(bf16[32,128,256]{1,2,0:T(8,128)(2,1)} %all-to-all-done) | data formatting | bytes 4194304 | tf_op jit(solution)/shard_map/all_to_all | solution.py:60
  50.5 4.3 %reshape_reshape.3 = bf16[8,512,2,128]{1,0,3,2:T(8,128)(2,1)} reshape(bf16[32,128,256]{1,0,2:T(8,128)(2,1)} %copy.131) | data formatting | bytes 4194304 | tf_op jit(solution)/shard_map/reshape;reshape | solution.py:61
  54.8 2.1 constant_dynamic-slice_fusion
  56.9 1.0 copy.137
  57.9 1.2 select_reduce_fusion.1
  59.3 6.9 %select_reduce_fusion = (f32[8,2,512]{2,1,0:T(2,128)S(1)}, f32[8,2,512,512]{2,3,1,0:T(8,128)S(1)}) fusion(pred[8,512]{1,0:T(8,128)(4,1)S(1)} %broadcast_compare_fusion, bf16[8,512,2,128]{1,0,3,2:T(8,128)(2,1)} %reshape_reshape.3, bf16[8,512,256]{2,1,0:T(8,128)(2,1)} %param.19), kind=kOutput, calls=%fused_computation.4 | convolution fusion | flops 1086316544 | bytes 21008384 | tf_op jit(solution)/shard_map/rqhd,rkhd->rhqk/dot_general | solution.py:65
  66.2 3.6 fusion
  69.8 2.1 copy-done.1
  74.7 3.9 %all-to-all-start.2 = ((f32[32,128,2,2]{1,2,3,0:T(2,128)}), f32[32,128,2,2]{1,2,3,0:T(2,128)S(1)}, u32[]{:S(2)}, u32[]{:S(2)}) async-start(f32[32,128,2,2]{1,2,3,0:T(2,128)} %copy.146), calls=%async_computation.2 | async-start | bytes 131072 | tf_op jit(solution)/shard_map/all_to_all | solution.py:120
  78.6 0.8 copy.139
  79.4 0.8 copy.142
  80.2 1.2 convolution_bitcast_fusion
  81.4 10.0 %fusion.11 = bf16[8,512,2,128]{3,1,2,0:T(8,128)(2,1)S(1)} fusion(f32[8,2,512,512]{2,3,1,0:T(8,128)} %copy-done.1, f32[8,2,512]{2,1,0:T(2,128)} %copy-done.6, pred[8,512]{1,0:T(8,128)(4,1)S(1)} %broadcast_compare_fusion, f32[8,512,2]{1,2,0:T(2,128)S(1)} %copy.142, f32[512,2,128]{2,0,1:T(8,128)S(1)} %convolution_bitcast_fusion, f32[8,512,2]{1,2,0:T(2,128)S(1)} %copy.139, ...), kind=kOutput, calls=%fused_computation.16 | convolution fusion | flops 1095761920 | bytes 21598216 | tf_op jit(solution)/shard_map/rhqk,rkhd->rqhd/dot_general | solution.py:82
  91.5 1.4 copy.144
  92.9 8.0 %all-to-all-start.1 = ((bf16[32,128,2,128]{3,1,2,0:T(8,128)(2,1)}), bf16[32,128,2,128]{3,1,2,0:T(8,128)(2,1)}, u32[]{:S(2)}, u32[]{:S(2)}) async-start(bf16[32,128,2,128]{3,1,2,0:T(8,128)(2,1)} %copy.144), calls=%async_computation.1 | async-start | bytes 4194304 | tf_op jit(solution)/shard_map/all_to_all | solution.py:123
  101.1 25.6 %all-to-all-done.1 = bf16[32,128,2,128]{3,1,2,0:T(8,128)(2,1)} async-done(((bf16[32,128,2,128]{3,1,2,0:T(8,128)(2,1)}), bf16[32,128,2,128]{3,1,2,0:T(8,128)(2,1)}, u32[]{:S(2)}, u32[]{:S(2)}) %all-to-all-start.1) | async-done | bytes 2097184 | tf_op jit(solution)/shard_map/all_to_all | solution.py:123
  126.7 2.5 multiply_reduce_fusion
  129.4 2.4 convolution_convert_fusion.1
  131.9 40.0 %reduce-scatter.4.cloned.1.call-done = bf16[128,256]{1,0:T(8,128)(2,1)} async-done(((bf16[128,2048]{1,0:T(8,128)(2,1)}), bf16[128,256]{1,0:T(8,128)(2,1)}) %reduce-scatter.4.cloned.1.call-update) | async-done | bytes 65552 | tf_op jit(solution)/shard_map/reduce_scatter | solution.py:139
  171.9 0.9 convert_add_fusion
  173.9 1.8 reduce-window.6
  176.4 3.4 scatter_custom_fusion
  179.8 24.5 %all-gather.2.cloned.1.call-done = f32[193,2048]{1,0:T(8,128)} async-done(((f32[193,256]{1,0:T(8,128)}), f32[193,2048]{1,0:T(8,128)}) %all-gather.2.cloned.1.call-update) | async-done | bytes 1581072 | tf_op jit(solution)/shard_map/all_gather | solution.py:143
  204.3 1.4 multiply_reduce_fusion.2
  205.8 0.9 slice.52
  206.6 1.4 multiply_convert_fusion
  208.8 1.9 fusion.73
  210.7 1.2 convolution_convert_fusion
  211.9 1.1 concatenate.7
  213.0 6.0 %gather_fusion = bf16[1024,2048]{1,0:T(8,128)(2,1)} fusion(bf16[129,2048]{1,0:T(8,128)(2,1)S(1)} %concatenate.7, s32[1024]{0:T(1024)S(1)} %fusion.61), kind=kCustom, calls=%fused_computation | custom fusion | bytes 8392704 | tf_op jit(solution)/shard_map/gather | solution.py:182
  219.0 7.2 %all-to-all-start.3 = ((bf16[32,2,16,2048]{3,2,1,0:T(8,128)(2,1)}), bf16[32,2,16,2048]{3,2,1,0:T(8,128)(2,1)}, u32[]{:S(2)}, u32[]{:S(2)}) async-start(bf16[32,2,16,2048]{3,2,1,0:T(8,128)(2,1)} %bitcast.173), calls=%async_computation.4 | async-start | bytes 8388608 | tf_op jit(solution)/shard_map/all_to_all | solution.py:183
  227.0 43.2 %reduce-scatter.6.cloned.1.call-done = bf16[128,256]{1,0:T(8,128)(2,1)} async-done(((bf16[128,2048]{1,0:T(8,128)(2,1)}), bf16[128,256]{1,0:T(8,128)(2,1)}) %reduce-scatter.6.cloned.1.call-update) | async-done | bytes 65552 | tf_op jit(solution)/shard_map/reduce_scatter | solution.py:167
  270.2 14.3 %all-to-all-done.3 = bf16[32,2,16,2048]{3,2,1,0:T(8,128)(2,1)} async-done(((bf16[32,2,16,2048]{3,2,1,0:T(8,128)(2,1)}), bf16[32,2,16,2048]{3,2,1,0:T(8,128)(2,1)}, u32[]{:S(2)}, u32[]{:S(2)}) %all-to-all-start.3) | async-done | bytes 4194336 | tf_op jit(solution)/shard_map/all_to_all | solution.py:183
  284.5 4.6 %fusion.21 = f32[32,2,16,2,176]{4,2,3,0,1:T(8,128)S(1)} fusion(bf16[2,2048,2,176]{1,3,2,0:T(8,128)(2,1)S(1)} %copy-done, bf16[32,2,16,2048]{3,2,1,0:T(8,128)(2,1)} %all-to-all-done.3), kind=kOutput, calls=%fused_computation.28 | convolution fusion | flops 1476395008 | bytes 8519680 | tf_op jit(solution)/shard_map/secd,edjf->secjf/dot_general | solution.py:185
  289.1 3.2 convert_bitcast_fusion
  292.4 63.6 %reduce-scatter.8.cloned.1.call-done = bf16[32,2,16,256]{3,2,0,1:T(8,128)(2,1)} async-done(((bf16[32,2,16,2048]{3,2,0,1:T(8,128)(2,1)}), bf16[32,2,16,256]{3,2,0,1:T(8,128)(2,1)}) %reduce-scatter.8.cloned.1.call-update) | async-done | bytes 524304 | tf_op jit(solution)/shard_map/reduce_scatter | solution.py:192
  355.9 1.9 copy.158
  357.8 6.6 %all-to-all-start.4 = ((bf16[32,2,16,256]{3,2,1,0:T(8,128)(2,1)}), bf16[32,2,16,256]{3,2,1,0:T(8,128)(2,1)S(1)}, u32[]{:S(2)}, u32[]{:S(2)}) async-start(bf16[32,2,16,256]{3,2,1,0:T(8,128)(2,1)} %copy.158), calls=%async_computation.7 | async-start | bytes 1048576 | tf_op jit(solution)/shard_map/all_to_all | solution.py:195
  364.5 1.5 fusion.34
  366.2 9.0 %all-to-all-done.4 = bf16[32,2,16,256]{3,2,1,0:T(8,128)(2,1)S(1)} async-done(((bf16[32,2,16,256]{3,2,1,0:T(8,128)(2,1)}), bf16[32,2,16,256]{3,2,1,0:T(8,128)(2,1)S(1)}, u32[]{:S(2)}, u32[]{:S(2)}) %all-to-all-start.4) | async-done | bytes 524320 | tf_op jit(solution)/shard_map/all_to_all | solution.py:195
  375.2 3.3 gather_fusion.1
  378.5 2.1 reshape.181
  380.6 1.6 multiply_reduce_fusion.1
  382.2 1.5 add_convert_fusion
  (72 shorter events, 7.3 us)
Async XLA Ops:
  6.5 277.9 %copy-start = (bf16[2,2048,2,176]{1,3,2,0:T(8,128)(2,1)S(1)}, bf16[2,2048,2,176]{1,3,2,0:T(8,128)(2,1)}, u32[]{:S(2)}) copy-start(bf16[2,2048,2,176]{1,3,2,0:T(8,128)(2,1)} %param.26) | copy-start | bytes 8650756
  6.5 11.5 %copy-start.11 = (s32[8]{0:T(128)S(1)}, s32[8]{0:T(128)}, u32[]{:S(2)}) copy-start(s32[8]{0:T(128)} %param.21) | copy-start | bytes 100
  9.4 36.8 %all-to-all-start = ((bf16[32,128,256]{1,2,0:T(8,128)(2,1)}), bf16[32,128,256]{1,2,0:T(8,128)(2,1)}, u32[]{:S(2)}, u32[]{:S(2)}) async-start(bf16[32,128,256]{1,2,0:T(8,128)(2,1)} %broadcast_in_dim.157), calls=%async_computation | async-start | bytes 4194304 | tf_op jit(solution)/shard_map/all_to_all | solution.py:60
  18.2 39.7 %copy-start.7 = (bf16[128,256]{1,0:T(8,128)(2,1)S(1)}, bf16[128,256]{1,0:T(8,128)(2,1)}, u32[]{:S(2)}) copy-start(bf16[128,256]{1,0:T(8,128)(2,1)} %param.17) | copy-start | bytes 196612
  66.2 5.7 %copy-start.1 = (f32[8,2,512,512]{2,3,1,0:T(8,128)}, f32[8,2,512,512]{2,3,1,0:T(8,128)S(1)}, u32[]{:S(2)}) copy-start(f32[8,2,512,512]{2,3,1,0:T(8,128)S(1)} %get-tuple-element.18) | copy-start | bytes 50331652
  66.2 5.7 %copy-start.6 = (f32[8,2,512]{2,1,0:T(2,128)}, f32[8,2,512]{2,1,0:T(2,128)S(1)}, u32[]{:S(2)}) copy-start(f32[8,2,512]{2,1,0:T(2,128)S(1)} %get-tuple-element.17) | copy-start | bytes 98308
  74.7 18.2 %all-to-all-start.2 = ((f32[32,128,2,2]{1,2,3,0:T(2,128)}), f32[32,128,2,2]{1,2,3,0:T(2,128)S(1)}, u32[]{:S(2)}, u32[]{:S(2)}) async-start(f32[32,128,2,2]{1,2,3,0:T(2,128)} %copy.146), calls=%async_computation.2 | async-start | bytes 131072 | tf_op jit(solution)/shard_map/all_to_all | solution.py:120
  92.9 39.0 %copy-start.9 = (bf16[256,64]{0,1:T(8,128)(2,1)S(1)}, bf16[256,64]{0,1:T(8,128)(2,1)}, u32[]{:S(2)}) copy-start(bf16[256,64]{0,1:T(8,128)(2,1)} %param.24) | copy-start | bytes 98308
  92.9 79.0 %copy-start.4 = (bf16[128,256]{1,0:T(8,128)(2,1)S(1)}, bf16[128,256]{1,0:T(8,128)(2,1)}, u32[]{:S(2)}) copy-start(bf16[128,256]{1,0:T(8,128)(2,1)} %param.15) | copy-start | bytes 196612
  92.9 79.8 %copy-start.10 = (f32[256]{0:T(256)S(1)}, f32[256]{0:T(256)}, u32[]{:S(2)}) copy-start(f32[256]{0:T(256)} %param.23) | copy-start | bytes 3076
  92.9 80.5 %copy-start.8 = (s32[128,6]{0,1:T(8,128)S(1)}, s32[128,6]{0,1:T(8,128)}, u32[]{:S(2)}) copy-start(s32[128,6]{0,1:T(8,128)} %param.25) | copy-start | bytes 9220
  92.9 33.8 %all-to-all-start.1 = ((bf16[32,128,2,128]{3,1,2,0:T(8,128)(2,1)}), bf16[32,128,2,128]{3,1,2,0:T(8,128)(2,1)}, u32[]{:S(2)}, u32[]{:S(2)}) async-start(bf16[32,128,2,128]{3,1,2,0:T(8,128)(2,1)} %copy.144), calls=%async_computation.1 | async-start | bytes 4194304 | tf_op jit(solution)/shard_map/all_to_all | solution.py:123
  100.9 70.9 %reduce-scatter.4.cloned.1.call-start = ((), (), s32[]{:S(2)}) async-start(), calls=%async_computation.8 | async-start | bytes 589824 | tf_op jit(solution)/shard_map/reduce_scatter | solution.py:139
  131.8 72.5 %all-gather.2.cloned.1.call-start = ((), (), s32[]{:S(2)}) async-start(), calls=%async_computation.9 | async-start | bytes 1843200 | tf_op jit(solution)/shard_map/all_gather | solution.py:143
  204.3 6.4 %copy-start.3 = (bf16[176,2048]{1,0:T(8,128)(2,1)S(1)}, bf16[176,2048]{1,0:T(8,128)(2,1)}, u32[]{:S(2)}) copy-start(bf16[176,2048]{1,0:T(8,128)(2,1)} %param.29) | copy-start | bytes 2162692
  208.0 0.8 copy-start.2
  219.0 65.5 %all-to-all-start.3 = ((bf16[32,2,16,2048]{3,2,1,0:T(8,128)(2,1)}), bf16[32,2,16,2048]{3,2,1,0:T(8,128)(2,1)}, u32[]{:S(2)}, u32[]{:S(2)}) async-start(bf16[32,2,16,2048]{3,2,1,0:T(8,128)(2,1)} %bitcast.173), calls=%async_computation.4 | async-start | bytes 8388608 | tf_op jit(solution)/shard_map/all_to_all | solution.py:183
  226.2 44.0 %reduce-scatter.6.cloned.1.call-start = ((), (), s32[]{:S(2)}) async-start(), calls=%async_computation.10 | async-start | bytes 589824 | tf_op jit(solution)/shard_map/reduce_scatter | solution.py:167
  226.9 129.0 %reduce-scatter.8.cloned.1.call-start = ((), (), s32[]{:S(2)}) async-start(), calls=%async_computation.11 | async-start | bytes 4718592 | tf_op jit(solution)/shard_map/reduce_scatter | solution.py:192
  284.5 4.6 %copy-start.12 = (bf16[2,176,2048]{2,1,0:T(8,128)(2,1)S(1)}, bf16[2,176,2048]{2,1,0:T(8,128)(2,1)}, u32[]{:S(2)}) copy-start(bf16[2,176,2048]{2,1,0:T(8,128)(2,1)} %param.27) | copy-start | bytes 4325380
  357.8 24.4 %copy-start.5 = (bf16[128,256]{1,0:T(8,128)(2,1)S(1)}, bf16[128,256]{1,0:T(8,128)(2,1)}, u32[]{:S(2)}) copy-start(bf16[128,256]{1,0:T(8,128)(2,1)} %param.15) | copy-start | bytes 196612
  357.8 17.4 %all-to-all-start.4 = ((bf16[32,2,16,256]{3,2,1,0:T(8,128)(2,1)}), bf16[32,2,16,256]{3,2,1,0:T(8,128)(2,1)S(1)}, u32[]{:S(2)}, u32[]{:S(2)}) async-start(bf16[32,2,16,256]{3,2,1,0:T(8,128)(2,1)} %copy.158), calls=%async_computation.7 | async-start | bytes 1048576 | tf_op jit(solution)/shard_map/all_to_all | solution.py:195
Sparse Core Ops, SparseCore 0:
  131.9 39.8 reduce-scatter.3
  173.7 30.5 all-gather.1
  229.5 40.6 reduce-scatter.5
  292.5 63.3 reduce-scatter.7

commit v7 on v6

--- a/solution.py
+++ b/solution.py
@@ -56,85 +56,87 @@
     exp_dev = expert_gate_up.shape[0]
     topk = expert_ids.shape[1]
     scaling = 1.0 / math.sqrt(HD)
-    spread = jnp.broadcast_to(queries[None], (seq_count,) + queries.shape)
-    every_query = lax.all_to_all(spread, "seq", 0, 0, tiled=True).reshape(tokens, width_local)
-    grouped = every_query.reshape(requests, NEW, heads_local, HD)
     first_place = seq_index * clen_dev
-
-    cached_scores = (
-        jnp.einsum(
-            "rqhd,rkhd->rhqk",
-            grouped,
-            cache_keys.reshape(requests, clen_dev, heads_local, HD),
-            preferred_element_type=jnp.float32,
-        )
-        * scaling
-    )
-    cached_visible = (
-        first_place + lax.iota(jnp.int32, clen_dev)[None, :] < cache_lengths[:, None]
-    )[:, None, None, :]
-    masked = jnp.where(cached_visible, cached_scores, negative)
-    max_cached = jnp.max(masked, -1)
-    cached_weights = jnp.where(
-        cached_visible, jnp.exp(cached_scores - max_cached[..., None]), 0.0
-    )
-    sum_cached = jnp.sum(cached_weights, -1)
-    out_cached = jnp.einsum(
-        "rhqk,rkhd->rqhd",
-        cached_weights.astype(jnp.bfloat16),
-        cache_values.reshape(requests, clen_dev, heads_local, HD),
-        preferred_element_type=jnp.float32,
-    )
-    max_cached = jnp.transpose(max_cached, (0, 2, 1))
-    sum_cached = jnp.transpose(sum_cached, (0, 2, 1))
     own_start = seq_index * tok_dev
     own_request = own_start // NEW
     offset = own_start % NEW
-    own_queries = lax.dynamic_index_in_dim(grouped, own_request, 0, keepdims=False)
-    new_scores = (
-        jnp.einsum(
-            "qhd,khd->hqk",
-            own_queries,
-            new_keys.reshape(tok_dev, heads_local, HD),
+
+    def attend(head):
+        own = queries.reshape(tok_dev, heads_local, HD)[:, head : head + 1]
+        spread = jnp.broadcast_to(own[None], (seq_count,) + own.shape)
+        grouped = lax.all_to_all(spread, "seq", 0, 0, tiled=True).reshape(requests, NEW, 1, HD)
+        keys = cache_keys.reshape(requests, clen_dev, heads_local, HD)[:, :, head : head + 1]
+        values = cache_values.reshape(requests, clen_dev, heads_local, HD)[:, :, head : head + 1]
+        cached_scores = (
+            jnp.einsum("rqhd,rkhd->rhqk", grouped, keys, preferred_element_type=jnp.float32)
+            * scaling
+        )
+        cached_visible = (
+            first_place + lax.iota(jnp.int32, clen_dev)[None, :] < cache_lengths[:, None]
+        )[:, None, None, :]
+        masked = jnp.where(cached_visible, cached_scores, negative)
+        max_cached = jnp.max(masked, -1)
+        cached_weights = jnp.where(
+            cached_visible, jnp.exp(cached_scores - max_cached[..., None]), 0.0
+        )
+        sum_cached = jnp.sum(cached_weights, -1)
+        out_cached = jnp.einsum(
+            "rhqk,rkhd->rqhd",
+            cached_weights.astype(jnp.bfloat16),
+            values,
             preferred_element_type=jnp.float32,
         )
-        * scaling
-    )
-    visible_new = (
-        lax.iota(jnp.int32, NEW)[:, None] >= offset + lax.iota(jnp.int32, tok_dev)[None, :]
-    )[None]
-    max_new, sum_new, out_new = block_partial(
-        new_scores, visible_new, new_values.reshape(tok_dev, heads_local, HD)
-    )
-    chosen_request = (lax.iota(jnp.int32, requests) == own_request)[:, None, None]
-    max_placed = jnp.where(chosen_request, jnp.transpose(max_new)[None], negative)
-    sum_placed = jnp.where(chosen_request, jnp.transpose(sum_new)[None], 0.0)
-    out_placed = jnp.where(chosen_request[..., None], out_new[None], 0.0)
-    local_max = jnp.maximum(max_cached, max_placed)
-    factor_cached = jnp.exp(max_cached - local_max)
-    factor_new = jnp.exp(max_placed - local_max)
-    local_sum = sum_cached * factor_cached + sum_placed * factor_new
-    local_out = out_cached * factor_cached[..., None] + out_placed * factor_new[..., None]
-    flat_max = local_max.reshape(seq_count, tok_dev, heads_local)
-    flat_sum = local_sum.reshape(seq_count, tok_dev, heads_local)
-    stats = lax.all_to_all(
-        jnp.stack([flat_max, flat_sum], -1), "seq", 0, 0, tiled=True
-    )
-    parts_out = lax.all_to_all(
-        local_out.reshape(seq_count, tok_dev, heads_local, HD).astype(jnp.bfloat16),
-        "seq",
-        0,
-        0,
-        tiled=True,
-    ).astype(jnp.float32)
-    part_max = stats[..., 0]
-    row_max = jnp.max(part_max, 0)
-    factors = jnp.exp(part_max - row_max[None])
-    row_sum = jnp.sum(stats[..., 1] * factors, 0)
-    weighted = jnp.sum(parts_out * factors[..., None], 0)
-    attended = (
-        (weighted / row_sum[..., None]).astype(jnp.bfloat16).reshape(tok_dev, heads_local * HD)
-    )
+        max_cached = jnp.transpose(max_cached, (0, 2, 1))
+        sum_cached = jnp.transpose(sum_cached, (0, 2, 1))
+        own_queries = lax.dynamic_index_in_dim(grouped, own_request, 0, keepdims=False)
+        new_scores = (
+            jnp.einsum(
+                "qhd,khd->hqk",
+                own_queries,
+                new_keys.reshape(tok_dev, heads_local, HD)[:, head : head + 1],
+                preferred_element_type=jnp.float32,
+            )
+            * scaling
+        )
+        visible_new = (
+            lax.iota(jnp.int32, NEW)[:, None] >= offset + lax.iota(jnp.int32, tok_dev)[None, :]
+        )[None]
+        max_new, sum_new, out_new = block_partial(
+            new_scores,
+            visible_new,
+            new_values.reshape(tok_dev, heads_local, HD)[:, head : head + 1],
+        )
+        chosen_request = (lax.iota(jnp.int32, requests) == own_request)[:, None, None]
+        max_placed = jnp.where(chosen_request, jnp.transpose(max_new)[None], negative)
+        sum_placed = jnp.where(chosen_request, jnp.transpose(sum_new)[None], 0.0)
+        out_placed = jnp.where(chosen_request[..., None], out_new[None], 0.0)
+        local_max = jnp.maximum(max_cached, max_placed)
+        factor_cached = jnp.exp(max_cached - local_max)
+        factor_new = jnp.exp(max_placed - local_max)
+        local_sum = sum_cached * factor_cached + sum_placed * factor_new
+        local_out = out_cached * factor_cached[..., None] + out_placed * factor_new[..., None]
+        stats = lax.all_to_all(
+            jnp.stack([local_max, local_sum], -1).reshape(seq_count, tok_dev, 2),
+            "seq",
+            0,
+            0,
+            tiled=True,
+        )
+        parts_out = lax.all_to_all(
+            local_out.reshape(seq_count, tok_dev, HD).astype(jnp.bfloat16),
+            "seq",
+            0,
+            0,
+            tiled=True,
+        ).astype(jnp.float32)
+        part_max = stats[..., 0]
+        row_max = jnp.max(part_max, 0)
+        factors = jnp.exp(part_max - row_max[None])
+        row_sum = jnp.sum(stats[..., 1] * factors, 0)
+        weighted = jnp.sum(parts_out * factors[..., None], 0)
+        return (weighted / row_sum[..., None]).astype(jnp.bfloat16)
+
+    attended = jnp.concatenate([attend(head) for head in range(heads_local)], 1)
     projected = jnp.dot(attended, out_proj, preferred_element_type=jnp.float32)
     attn_out = lax.psum_scatter(
         projected.astype(jnp.bfloat16), "tensor", scatter_dimension=1, tiled=True

time: 392 us -> 412 us (1.051)
  starting transfers between devices: 34.4 us -> 51.7 us
  matrix products: 34 us -> 48.2 us
  waiting for transfers between devices: 249 us -> 235 us
  other arithmetic: 17.7 us -> 22.3 us
    all_to_all x3 -> x6, starting transfers between devices: 20.4 us -> 38 us  [the longest x2 14.4 us: attend(): lax.all_to_all(local_out.reshape(seq_count, tok_dev, HD).astype(jnp.bfloa...]
    dot_general x3 -> x6, matrix products: 18.1 us -> 31.4 us  [the longest x2 14.4 us: attend(): jnp.einsum('rqhd,rkhd->rhqk', grouped, keys, preferred_element_type=jnp.f...]
    all_to_all x3 -> x6, waiting for transfers between devices: 53.6 us -> 41.3 us  [the longest x2 19.6 us: attend(): lax.all_to_all(local_out.reshape(seq_count, tok_dev, HD).astype(jnp.bfloa...]
    unnamed x28 -> x56, local copies, waits for them, and re-layouts: 4.16 us -> 10.2 us
    broadcast_in_dim x1 -> x12, local copies, waits for them, and re-layouts: 1.77 us -> 7.75 us  [the longest x6 3.35 us: attend(): jnp.where(chosen_request, jnp.transpose(max_new)[None], negative)]
    another operation x4 -> x0, local copies, waits for them, and re-layouts: 5.65 us -> none  [the longest x1 4.35 us: shards(): grouped = every_query.reshape(requests, NEW, heads_local, HD)]
    all_to_all x1 -> x0, local copies, waits for them, and re-layouts: 4.24 us -> none  [shards(): lax.all_to_all(spread, 'seq', 0, 0, tiled=True).reshape(tokens, width_local)]
  transfers between devices with their start and end apart: 9 -> 12, of which waited for: 8 -> 11; matrix products, arithmetic and copies ran while one was open for 6% -> 10% of each run, Pallas kernels for 0% -> 0%
where the time goes in v7:
time: 412 us; the launch traced here: 410 us
  waiting for transfers between devices  235 us (57%)
  starting transfers between devices  51.7 us (13%)
  matrix products  48.2 us (12%)
  local copies, waits for them, and re-layouts  39.1 us (9%)
  other arithmetic  22.3 us (5%)
  between operations  13.8 us (3%)
    reduce_scatter x1, waiting for transfers between devices, shards(): lax.psum_scatter(expert_term.astype(jnp.bfloat16), 'tensor', scatter_dime...  62.8 us
    reduce_scatter x1, waiting for transfers between devices, shards(): lax.psum_scatter(shared_term, 'tensor', scatter_dimension=1, tiled=True)  42.2 us
    reduce_scatter x1, waiting for transfers between devices, shards(): lax.psum_scatter(projected.astype(jnp.bfloat16), 'tensor', scatter_dimens...  39.2 us
    all_gather x1, waiting for transfers between devices, shards(): lax.all_gather(jnp.concatenate([stream, norm_gain[None], router.astype(jn...  24.3 us
    all_to_all x2, waiting for transfers between devices, attend(): lax.all_to_all(local_out.reshape(seq_count, tok_dev, HD).astype(jnp.bfloa...  19.6 us
    all_to_all x2, waiting for transfers between devices, attend(): lax.all_to_all(spread, 'seq', 0, 0, tiled=True)  17.8 us
    all_to_all x1, waiting for transfers between devices, shards(): lax.all_to_all(outgoing, 'seq', split_axis=0, concat_axis=0, tiled=True)  15.3 us
    all_to_all x2, starting transfers between devices, attend(): lax.all_to_all(local_out.reshape(seq_count, tok_dev, HD).astype(jnp.bfloa...  14.4 us
  transfers between devices with their start and end apart: 12, of which 11 were waited for; matrix products, arithmetic and copies ran while one was open for 10% of the time, Pallas kernels for 0%

profile of v7, /device:TPU:65, one launch (start us, length us, event | category | flops | bytes accessed | tf_op | source)
XLA Modules:
  0.0 410.0 jit_solution(5561417135107138096)
XLA Ops:
  7.8 1.2 broadcast_in_dim.227
  9.0 8.5 %all-to-all-start = ((bf16[32,128,1,128]{3,1,2,0:T(8,128)(2,1)}), bf16[32,128,1,128]{3,1,2,0:T(8,128)(2,1)}, u32[]{:S(2)}, u32[]{:S(2)}) async-start(bf16[32,128,1,128]{3,1,2,0:T(8,128)(2,1)} %broadcast_in_dim.227), calls=%async_computation | async-start | bytes 2097152 | tf_op jit(solution)/shard_map/all_to_all | solution.py:67
  17.7 16.6 %all-to-all-done = bf16[32,128,1,128]{3,1,2,0:T(8,128)(2,1)} async-done(((bf16[32,128,1,128]{3,1,2,0:T(8,128)(2,1)}), bf16[32,128,1,128]{3,1,2,0:T(8,128)(2,1)}, u32[]{:S(2)}, u32[]{:S(2)}) %all-to-all-start) | async-done | bytes 1048608 | tf_op jit(solution)/shard_map/all_to_all | solution.py:67
  34.3 1.2 broadcast_in_dim.249
  35.5 4.7 %all-to-all-start.3 = ((bf16[32,128,1,128]{3,1,2,0:T(8,128)(2,1)}), bf16[32,128,1,128]{3,1,2,0:T(8,128)(2,1)}, u32[]{:S(2)}, u32[]{:S(2)}) async-start(bf16[32,128,1,128]{3,1,2,0:T(8,128)(2,1)} %broadcast_in_dim.249), calls=%async_computation.3 | async-start | bytes 2097152 | tf_op jit(solution)/shard_map/all_to_all | solution.py:67
  41.1 3.9 copy.95
  45.2 4.0 copy.97
  49.3 5.5 %select_reduce_fusion.1 = (f32[8,512]{1,0:T(8,128)S(1)}, f32[8,512,512]{1,2,0:T(8,128)}) fusion(pred[8,512]{1,0:T(8,128)(4,1)S(1)} %broadcast_compare_fusion, bf16[8,512,128]{2,1,0:T(8,128)(2,1)} %bitcast.2, bf16[8,512,2,128]{1,3,2,0:T(8,128)(2,1)} %bitcast.198), kind=kOutput, calls=%fused_computation.6 | convolution fusion | flops 543158272 | bytes 10506240 | tf_op jit(solution)/shard_map/rqhd,rkhd->rhqk/dot_general | solution.py:71
  55.9 8.9 %fusion = (f32[8,512]{1,0:T(8,128)}, f32[8,512]{1,0:T(8,128)S(1)}, f32[8,512,512]{1,2,0:T(8,128)}) fusion(f32[8,512,512]{1,2,0:T(8,128)} %get-tuple-element.36, f32[8,512]{1,0:T(8,128)S(1)} %get-tuple-element.35, pred[8,512]{1,0:T(8,128)(4,1)S(1)} %broadcast_compare_fusion, bf16[8,512,128]{2,1,0:T(8,128)(2,1)} %bitcast.21, bf16[8,512,2,128]{1,3,2,0:T(8,128)(2,1)} %bitcast.199), kind=kOutput, calls=%fused_computation.7 | convolution fusion | flops 551542784 | bytes 18927616 | tf_op jit(solution)/shard_map/rqhd,rkhd->rhqk/dot_general | solution.py:71
  66.0 1.7 fusion.46
  73.2 4.4 %fusion.2 = f32[8,512]{1,0:T(8,128)S(1)} fusion(f32[8,512,512]{1,2,0:T(8,128)} %get-tuple-element.40, f32[8,512]{1,0:T(8,128)S(1)} %get-tuple-element.14, pred[8,512]{1,0:T(8,128)(4,1)} %copy-done.9), kind=kLoop, calls=%fused_computation.9 | loop fusion | flops 8384512 | bytes 8425472 | tf_op jit(solution)/shard_map/reduce_sum | solution.py:82
  78.9 1.6 fusion.95
  81.1 6.5 %all-to-all-start.2 = ((f32[32,128,2]{1,2,0:T(2,128)}), f32[32,128,2]{1,2,0:T(2,128)S(1)}, u32[]{:S(2)}, u32[]{:S(2)}) async-start(f32[32,128,2]{1,2,0:T(2,128)} %pad_maximum_fusion.1), calls=%async_computation.2 | async-start | bytes 65536 | tf_op jit(solution)/shard_map/all_to_all | solution.py:118
  87.7 1.7 fusion.52
  89.4 1.4 pad_maximum_fusion.2
  90.8 4.0 all-to-all-done.2
  94.8 3.9 all-to-all-start.5
  98.7 7.5 %fusion.24 = bf16[8,512,1,128]{3,1,0,2:T(8,128)(2,1)} fusion(f32[8,512,512]{1,2,0:T(8,128)} %get-tuple-element.36, f32[8,512]{1,0:T(8,128)S(1)} %get-tuple-element.35, pred[8,512]{1,0:T(8,128)(4,1)} %copy-done.9, bf16[8,512,2,128]{1,3,2,0:T(8,128)(2,1)} %bitcast.200, f32[8,512]{1,0:T(8,128)} %get-tuple-element.28, f32[512,128]{1,0:T(8,128)} %fusion.52, ...), kind=kOutput, calls=%fused_computation.34 | convolution fusion | flops 547880960 | bytes 10801664 | tf_op jit(solution)/shard_map/rhqk,rkhd->rqhd/dot_general | solution.py:83
  106.3 8.0 %all-to-all-start.1 = ((bf16[32,128,128]{2,1,0:T(8,128)(2,1)}), bf16[32,128,128]{2,1,0:T(8,128)(2,1)}, u32[]{:S(2)}, u32[]{:S(2)}) async-start(bf16[32,128,128]{2,1,0:T(8,128)(2,1)} %bitcast.204), calls=%async_computation.1 | async-start | bytes 2097152 | tf_op jit(solution)/shard_map/all_to_all | solution.py:125
  114.7 6.6 %fusion.21 = bf16[8,512,1,128]{3,1,0,2:T(8,128)(2,1)} fusion(f32[8,512,512]{1,2,0:T(8,128)} %get-tuple-element.40, f32[8,512]{1,0:T(8,128)S(1)} %get-tuple-element.14, pred[8,512]{1,0:T(8,128)(4,1)S(1)} %copy-done.10, bf16[8,512,2,128]{1,3,2,0:T(8,128)(2,1)} %bitcast.201, f32[8,512]{1,0:T(8,128)S(1)} %copy-done.16, f32[512,128]{1,0:T(8,128)S(1)} %fusion.50, ...), kind=kOutput, calls=%fused_computation.30 | convolution fusion | flops 547880960 | bytes 10801160 | tf_op jit(solution)/shard_map/rhqk,rkhd->rqhd/dot_general | solution.py:83
  121.3 6.8 %all-to-all-done.1 = bf16[32,128,128]{2,1,0:T(8,128)(2,1)} async-done(((bf16[32,128,128]{2,1,0:T(8,128)(2,1)}), bf16[32,128,128]{2,1,0:T(8,128)(2,1)}, u32[]{:S(2)}, u32[]{:S(2)}) %all-to-all-start.1) | async-done | bytes 1048608 | tf_op jit(solution)/shard_map/all_to_all | solution.py:125
  128.1 6.4 %all-to-all-start.4 = ((bf16[32,128,128]{2,1,0:T(8,128)(2,1)}), bf16[32,128,128]{2,1,0:T(8,128)(2,1)}, u32[]{:S(2)}, u32[]{:S(2)}) async-start(bf16[32,128,128]{2,1,0:T(8,128)(2,1)} %bitcast.203), calls=%async_computation.4 | async-start | bytes 2097152 | tf_op jit(solution)/shard_map/all_to_all | solution.py:125
  134.7 1.7 multiply_reduce_fusion.1
  136.6 12.8 %all-to-all-done.4 = bf16[32,128,128]{2,1,0:T(8,128)(2,1)} async-done(((bf16[32,128,128]{2,1,0:T(8,128)(2,1)}), bf16[32,128,128]{2,1,0:T(8,128)(2,1)}, u32[]{:S(2)}, u32[]{:S(2)}) %all-to-all-start.4) | async-done | bytes 1048608 | tf_op jit(solution)/shard_map/all_to_all | solution.py:125
  149.3 1.7 multiply_reduce_fusion
  151.2 2.3 convolution_convert_fusion.1
  153.6 39.2 %reduce-scatter.4.cloned.1.call-done = bf16[128,256]{1,0:T(8,128)(2,1)} async-done(((bf16[128,2048]{1,0:T(8,128)(2,1)}), bf16[128,256]{1,0:T(8,128)(2,1)}) %reduce-scatter.4.cloned.1.call-update) | async-done | bytes 65552 | tf_op jit(solution)/shard_map/reduce_scatter | solution.py:141
  194.8 1.8 reduce-window.6
  197.3 3.4 scatter_custom_fusion
  200.7 24.3 %all-gather.2.cloned.1.call-done = f32[193,2048]{1,0:T(8,128)} async-done(((f32[193,256]{1,0:T(8,128)}), f32[193,2048]{1,0:T(8,128)}) %all-gather.2.cloned.1.call-update) | async-done | bytes 1581072 | tf_op jit(solution)/shard_map/all_gather | solution.py:145
  225.0 1.4 multiply_reduce_fusion.3
  227.3 1.4 multiply_convert_fusion
  229.5 1.9 fusion.100
  233.7 6.0 %gather_fusion = bf16[1024,2048]{1,0:T(8,128)(2,1)} fusion(bf16[129,2048]{1,0:T(8,128)(2,1)S(1)} %concatenate.13, s32[1024]{0:T(1024)S(1)} %fusion.79), kind=kCustom, calls=%fused_computation | custom fusion | bytes 8392704 | tf_op jit(solution)/shard_map/gather | solution.py:184
  239.7 7.1 %all-to-all-start.6 = ((bf16[32,2,16,2048]{3,2,1,0:T(8,128)(2,1)}), bf16[32,2,16,2048]{3,2,1,0:T(8,128)(2,1)}, u32[]{:S(2)}, u32[]{:S(2)}) async-start(bf16[32,2,16,2048]{3,2,1,0:T(8,128)(2,1)} %bitcast.197), calls=%async_computation.7 | async-start | bytes 8388608 | tf_op jit(solution)/shard_map/all_to_all | solution.py:185
  247.6 42.2 %reduce-scatter.6.cloned.1.call-done = bf16[128,256]{1,0:T(8,128)(2,1)} async-done(((bf16[128,2048]{1,0:T(8,128)(2,1)}), bf16[128,256]{1,0:T(8,128)(2,1)}) %reduce-scatter.6.cloned.1.call-update) | async-done | bytes 65552 | tf_op jit(solution)/shard_map/reduce_scatter | solution.py:169
  289.8 15.3 %all-to-all-done.6 = bf16[32,2,16,2048]{3,2,1,0:T(8,128)(2,1)} async-done(((bf16[32,2,16,2048]{3,2,1,0:T(8,128)(2,1)}), bf16[32,2,16,2048]{3,2,1,0:T(8,128)(2,1)}, u32[]{:S(2)}, u32[]{:S(2)}) %all-to-all-start.6) | async-done | bytes 4194336 | tf_op jit(solution)/shard_map/all_to_all | solution.py:185
  305.1 4.6 %fusion.25 = f32[32,2,16,2,176]{4,2,3,0,1:T(8,128)S(1)} fusion(bf16[2,2048,2,176]{1,3,2,0:T(8,128)(2,1)S(1)} %copy-done, bf16[32,2,16,2048]{3,2,1,0:T(8,128)(2,1)} %all-to-all-done.6), kind=kOutput, calls=%fused_computation.37 | convolution fusion | flops 1476395008 | bytes 8519680 | tf_op jit(solution)/shard_map/secd,edjf->secjf/dot_general | solution.py:187
  309.8 3.2 convert_bitcast_fusion
  313.0 62.8 %reduce-scatter.8.cloned.1.call-done = bf16[32,2,16,256]{3,2,0,1:T(8,128)(2,1)} async-done(((bf16[32,2,16,2048]{3,2,0,1:T(8,128)(2,1)}), bf16[32,2,16,256]{3,2,0,1:T(8,128)(2,1)}) %reduce-scatter.8.cloned.1.call-update) | async-done | bytes 524304 | tf_op jit(solution)/shard_map/reduce_scatter | solution.py:194
  375.9 1.9 copy.119
  377.7 6.5 %all-to-all-start.7 = ((bf16[32,2,16,256]{3,2,1,0:T(8,128)(2,1)}), bf16[32,2,16,256]{3,2,1,0:T(8,128)(2,1)S(1)}, u32[]{:S(2)}, u32[]{:S(2)}) async-start(bf16[32,2,16,256]{3,2,1,0:T(8,128)(2,1)} %copy.119), calls=%async_computation.10 | async-start | bytes 1048576 | tf_op jit(solution)/shard_map/all_to_all | solution.py:197
  384.2 1.5 fusion.41
  386.0 9.0 %all-to-all-done.7 = bf16[32,2,16,256]{3,2,1,0:T(8,128)(2,1)S(1)} async-done(((bf16[32,2,16,256]{3,2,1,0:T(8,128)(2,1)}), bf16[32,2,16,256]{3,2,1,0:T(8,128)(2,1)S(1)}, u32[]{:S(2)}, u32[]{:S(2)}) %all-to-all-start.7) | async-done | bytes 524320 | tf_op jit(solution)/shard_map/all_to_all | solution.py:197
  395.0 3.3 gather_fusion.1
  398.2 2.1 reshape.909
  400.3 1.6 multiply_reduce_fusion.2
  402.0 1.5 add_convert_fusion
  (124 shorter events, 20.5 us)
Async XLA Ops:
  6.5 298.6 %copy-start = (bf16[2,2048,2,176]{1,3,2,0:T(8,128)(2,1)S(1)}, bf16[2,2048,2,176]{1,3,2,0:T(8,128)(2,1)}, u32[]{:S(2)}) copy-start(bf16[2,2048,2,176]{1,3,2,0:T(8,128)(2,1)} %param.26) | copy-start | bytes 8650756
  6.5 33.7 %copy-start.7 = (bf16[128,256]{1,0:T(8,128)(2,1)S(1)}, bf16[128,256]{1,0:T(8,128)(2,1)}, u32[]{:S(2)}) copy-start(bf16[128,256]{1,0:T(8,128)(2,1)} %param.17) | copy-start | bytes 196612
  9.0 25.3 %all-to-all-start = ((bf16[32,128,1,128]{3,1,2,0:T(8,128)(2,1)}), bf16[32,128,1,128]{3,1,2,0:T(8,128)(2,1)}, u32[]{:S(2)}, u32[]{:S(2)}) async-start(bf16[32,128,1,128]{3,1,2,0:T(8,128)(2,1)} %broadcast_in_dim.227), calls=%async_computation | async-start | bytes 2097152 | tf_op jit(solution)/shard_map/all_to_all | solution.py:67
  17.6 27.5 %copy-start.8 = (bf16[128,256]{1,0:T(8,128)(2,1)S(1)}, bf16[128,256]{1,0:T(8,128)(2,1)}, u32[]{:S(2)}) copy-start(bf16[128,256]{1,0:T(8,128)(2,1)} %param.18) | copy-start | bytes 196612
  35.5 20.4 %all-to-all-start.3 = ((bf16[32,128,1,128]{3,1,2,0:T(8,128)(2,1)}), bf16[32,128,1,128]{3,1,2,0:T(8,128)(2,1)}, u32[]{:S(2)}, u32[]{:S(2)}) async-start(bf16[32,128,1,128]{3,1,2,0:T(8,128)(2,1)} %broadcast_in_dim.249), calls=%async_computation.3 | async-start | bytes 2097152 | tf_op jit(solution)/shard_map/all_to_all | solution.py:67
  40.3 24.5 %copy-start.4 = (bf16[128,256]{0,1:T(8,128)(2,1)}, bf16[128,256]{0,1:T(8,128)(2,1)S(1)}, u32[]{:S(2)}) copy-start(bf16[128,256]{0,1:T(8,128)(2,1)S(1)} %copy.100) | copy-start | bytes 196612
  40.4 27.4 %copy-start.21 = (pred[8]{0:T(512)(128)(4,1)}, pred[8]{0:T(512)(128)(4,1)S(1)}, u32[]{:S(2)}) copy-start(pred[8]{0:T(512)(128)(4,1)S(1)} %iota_compare_fusion.4) | copy-start | bytes 28
  41.1 8.0 %copy-start.23 = (s32[8]{0:T(128)S(1)}, s32[8]{0:T(128)}, u32[]{:S(2)}) copy-start(s32[8]{0:T(128)} %param.21) | copy-start | bytes 100
  49.2 19.3 %copy-start.18 = (s32[128]{0:T(128)}, s32[128]{0:T(128)S(1)}, u32[]{:S(2)}) copy-start(s32[128]{0:T(128)S(1)} %iota_add_fusion.1) | copy-start | bytes 1540
  49.3 6.7 %copy-start.9 = (pred[8,512]{1,0:T(8,128)(4,1)}, pred[8,512]{1,0:T(8,128)(4,1)S(1)}, u32[]{:S(2)}) copy-start(pred[8,512]{1,0:T(8,128)(4,1)S(1)} %broadcast_compare_fusion) | copy-start | bytes 12292
  66.0 2.5 copy-start.14
  67.7 0.7 copy-start.12
  81.1 13.7 %all-to-all-start.2 = ((f32[32,128,2]{1,2,0:T(2,128)}), f32[32,128,2]{1,2,0:T(2,128)S(1)}, u32[]{:S(2)}, u32[]{:S(2)}) async-start(f32[32,128,2]{1,2,0:T(2,128)} %pad_maximum_fusion.1), calls=%async_computation.2 | async-start | bytes 65536 | tf_op jit(solution)/shard_map/all_to_all | solution.py:118
  94.8 11.4 %copy-start.5 = (f32[32,128,2]{1,2,0:T(2,128)}, f32[32,128,2]{1,2,0:T(2,128)S(1)}, u32[]{:S(2)}) copy-start(f32[32,128,2]{1,2,0:T(2,128)S(1)} %all-to-all-done.2) | copy-start | bytes 98308
  94.8 11.4 %all-to-all-start.5 = ((f32[32,128,2]{1,2,0:T(2,128)}), f32[32,128,2]{1,2,0:T(2,128)S(1)}, u32[]{:S(2)}, u32[]{:S(2)}) async-start(f32[32,128,2]{1,2,0:T(2,128)} %pad_maximum_fusion.2), calls=%async_computation.5 | async-start | bytes 65536 | tf_op jit(solution)/shard_map/all_to_all | solution.py:118
  98.7 15.6 %copy-start.13 = (f32[512]{0:T(512)S(1)}, f32[512]{0:T(512)}, u32[]{:S(2)}) copy-start(f32[512]{0:T(512)} %copy-done.12) | copy-start | bytes 6148
  98.7 15.6 %copy-start.19 = (s32[128]{0:T(128)S(1)}, s32[128]{0:T(128)}, u32[]{:S(2)}) copy-start(s32[128]{0:T(128)} %copy-done.18) | copy-start | bytes 1540
  98.7 16.0 %copy-start.10 = (pred[8,512]{1,0:T(8,128)(4,1)S(1)}, pred[8,512]{1,0:T(8,128)(4,1)}, u32[]{:S(2)}) copy-start(pred[8,512]{1,0:T(8,128)(4,1)} %copy-done.9) | copy-start | bytes 12292
  98.7 16.0 %copy-start.16 = (f32[8,512]{1,0:T(8,128)S(1)}, f32[8,512]{1,0:T(8,128)}, u32[]{:S(2)}) copy-start(f32[8,512]{1,0:T(8,128)} %get-tuple-element.33) | copy-start | bytes 49156
  98.7 16.0 %copy-start.17 = (f32[8,512]{1,0:T(8,128)S(1)}, f32[8,512]{1,0:T(8,128)}, u32[]{:S(2)}) copy-start(f32[8,512]{1,0:T(8,128)} %get-tuple-element.34) | copy-start | bytes 49156
  98.7 16.0 %copy-start.22 = (pred[8]{0:T(512)(128)(4,1)S(1)}, pred[8]{0:T(512)(128)(4,1)}, u32[]{:S(2)}) copy-start(pred[8]{0:T(512)(128)(4,1)} %copy-done.21) | copy-start | bytes 28
  106.3 21.9 %all-to-all-start.1 = ((bf16[32,128,128]{2,1,0:T(8,128)(2,1)}), bf16[32,128,128]{2,1,0:T(8,128)(2,1)}, u32[]{:S(2)}, u32[]{:S(2)}) async-start(bf16[32,128,128]{2,1,0:T(8,128)(2,1)} %bitcast.204), calls=%async_computation.1 | async-start | bytes 2097152 | tf_op jit(solution)/shard_map/all_to_all | solution.py:125
  114.7 19.8 %copy-start.6 = (f32[32,128,2]{1,2,0:T(2,128)S(1)}, f32[32,128,2]{1,2,0:T(2,128)}, u32[]{:S(2)}) copy-start(f32[32,128,2]{1,2,0:T(2,128)} %copy-done.5) | copy-start | bytes 98308
  121.3 32.3 %copy-start.15 = (bf16[256,64]{0,1:T(8,128)(2,1)S(1)}, bf16[256,64]{0,1:T(8,128)(2,1)}, u32[]{:S(2)}) copy-start(bf16[256,64]{0,1:T(8,128)(2,1)} %param.24) | copy-start | bytes 98308
  121.3 71.5 %copy-start.3 = (bf16[128,256]{1,0:T(8,128)(2,1)S(1)}, bf16[128,256]{1,0:T(8,128)(2,1)}, u32[]{:S(2)}) copy-start(bf16[128,256]{1,0:T(8,128)(2,1)} %param.15) | copy-start | bytes 196612
  121.3 72.4 %copy-start.20 = (f32[256]{0:T(256)S(1)}, f32[256]{0:T(256)}, u32[]{:S(2)}) copy-start(f32[256]{0:T(256)} %param.23) | copy-start | bytes 3076
  121.3 73.1 %copy-start.11 = (s32[128,6]{0,1:T(8,128)S(1)}, s32[128,6]{0,1:T(8,128)}, u32[]{:S(2)}) copy-start(s32[128,6]{0,1:T(8,128)} %param.25) | copy-start | bytes 9220
  128.1 21.2 %all-to-all-start.4 = ((bf16[32,128,128]{2,1,0:T(8,128)(2,1)}), bf16[32,128,128]{2,1,0:T(8,128)(2,1)}, u32[]{:S(2)}, u32[]{:S(2)}) async-start(bf16[32,128,128]{2,1,0:T(8,128)(2,1)} %bitcast.203), calls=%async_computation.4 | async-start | bytes 2097152 | tf_op jit(solution)/shard_map/all_to_all | solution.py:125
  134.5 58.3 %reduce-scatter.4.cloned.1.call-start = ((), (), s32[]{:S(2)}) async-start(), calls=%async_computation.11 | async-start | bytes 589824 | tf_op jit(solution)/shard_map/reduce_scatter | solution.py:141
  153.5 71.5 %all-gather.2.cloned.1.call-start = ((), (), s32[]{:S(2)}) async-start(), calls=%async_computation.12 | async-start | bytes 1843200 | tf_op jit(solution)/shard_map/all_gather | solution.py:145
  225.0 6.4 %copy-start.2 = (bf16[176,2048]{1,0:T(8,128)(2,1)S(1)}, bf16[176,2048]{1,0:T(8,128)(2,1)}, u32[]{:S(2)}) copy-start(bf16[176,2048]{1,0:T(8,128)(2,1)} %param.29) | copy-start | bytes 2162692
  228.7 0.8 copy-start.1
  239.7 65.4 %all-to-all-start.6 = ((bf16[32,2,16,2048]{3,2,1,0:T(8,128)(2,1)}), bf16[32,2,16,2048]{3,2,1,0:T(8,128)(2,1)}, u32[]{:S(2)}, u32[]{:S(2)}) async-start(bf16[32,2,16,2048]{3,2,1,0:T(8,128)(2,1)} %bitcast.197), calls=%async_computation.7 | async-start | bytes 8388608 | tf_op jit(solution)/shard_map/all_to_all | solution.py:185
  246.8 43.0 %reduce-scatter.6.cloned.1.call-start = ((), (), s32[]{:S(2)}) async-start(), calls=%async_computation.13 | async-start | bytes 589824 | tf_op jit(solution)/shard_map/reduce_scatter | solution.py:169
  247.5 128.3 %reduce-scatter.8.cloned.1.call-start = ((), (), s32[]{:S(2)}) async-start(), calls=%async_computation.14 | async-start | bytes 4718592 | tf_op jit(solution)/shard_map/reduce_scatter | solution.py:194
  305.1 4.6 %copy-start.24 = (bf16[2,176,2048]{2,1,0:T(8,128)(2,1)S(1)}, bf16[2,176,2048]{2,1,0:T(8,128)(2,1)}, u32[]{:S(2)}) copy-start(bf16[2,176,2048]{2,1,0:T(8,128)(2,1)} %param.27) | copy-start | bytes 4325380
  377.7 17.2 %all-to-all-start.7 = ((bf16[32,2,16,256]{3,2,1,0:T(8,128)(2,1)}), bf16[32,2,16,256]{3,2,1,0:T(8,128)(2,1)S(1)}, u32[]{:S(2)}, u32[]{:S(2)}) async-start(bf16[32,2,16,256]{3,2,1,0:T(8,128)(2,1)} %copy.119), calls=%async_computation.10 | async-start | bytes 1048576 | tf_op jit(solution)/shard_map/all_to_all | solution.py:197
Sparse Core Ops, SparseCore 0:
  153.6 39.0 reduce-scatter.3
  194.6 30.3 all-gather.1
  250.1 39.6 reduce-scatter.5
  313.1 62.6 reduce-scatter.7

commit v8 on v6

--- a/solution.py
+++ b/solution.py
@@ -161,10 +161,6 @@
     )
     shared_act = (jax.nn.silu(shared_pair[:, 0]) * shared_pair[:, 1]).astype(jnp.bfloat16)
     shared_term = jnp.dot(shared_act, shared_down, preferred_element_type=jnp.float32)
-    shared_term, normed_full = lax.optimization_barrier(
-        (shared_term.astype(jnp.bfloat16), normed_full)
-    )
-    shared_out = lax.psum_scatter(shared_term, "tensor", scatter_dimension=1, tiled=True)
     cap = tensor_count * (
         (4 * tok_dev * topk + 3 * experts * tensor_count - 1) // (3 * experts * tensor_count)
     )
@@ -181,7 +177,6 @@
     padded_full = jnp.concatenate([normed_full, jnp.zeros((1, D), jnp.bfloat16)], 0)
     outgoing = padded_full[source_rows].reshape(seq_count, exp_dev, cap, D)
     routed_rows = lax.all_to_all(outgoing, "seq", split_axis=0, concat_axis=0, tiled=True)
-    routed_rows, shared_out = lax.optimization_barrier((routed_rows, shared_out))
     expert_pair = jnp.einsum(
         "secd,edjf->secjf", routed_rows, expert_gate_up, preferred_element_type=jnp.float32
     )
@@ -189,9 +184,21 @@
     expert_term = jnp.einsum(
         "secf,efd->secd", expert_act, expert_down, preferred_element_type=jnp.float32
     )
-    expert_total = lax.psum_scatter(
-        expert_term.astype(jnp.bfloat16), "tensor", scatter_dimension=3, tiled=True
-    )
+    expert_rows = seq_count * exp_dev * cap
+    summed = lax.psum_scatter(
+        jnp.concatenate(
+            [
+                expert_term.astype(jnp.bfloat16).reshape(expert_rows, D),
+                shared_term.astype(jnp.bfloat16),
+            ],
+            0,
+        ),
+        "tensor",
+        scatter_dimension=1,
+        tiled=True,
+    )
+    expert_total = summed[:expert_rows].reshape(seq_count, exp_dev, cap, width_local)
+    shared_out = summed[expert_rows:]
     returned = lax.all_to_all(expert_total, "seq", split_axis=0, concat_axis=0, tiled=True)
     picked = returned.reshape(experts * cap, width_local)[slot_index].reshape(
         tok_dev, topk, width_local

time: 392 us -> 394 us (level)
    all_to_all x1, waiting for transfers between devices: 14.3 us -> 53.5 us  [shards(): lax.all_to_all(outgoing, 'seq', split_axis=0, concat_axis=0, tiled=True)]
    reduce_scatter x2 -> x1, waiting for transfers between devices: 107 us -> 69.7 us  [shards(): lax.psum_scatter(jnp.concatenate([expert_term.astype(jnp.bfloat16).reshap...]
  transfers between devices with their start and end apart: 9 -> 8, of which waited for: 8 -> 7; matrix products, arithmetic and copies ran while one was open for 6% -> 7% of each run, Pallas kernels for 0% -> 0%
where the time goes in v8:
time: 394 us; the launch traced here: 393 us
  waiting for transfers between devices  251 us (64%)
  local copies, waits for them, and re-layouts  41 us (10%)
  starting transfers between devices  34.7 us (9%)
  matrix products  32.4 us (8%)
  other arithmetic  20.1 us (5%)
  between operations  13.6 us (3%)
    reduce_scatter x1, waiting for transfers between devices, shards(): lax.psum_scatter(jnp.concatenate([expert_term.astype(jnp.bfloat16).reshap...  69.7 us
    all_to_all x1, waiting for transfers between devices, shards(): lax.all_to_all(outgoing, 'seq', split_axis=0, concat_axis=0, tiled=True)  53.5 us
    reduce_scatter x1, waiting for transfers between devices, shards(): lax.psum_scatter(projected.astype(jnp.bfloat16), 'tensor', scatter_dimens...  40 us
    all_to_all x1, waiting for transfers between devices, shards(): lax.all_to_all(spread, 'seq', 0, 0, tiled=True).reshape(tokens, width_local)  28 us
    all_to_all x1, waiting for transfers between devices, shards(): lax.all_to_all(local_out.reshape(seq_count, tok_dev, heads_local, HD).ast...  25.6 us
    all_gather x1, waiting for transfers between devices, shards(): lax.all_gather(jnp.concatenate([stream, norm_gain[None], router.astype(jn...  24.5 us
    dot_general x1, matrix products, shards(): jnp.einsum('rhqk,rkhd->rqhd', cached_weights.astype(jnp.bfloat16), cache_...  9.95 us
    all_to_all x1, waiting for transfers between devices, shards(): lax.all_to_all(expert_total, 'seq', split_axis=0, concat_axis=0, tiled=True)  9.37 us
  transfers between devices with their start and end apart: 8, of which 7 were waited for; matrix products, arithmetic and copies ran while one was open for 7% of the time, Pallas kernels for 0%

profile of v8, /device:TPU:65, one launch (start us, length us, event | category | flops | bytes accessed | tf_op | source)
XLA Modules:
  0.0 392.5 jit_solution(1531813881001990388)
XLA Ops:
  6.5 1.1 copy.130
  7.7 1.8 broadcast_in_dim.157
  9.4 8.5 %all-to-all-start = ((bf16[32,128,256]{1,2,0:T(8,128)(2,1)}), bf16[32,128,256]{1,2,0:T(8,128)(2,1)}, u32[]{:S(2)}, u32[]{:S(2)}) async-start(bf16[32,128,256]{1,2,0:T(8,128)(2,1)} %broadcast_in_dim.157), calls=%async_computation | async-start | bytes 4194304 | tf_op jit(solution)/shard_map/all_to_all | solution.py:60
  18.2 28.0 %all-to-all-done = bf16[32,128,256]{1,2,0:T(8,128)(2,1)} async-done(((bf16[32,128,256]{1,2,0:T(8,128)(2,1)}), bf16[32,128,256]{1,2,0:T(8,128)(2,1)}, u32[]{:S(2)}, u32[]{:S(2)}) %all-to-all-start) | async-done | bytes 2097184 | tf_op jit(solution)/shard_map/all_to_all | solution.py:60
  46.2 4.2 %copy.131 = bf16[32,128,256]{1,0,2:T(8,128)(2,1)} copy(bf16[32,128,256]{1,2,0:T(8,128)(2,1)} %all-to-all-done) | data formatting | bytes 4194304 | tf_op jit(solution)/shard_map/all_to_all | solution.py:60
  50.5 4.3 %reshape_reshape.3 = bf16[8,512,2,128]{1,0,3,2:T(8,128)(2,1)} reshape(bf16[32,128,256]{1,0,2:T(8,128)(2,1)} %copy.131) | data formatting | bytes 4194304 | tf_op jit(solution)/shard_map/reshape;reshape | solution.py:61
  54.8 2.1 constant_dynamic-slice_fusion
  56.9 1.0 copy.137
  57.9 1.2 select_reduce_fusion.1
  59.3 6.9 %select_reduce_fusion = (f32[8,2,512]{2,1,0:T(2,128)S(1)}, f32[8,2,512,512]{2,3,1,0:T(8,128)S(1)}) fusion(pred[8,512]{1,0:T(8,128)(4,1)S(1)} %broadcast_compare_fusion, bf16[8,512,2,128]{1,0,3,2:T(8,128)(2,1)} %reshape_reshape.3, bf16[8,512,256]{2,1,0:T(8,128)(2,1)} %param.19), kind=kOutput, calls=%fused_computation.4 | convolution fusion | flops 1086316544 | bytes 21008384 | tf_op jit(solution)/shard_map/rqhd,rkhd->rhqk/dot_general | solution.py:65
  66.2 3.6 fusion
  69.8 2.1 copy-done.1
  74.7 3.9 all-to-all-start.2
  78.6 0.8 copy.139
  79.4 0.8 copy.142
  80.2 1.2 convolution_bitcast_fusion
  81.4 10.0 %fusion.11 = bf16[8,512,2,128]{3,1,2,0:T(8,128)(2,1)S(1)} fusion(f32[8,2,512,512]{2,3,1,0:T(8,128)} %copy-done.1, f32[8,2,512]{2,1,0:T(2,128)} %copy-done.6, pred[8,512]{1,0:T(8,128)(4,1)S(1)} %broadcast_compare_fusion, f32[8,512,2]{1,2,0:T(2,128)S(1)} %copy.142, f32[512,2,128]{2,0,1:T(8,128)S(1)} %convolution_bitcast_fusion, f32[8,512,2]{1,2,0:T(2,128)S(1)} %copy.139, ...), kind=kOutput, calls=%fused_computation.17 | convolution fusion | flops 1095761920 | bytes 21598216 | tf_op jit(solution)/shard_map/rhqk,rkhd->rqhd/dot_general | solution.py:82
  91.5 1.4 copy.144
  92.9 8.0 %all-to-all-start.1 = ((bf16[32,128,2,128]{3,1,2,0:T(8,128)(2,1)}), bf16[32,128,2,128]{3,1,2,0:T(8,128)(2,1)}, u32[]{:S(2)}, u32[]{:S(2)}) async-start(bf16[32,128,2,128]{3,1,2,0:T(8,128)(2,1)} %copy.144), calls=%async_computation.1 | async-start | bytes 4194304 | tf_op jit(solution)/shard_map/all_to_all | solution.py:123
  101.1 25.6 %all-to-all-done.1 = bf16[32,128,2,128]{3,1,2,0:T(8,128)(2,1)} async-done(((bf16[32,128,2,128]{3,1,2,0:T(8,128)(2,1)}), bf16[32,128,2,128]{3,1,2,0:T(8,128)(2,1)}, u32[]{:S(2)}, u32[]{:S(2)}) %all-to-all-start.1) | async-done | bytes 2097184 | tf_op jit(solution)/shard_map/all_to_all | solution.py:123
  126.7 2.5 multiply_reduce_fusion
  129.4 2.4 convolution_convert_fusion.1
  131.9 40.0 %reduce-scatter.3.cloned.1.call-done = bf16[128,256]{1,0:T(8,128)(2,1)} async-done(((bf16[128,2048]{1,0:T(8,128)(2,1)}), bf16[128,256]{1,0:T(8,128)(2,1)}) %reduce-scatter.3.cloned.1.call-update) | async-done | bytes 65552 | tf_op jit(solution)/shard_map/reduce_scatter | solution.py:139
  171.9 0.9 convert_add_fusion
  173.9 1.8 reduce-window.6
  176.4 3.4 scatter_custom_fusion
  179.8 24.5 %all-gather.2.cloned.1.call-done = f32[193,2048]{1,0:T(8,128)} async-done(((f32[193,256]{1,0:T(8,128)}), f32[193,2048]{1,0:T(8,128)}) %all-gather.2.cloned.1.call-update) | async-done | bytes 1581072 | tf_op jit(solution)/shard_map/all_gather | solution.py:143
  204.3 1.4 multiply_reduce_fusion.2
  205.7 0.9 slice.60
  206.6 1.4 multiply_convert_fusion
  208.0 0.8 copy-done.2
  208.8 6.0 %gather_fusion = bf16[1024,2048]{1,0:T(8,128)(2,1)} fusion(bf16[129,2048]{1,0:T(8,128)(2,1)S(1)} %concatenate.10, s32[1024]{0:T(1024)S(1)} %fusion.61), kind=kCustom, calls=%fused_computation | custom fusion | bytes 8392704 | tf_op jit(solution)/shard_map/gather | solution.py:178
  214.8 7.3 %all-to-all-start.3 = ((bf16[32,2,16,2048]{3,2,1,0:T(8,128)(2,1)}), bf16[32,2,16,2048]{3,2,1,0:T(8,128)(2,1)}, u32[]{:S(2)}, u32[]{:S(2)}) async-start(bf16[32,2,16,2048]{3,2,1,0:T(8,128)(2,1)} %bitcast.175), calls=%async_computation.4 | async-start | bytes 8388608 | tf_op jit(solution)/shard_map/all_to_all | solution.py:179
  222.2 1.9 fusion.73
  224.1 1.5 convolution_convert_fusion
  225.6 53.5 %all-to-all-done.3 = bf16[32,2,16,2048]{3,2,1,0:T(8,128)(2,1)} async-done(((bf16[32,2,16,2048]{3,2,1,0:T(8,128)(2,1)}), bf16[32,2,16,2048]{3,2,1,0:T(8,128)(2,1)}, u32[]{:S(2)}, u32[]{:S(2)}) %all-to-all-start.3) | async-done | bytes 4194336 | tf_op jit(solution)/shard_map/all_to_all | solution.py:179
  279.1 4.6 %fusion.21 = f32[32,2,16,2,176]{4,2,3,0,1:T(8,128)S(1)} fusion(bf16[2,2048,2,176]{1,3,2,0:T(8,128)(2,1)S(1)} %copy-done, bf16[32,2,16,2048]{3,2,1,0:T(8,128)(2,1)} %all-to-all-done.3), kind=kOutput, calls=%fused_computation.29 | convolution fusion | flops 1476395008 | bytes 8519680 | tf_op jit(solution)/shard_map/secd,edjf->secjf/dot_general | solution.py:180
  283.7 1.3 convert_bitcast_fusion
  285.3 2.5 pad_maximum_fusion
  287.9 69.7 %reduce-scatter.5.cloned.1.call-done = bf16[1152,256]{1,0:T(8,128)(2,1)} async-done(((bf16[1152,2048]{1,0:T(8,128)(2,1)}), bf16[1152,256]{1,0:T(8,128)(2,1)}) %reduce-scatter.5.cloned.1.call-update) | async-done | bytes 589840 | tf_op jit(solution)/shard_map/reduce_scatter | solution.py:188
  357.6 1.9 slice.68
  359.5 6.9 %all-to-all-start.4 = ((bf16[32,2,16,256]{3,2,1,0:T(8,128)(2,1)}), bf16[32,2,16,256]{3,2,1,0:T(8,128)(2,1)S(1)}, u32[]{:S(2)}, u32[]{:S(2)}) async-start(bf16[32,2,16,256]{3,2,1,0:T(8,128)(2,1)} %bitcast.178), calls=%async_computation.6 | async-start | bytes 1048576 | tf_op jit(solution)/shard_map/all_to_all | solution.py:202
  366.4 1.5 fusion.34
  368.1 9.4 %all-to-all-done.4 = bf16[32,2,16,256]{3,2,1,0:T(8,128)(2,1)S(1)} async-done(((bf16[32,2,16,256]{3,2,1,0:T(8,128)(2,1)}), bf16[32,2,16,256]{3,2,1,0:T(8,128)(2,1)S(1)}, u32[]{:S(2)}, u32[]{:S(2)}) %all-to-all-start.4) | async-done | bytes 524320 | tf_op jit(solution)/shard_map/all_to_all | solution.py:202
  377.5 3.3 gather_fusion.1
  380.7 2.1 reshape.189
  382.8 1.6 multiply_reduce_fusion.1
  384.4 1.5 add_convert_fusion
  (71 shorter events, 6.2 us)
Async XLA Ops:
  6.5 272.5 %copy-start = (bf16[2,2048,2,176]{1,3,2,0:T(8,128)(2,1)S(1)}, bf16[2,2048,2,176]{1,3,2,0:T(8,128)(2,1)}, u32[]{:S(2)}) copy-start(bf16[2,2048,2,176]{1,3,2,0:T(8,128)(2,1)} %param.26) | copy-start | bytes 8650756
  6.5 11.5 %copy-start.11 = (s32[8]{0:T(128)S(1)}, s32[8]{0:T(128)}, u32[]{:S(2)}) copy-start(s32[8]{0:T(128)} %param.21) | copy-start | bytes 100
  9.4 36.8 %all-to-all-start = ((bf16[32,128,256]{1,2,0:T(8,128)(2,1)}), bf16[32,128,256]{1,2,0:T(8,128)(2,1)}, u32[]{:S(2)}, u32[]{:S(2)}) async-start(bf16[32,128,256]{1,2,0:T(8,128)(2,1)} %broadcast_in_dim.157), calls=%async_computation | async-start | bytes 4194304 | tf_op jit(solution)/shard_map/all_to_all | solution.py:60
  18.2 39.7 %copy-start.7 = (bf16[128,256]{1,0:T(8,128)(2,1)S(1)}, bf16[128,256]{1,0:T(8,128)(2,1)}, u32[]{:S(2)}) copy-start(bf16[128,256]{1,0:T(8,128)(2,1)} %param.17) | copy-start | bytes 196612
  66.2 5.7 %copy-start.1 = (f32[8,2,512,512]{2,3,1,0:T(8,128)}, f32[8,2,512,512]{2,3,1,0:T(8,128)S(1)}, u32[]{:S(2)}) copy-start(f32[8,2,512,512]{2,3,1,0:T(8,128)S(1)} %get-tuple-element.10) | copy-start | bytes 50331652
  66.2 5.7 %copy-start.6 = (f32[8,2,512]{2,1,0:T(2,128)}, f32[8,2,512]{2,1,0:T(2,128)S(1)}, u32[]{:S(2)}) copy-start(f32[8,2,512]{2,1,0:T(2,128)S(1)} %get-tuple-element.9) | copy-start | bytes 98308
  74.7 18.2 %all-to-all-start.2 = ((f32[32,128,2,2]{1,2,3,0:T(2,128)}), f32[32,128,2,2]{1,2,3,0:T(2,128)S(1)}, u32[]{:S(2)}, u32[]{:S(2)}) async-start(f32[32,128,2,2]{1,2,3,0:T(2,128)} %copy.146), calls=%async_computation.2 | async-start | bytes 131072 | tf_op jit(solution)/shard_map/all_to_all | solution.py:120
  92.9 39.0 %copy-start.9 = (bf16[256,64]{0,1:T(8,128)(2,1)S(1)}, bf16[256,64]{0,1:T(8,128)(2,1)}, u32[]{:S(2)}) copy-start(bf16[256,64]{0,1:T(8,128)(2,1)} %param.24) | copy-start | bytes 98308
  92.9 79.0 %copy-start.4 = (bf16[128,256]{1,0:T(8,128)(2,1)S(1)}, bf16[128,256]{1,0:T(8,128)(2,1)}, u32[]{:S(2)}) copy-start(bf16[128,256]{1,0:T(8,128)(2,1)} %param.15) | copy-start | bytes 196612
  92.9 79.8 %copy-start.10 = (f32[256]{0:T(256)S(1)}, f32[256]{0:T(256)}, u32[]{:S(2)}) copy-start(f32[256]{0:T(256)} %param.23) | copy-start | bytes 3076
  92.9 80.5 %copy-start.8 = (s32[128,6]{0,1:T(8,128)S(1)}, s32[128,6]{0,1:T(8,128)}, u32[]{:S(2)}) copy-start(s32[128,6]{0,1:T(8,128)} %param.25) | copy-start | bytes 9220
  92.9 33.8 %all-to-all-start.1 = ((bf16[32,128,2,128]{3,1,2,0:T(8,128)(2,1)}), bf16[32,128,2,128]{3,1,2,0:T(8,128)(2,1)}, u32[]{:S(2)}, u32[]{:S(2)}) async-start(bf16[32,128,2,128]{3,1,2,0:T(8,128)(2,1)} %copy.144), calls=%async_computation.1 | async-start | bytes 4194304 | tf_op jit(solution)/shard_map/all_to_all | solution.py:123
  100.9 70.9 %reduce-scatter.3.cloned.1.call-start = ((), (), s32[]{:S(2)}) async-start(), calls=%async_computation.7 | async-start | bytes 589824 | tf_op jit(solution)/shard_map/reduce_scatter | solution.py:139
  131.8 72.5 %all-gather.2.cloned.1.call-start = ((), (), s32[]{:S(2)}) async-start(), calls=%async_computation.8 | async-start | bytes 1843200 | tf_op jit(solution)/shard_map/all_gather | solution.py:143
  207.9 0.8 copy-start.2
  214.8 7.4 %copy-start.3 = (bf16[128,2048]{1,0:T(8,128)(2,1)S(1)}, bf16[128,2048]{1,0:T(8,128)(2,1)}, u32[]{:S(2)}) copy-start(bf16[128,2048]{1,0:T(8,128)(2,1)} %copy-done.2) | copy-start | bytes 1572868
  214.8 64.3 %all-to-all-start.3 = ((bf16[32,2,16,2048]{3,2,1,0:T(8,128)(2,1)}), bf16[32,2,16,2048]{3,2,1,0:T(8,128)(2,1)}, u32[]{:S(2)}, u32[]{:S(2)}) async-start(bf16[32,2,16,2048]{3,2,1,0:T(8,128)(2,1)} %bitcast.175), calls=%async_computation.4 | async-start | bytes 8388608 | tf_op jit(solution)/shard_map/all_to_all | solution.py:179
  222.1 135.5 %reduce-scatter.5.cloned.1.call-start = ((), (), s32[]{:S(2)}) async-start(), calls=%async_computation.9 | async-start | bytes 5308416 | tf_op jit(solution)/shard_map/reduce_scatter | solution.py:188
  279.1 4.6 %copy-start.12 = (bf16[2,176,2048]{2,1,0:T(8,128)(2,1)S(1)}, bf16[2,176,2048]{2,1,0:T(8,128)(2,1)}, u32[]{:S(2)}) copy-start(bf16[2,176,2048]{2,1,0:T(8,128)(2,1)} %param.27) | copy-start | bytes 4325380
  359.5 24.9 %copy-start.5 = (bf16[128,256]{1,0:T(8,128)(2,1)S(1)}, bf16[128,256]{1,0:T(8,128)(2,1)}, u32[]{:S(2)}) copy-start(bf16[128,256]{1,0:T(8,128)(2,1)} %param.15) | copy-start | bytes 196612
  359.5 18.0 %all-to-all-start.4 = ((bf16[32,2,16,256]{3,2,1,0:T(8,128)(2,1)}), bf16[32,2,16,256]{3,2,1,0:T(8,128)(2,1)S(1)}, u32[]{:S(2)}, u32[]{:S(2)}) async-start(bf16[32,2,16,256]{3,2,1,0:T(8,128)(2,1)} %bitcast.178), calls=%async_computation.6 | async-start | bytes 1048576 | tf_op jit(solution)/shard_map/all_to_all | solution.py:202
Sparse Core Ops, SparseCore 0:
  131.9 39.8 reduce-scatter.2
  173.7 30.5 all-gather.1
  288.0 69.5 reduce-scatter.4

commit v9 on v6

--- a/solution.py
+++ b/solution.py
@@ -136,9 +136,16 @@
         (weighted / row_sum[..., None]).astype(jnp.bfloat16).reshape(tok_dev, heads_local * HD)
     )
     projected = jnp.dot(attended, out_proj, preferred_element_type=jnp.float32)
-    attn_out = lax.psum_scatter(
-        projected.astype(jnp.bfloat16), "tensor", scatter_dimension=1, tiled=True
-    ).astype(jnp.float32)
+    attn_parts = lax.all_to_all(
+        jnp.transpose(
+            projected.astype(jnp.bfloat16).reshape(tok_dev, tensor_count, width_local), (1, 0, 2)
+        ),
+        "tensor",
+        0,
+        0,
+        tiled=True,
+    )
+    attn_out = jnp.sum(attn_parts.astype(jnp.float32), 0)
     stream = residual.astype(jnp.float32) + attn_out
     gathered = lax.all_gather(
         jnp.concatenate([stream, norm_gain[None], router.astype(jnp.float32).T], 0),

time: 392 us -> 376 us (0.959)
  waiting for transfers between devices: 249 us -> 220 us
  starting transfers between devices: 34.4 us -> 45.4 us
    reduce_scatter x1 -> x0, waiting for transfers between devices: 40 us -> none  [shards(): lax.psum_scatter(projected.astype(jnp.bfloat16), 'tensor', scatter_dimens...]
    all_to_all x0 -> x1, waiting for transfers between devices: none -> 13.9 us  [shards(): lax.all_to_all(jnp.transpose(projected.astype(jnp.bfloat16).reshape(tok_d...]
    all_to_all x0 -> x1, starting transfers between devices: none -> 11.2 us  [shards(): lax.all_to_all(jnp.transpose(projected.astype(jnp.bfloat16).reshape(tok_d...]
where the time goes in v9:
time: 376 us; the launch traced here: 374 us
  waiting for transfers between devices  220 us (59%)
  starting transfers between devices  45.4 us (12%)
  local copies, waits for them, and re-layouts  43.8 us (12%)
  matrix products  33.2 us (9%)
  other arithmetic  18.5 us (5%)
  between operations  13.5 us (4%)
    reduce_scatter x1, waiting for transfers between devices, shards(): lax.psum_scatter(expert_term.astype(jnp.bfloat16), 'tensor', scatter_dime...  63.3 us
    reduce_scatter x1, waiting for transfers between devices, shards(): lax.psum_scatter(shared_term, 'tensor', scatter_dimension=1, tiled=True)  43 us
    all_to_all x1, waiting for transfers between devices, shards(): lax.all_to_all(spread, 'seq', 0, 0, tiled=True).reshape(tokens, width_local)  28 us
    all_to_all x1, waiting for transfers between devices, shards(): lax.all_to_all(local_out.reshape(seq_count, tok_dev, heads_local, HD).ast...  25.4 us
    all_gather x1, waiting for transfers between devices, shards(): lax.all_gather(jnp.concatenate([stream, norm_gain[None], router.astype(jn...  22.3 us
    all_to_all x1, waiting for transfers between devices, shards(): lax.all_to_all(outgoing, 'seq', split_axis=0, concat_axis=0, tiled=True)  14.5 us
    all_to_all x1, waiting for transfers between devices, shards(): lax.all_to_all(jnp.transpose(projected.astype(jnp.bfloat16).reshape(tok_d...  13.9 us
    all_to_all x1, starting transfers between devices, shards(): lax.all_to_all(jnp.transpose(projected.astype(jnp.bfloat16).reshape(tok_d...  11.2 us
  transfers between devices with their start and end apart: 9, of which 8 were waited for; matrix products, arithmetic and copies ran while one was open for 6% of the time, Pallas kernels for 0%

profile of v9, /device:TPU:65, one launch (start us, length us, event | category | flops | bytes accessed | tf_op | source)
XLA Modules:
  0.0 374.1 jit_solution(12005836776888206941)
XLA Ops:
  6.5 1.1 copy.133
  7.7 1.8 broadcast_in_dim.157
  9.4 8.5 %all-to-all-start = ((bf16[32,128,256]{1,2,0:T(8,128)(2,1)}), bf16[32,128,256]{1,2,0:T(8,128)(2,1)}, u32[]{:S(2)}, u32[]{:S(2)}) async-start(bf16[32,128,256]{1,2,0:T(8,128)(2,1)} %broadcast_in_dim.157), calls=%async_computation | async-start | bytes 4194304 | tf_op jit(solution)/shard_map/all_to_all | solution.py:60
  18.2 28.0 %all-to-all-done = bf16[32,128,256]{1,2,0:T(8,128)(2,1)} async-done(((bf16[32,128,256]{1,2,0:T(8,128)(2,1)}), bf16[32,128,256]{1,2,0:T(8,128)(2,1)}, u32[]{:S(2)}, u32[]{:S(2)}) %all-to-all-start) | async-done | bytes 2097184 | tf_op jit(solution)/shard_map/all_to_all | solution.py:60
  46.2 4.2 %copy.134 = bf16[32,128,256]{1,0,2:T(8,128)(2,1)} copy(bf16[32,128,256]{1,2,0:T(8,128)(2,1)} %all-to-all-done) | data formatting | bytes 4194304 | tf_op jit(solution)/shard_map/all_to_all | solution.py:60
  50.5 4.3 %reshape_reshape.3 = bf16[8,512,2,128]{1,0,3,2:T(8,128)(2,1)} reshape(bf16[32,128,256]{1,0,2:T(8,128)(2,1)} %copy.134) | data formatting | bytes 4194304 | tf_op jit(solution)/shard_map/reshape;reshape | solution.py:61
  54.8 2.1 constant_dynamic-slice_fusion
  56.9 1.0 copy.140
  57.9 1.2 select_reduce_fusion.1
  59.3 6.9 %select_reduce_fusion = (f32[8,2,512]{2,1,0:T(2,128)S(1)}, f32[8,2,512,512]{2,3,1,0:T(8,128)S(1)}) fusion(pred[8,512]{1,0:T(8,128)(4,1)S(1)} %broadcast_compare_fusion, bf16[8,512,2,128]{1,0,3,2:T(8,128)(2,1)} %reshape_reshape.3, bf16[8,512,256]{2,1,0:T(8,128)(2,1)} %param.19), kind=kOutput, calls=%fused_computation.4 | convolution fusion | flops 1086316544 | bytes 21008384 | tf_op jit(solution)/shard_map/rqhd,rkhd->rhqk/dot_general | solution.py:65
  66.2 3.6 fusion
  69.8 2.1 copy-done.1
  74.7 3.9 %all-to-all-start.2 = ((f32[32,128,2,2]{1,2,3,0:T(2,128)}), f32[32,128,2,2]{1,2,3,0:T(2,128)S(1)}, u32[]{:S(2)}, u32[]{:S(2)}) async-start(f32[32,128,2,2]{1,2,3,0:T(2,128)} %copy.149), calls=%async_computation.2 | async-start | bytes 131072 | tf_op jit(solution)/shard_map/all_to_all | solution.py:120
  80.2 1.2 convolution_bitcast_fusion
  81.4 10.0 %fusion.11 = bf16[8,512,2,128]{3,1,2,0:T(8,128)(2,1)S(1)} fusion(f32[8,2,512,512]{2,3,1,0:T(8,128)} %copy-done.1, f32[8,2,512]{2,1,0:T(2,128)} %copy-done.6, pred[8,512]{1,0:T(8,128)(4,1)S(1)} %broadcast_compare_fusion, f32[8,512,2]{1,2,0:T(2,128)S(1)} %copy.145, f32[512,2,128]{2,0,1:T(8,128)S(1)} %convolution_bitcast_fusion, f32[8,512,2]{1,2,0:T(2,128)S(1)} %copy.142, ...), kind=kOutput, calls=%fused_computation.16 | convolution fusion | flops 1095761920 | bytes 21598216 | tf_op jit(solution)/shard_map/rhqk,rkhd->rqhd/dot_general | solution.py:82
  91.5 1.4 copy.147
  92.9 8.0 %all-to-all-start.1 = ((bf16[32,128,2,128]{3,1,2,0:T(8,128)(2,1)}), bf16[32,128,2,128]{3,1,2,0:T(8,128)(2,1)}, u32[]{:S(2)}, u32[]{:S(2)}) async-start(bf16[32,128,2,128]{3,1,2,0:T(8,128)(2,1)} %copy.147), calls=%async_computation.1 | async-start | bytes 4194304 | tf_op jit(solution)/shard_map/all_to_all | solution.py:123
  101.1 25.4 %all-to-all-done.1 = bf16[32,128,2,128]{3,1,2,0:T(8,128)(2,1)} async-done(((bf16[32,128,2,128]{3,1,2,0:T(8,128)(2,1)}), bf16[32,128,2,128]{3,1,2,0:T(8,128)(2,1)}, u32[]{:S(2)}, u32[]{:S(2)}) %all-to-all-start.1) | async-done | bytes 2097184 | tf_op jit(solution)/shard_map/all_to_all | solution.py:123
  126.5 2.5 multiply_reduce_fusion
  129.3 1.6 convolution_convert_fusion.1
  130.8 0.8 copy.219
  131.7 11.2 %all-to-all-start.3 = ((bf16[8,128,256]{2,1,0:T(8,128)(2,1)}), bf16[8,128,256]{2,1,0:T(8,128)(2,1)S(1)}, u32[]{:S(2)}, u32[]{:S(2)}) async-start(bf16[8,128,256]{2,1,0:T(8,128)(2,1)} %bitcast.183), calls=%async_computation.3 | async-start | bytes 1048576 | tf_op jit(solution)/shard_map/all_to_all | solution.py:139
  143.6 13.9 %all-to-all-done.3 = bf16[8,128,256]{2,1,0:T(8,128)(2,1)S(1)} async-done(((bf16[8,128,256]{2,1,0:T(8,128)(2,1)}), bf16[8,128,256]{2,1,0:T(8,128)(2,1)S(1)}, u32[]{:S(2)}, u32[]{:S(2)}) %all-to-all-start.3) | async-done | bytes 524320 | tf_op jit(solution)/shard_map/all_to_all | solution.py:139
  157.6 0.9 convert_add_fusion
  160.3 1.8 reduce-window.6
  162.8 3.4 scatter_custom_fusion
  166.2 22.3 %all-gather.2.cloned.1.call-done = f32[193,2048]{1,0:T(8,128)} async-done(((f32[193,256]{1,0:T(8,128)}), f32[193,2048]{1,0:T(8,128)}) %all-gather.2.cloned.1.call-update) | async-done | bytes 1581072 | tf_op jit(solution)/shard_map/all_gather | solution.py:150
  188.5 1.4 multiply_reduce_fusion.2
  190.0 0.9 slice.52
  190.8 1.4 multiply_convert_fusion
  193.0 1.9 fusion.73
  194.9 1.2 convolution_convert_fusion
  196.1 1.1 concatenate.7
  197.2 6.0 %gather_fusion = bf16[1024,2048]{1,0:T(8,128)(2,1)} fusion(bf16[129,2048]{1,0:T(8,128)(2,1)S(1)} %concatenate.7, s32[1024]{0:T(1024)S(1)} %fusion.61), kind=kCustom, calls=%fused_computation | custom fusion | bytes 8392704 | tf_op jit(solution)/shard_map/gather | solution.py:189
  203.2 7.1 %all-to-all-start.4 = ((bf16[32,2,16,2048]{3,2,1,0:T(8,128)(2,1)}), bf16[32,2,16,2048]{3,2,1,0:T(8,128)(2,1)}, u32[]{:S(2)}, u32[]{:S(2)}) async-start(bf16[32,2,16,2048]{3,2,1,0:T(8,128)(2,1)} %bitcast.180), calls=%async_computation.4 | async-start | bytes 8388608 | tf_op jit(solution)/shard_map/all_to_all | solution.py:190
  211.1 43.0 %reduce-scatter.3.cloned.1.call-done = bf16[128,256]{1,0:T(8,128)(2,1)} async-done(((bf16[128,2048]{1,0:T(8,128)(2,1)}), bf16[128,256]{1,0:T(8,128)(2,1)}) %reduce-scatter.3.cloned.1.call-update) | async-done | bytes 65552 | tf_op jit(solution)/shard_map/reduce_scatter | solution.py:174
  254.1 14.5 %all-to-all-done.4 = bf16[32,2,16,2048]{3,2,1,0:T(8,128)(2,1)} async-done(((bf16[32,2,16,2048]{3,2,1,0:T(8,128)(2,1)}), bf16[32,2,16,2048]{3,2,1,0:T(8,128)(2,1)}, u32[]{:S(2)}, u32[]{:S(2)}) %all-to-all-start.4) | async-done | bytes 4194336 | tf_op jit(solution)/shard_map/all_to_all | solution.py:190
  268.6 4.6 %fusion.21 = f32[32,2,16,2,176]{4,2,3,0,1:T(8,128)S(1)} fusion(bf16[2,2048,2,176]{1,3,2,0:T(8,128)(2,1)S(1)} %copy-done, bf16[32,2,16,2048]{3,2,1,0:T(8,128)(2,1)} %all-to-all-done.4), kind=kOutput, calls=%fused_computation.28 | convolution fusion | flops 1476395008 | bytes 8519680 | tf_op jit(solution)/shard_map/secd,edjf->secjf/dot_general | solution.py:192
  273.2 3.2 convert_bitcast_fusion
  276.5 63.3 %reduce-scatter.5.cloned.1.call-done = bf16[32,2,16,256]{3,2,0,1:T(8,128)(2,1)} async-done(((bf16[32,2,16,2048]{3,2,0,1:T(8,128)(2,1)}), bf16[32,2,16,256]{3,2,0,1:T(8,128)(2,1)}) %reduce-scatter.5.cloned.1.call-update) | async-done | bytes 524304 | tf_op jit(solution)/shard_map/reduce_scatter | solution.py:199
  339.8 1.9 copy.162
  341.7 6.6 %all-to-all-start.5 = ((bf16[32,2,16,256]{3,2,1,0:T(8,128)(2,1)}), bf16[32,2,16,256]{3,2,1,0:T(8,128)(2,1)S(1)}, u32[]{:S(2)}, u32[]{:S(2)}) async-start(bf16[32,2,16,256]{3,2,1,0:T(8,128)(2,1)} %copy.162), calls=%async_computation.7 | async-start | bytes 1048576 | tf_op jit(solution)/shard_map/all_to_all | solution.py:202
  348.3 1.5 fusion.34
  350.7 8.4 %all-to-all-done.5 = bf16[32,2,16,256]{3,2,1,0:T(8,128)(2,1)S(1)} async-done(((bf16[32,2,16,256]{3,2,1,0:T(8,128)(2,1)}), bf16[32,2,16,256]{3,2,1,0:T(8,128)(2,1)S(1)}, u32[]{:S(2)}, u32[]{:S(2)}) %all-to-all-start.5) | async-done | bytes 524320 | tf_op jit(solution)/shard_map/all_to_all | solution.py:202
  359.1 3.3 gather_fusion.1
  362.4 2.1 reshape.185
  364.5 1.6 multiply_reduce_fusion.1
  366.1 1.5 add_convert_fusion
  (71 shorter events, 10.9 us)
Async XLA Ops:
  6.5 262.1 %copy-start = (bf16[2,2048,2,176]{1,3,2,0:T(8,128)(2,1)S(1)}, bf16[2,2048,2,176]{1,3,2,0:T(8,128)(2,1)}, u32[]{:S(2)}) copy-start(bf16[2,2048,2,176]{1,3,2,0:T(8,128)(2,1)} %param.26) | copy-start | bytes 8650756
  6.5 11.5 %copy-start.10 = (s32[8]{0:T(128)S(1)}, s32[8]{0:T(128)}, u32[]{:S(2)}) copy-start(s32[8]{0:T(128)} %param.21) | copy-start | bytes 100
  9.4 36.8 %all-to-all-start = ((bf16[32,128,256]{1,2,0:T(8,128)(2,1)}), bf16[32,128,256]{1,2,0:T(8,128)(2,1)}, u32[]{:S(2)}, u32[]{:S(2)}) async-start(bf16[32,128,256]{1,2,0:T(8,128)(2,1)} %broadcast_in_dim.157), calls=%async_computation | async-start | bytes 4194304 | tf_op jit(solution)/shard_map/all_to_all | solution.py:60
  18.2 39.7 %copy-start.7 = (bf16[128,256]{1,0:T(8,128)(2,1)S(1)}, bf16[128,256]{1,0:T(8,128)(2,1)}, u32[]{:S(2)}) copy-start(bf16[128,256]{1,0:T(8,128)(2,1)} %param.17) | copy-start | bytes 196612
  66.2 5.7 %copy-start.1 = (f32[8,2,512,512]{2,3,1,0:T(8,128)}, f32[8,2,512,512]{2,3,1,0:T(8,128)S(1)}, u32[]{:S(2)}) copy-start(f32[8,2,512,512]{2,3,1,0:T(8,128)S(1)} %get-tuple-element.18) | copy-start | bytes 50331652
  66.2 5.7 %copy-start.6 = (f32[8,2,512]{2,1,0:T(2,128)}, f32[8,2,512]{2,1,0:T(2,128)S(1)}, u32[]{:S(2)}) copy-start(f32[8,2,512]{2,1,0:T(2,128)S(1)} %get-tuple-element.17) | copy-start | bytes 98308
  74.7 18.2 %all-to-all-start.2 = ((f32[32,128,2,2]{1,2,3,0:T(2,128)}), f32[32,128,2,2]{1,2,3,0:T(2,128)S(1)}, u32[]{:S(2)}, u32[]{:S(2)}) async-start(f32[32,128,2,2]{1,2,3,0:T(2,128)} %copy.149), calls=%async_computation.2 | async-start | bytes 131072 | tf_op jit(solution)/shard_map/all_to_all | solution.py:120
  92.9 33.6 %all-to-all-start.1 = ((bf16[32,128,2,128]{3,1,2,0:T(8,128)(2,1)}), bf16[32,128,2,128]{3,1,2,0:T(8,128)(2,1)}, u32[]{:S(2)}, u32[]{:S(2)}) async-start(bf16[32,128,2,128]{3,1,2,0:T(8,128)(2,1)} %copy.147), calls=%async_computation.1 | async-start | bytes 4194304 | tf_op jit(solution)/shard_map/all_to_all | solution.py:123
  100.9 58.2 %copy-start.9 = (f32[256]{0:T(256)S(1)}, f32[256]{0:T(256)}, u32[]{:S(2)}) copy-start(f32[256]{0:T(256)} %param.23) | copy-start | bytes 3076
  101.0 58.9 %copy-start.8 = (s32[128,6]{0,1:T(8,128)S(1)}, s32[128,6]{0,1:T(8,128)}, u32[]{:S(2)}) copy-start(s32[128,6]{0,1:T(8,128)} %param.25) | copy-start | bytes 9220
  131.7 25.9 %all-to-all-start.3 = ((bf16[8,128,256]{2,1,0:T(8,128)(2,1)}), bf16[8,128,256]{2,1,0:T(8,128)(2,1)S(1)}, u32[]{:S(2)}, u32[]{:S(2)}) async-start(bf16[8,128,256]{2,1,0:T(8,128)(2,1)} %bitcast.183), calls=%async_computation.3 | async-start | bytes 1048576 | tf_op jit(solution)/shard_map/all_to_all | solution.py:139
  142.9 45.7 %all-gather.2.cloned.1.call-start = ((), (), s32[]{:S(2)}) async-start(), calls=%async_computation.8 | async-start | bytes 1843200 | tf_op jit(solution)/shard_map/all_gather | solution.py:150
  158.5 0.7 copy-start.3
  188.5 6.4 %copy-start.5 = (bf16[176,2048]{1,0:T(8,128)(2,1)S(1)}, bf16[176,2048]{1,0:T(8,128)(2,1)}, u32[]{:S(2)}) copy-start(bf16[176,2048]{1,0:T(8,128)(2,1)} %param.29) | copy-start | bytes 2162692
  192.2 0.8 copy-start.2
  203.2 65.4 %all-to-all-start.4 = ((bf16[32,2,16,2048]{3,2,1,0:T(8,128)(2,1)}), bf16[32,2,16,2048]{3,2,1,0:T(8,128)(2,1)}, u32[]{:S(2)}, u32[]{:S(2)}) async-start(bf16[32,2,16,2048]{3,2,1,0:T(8,128)(2,1)} %bitcast.180), calls=%async_computation.4 | async-start | bytes 8388608 | tf_op jit(solution)/shard_map/all_to_all | solution.py:190
  210.3 43.8 %reduce-scatter.3.cloned.1.call-start = ((), (), s32[]{:S(2)}) async-start(), calls=%async_computation.9 | async-start | bytes 589824 | tf_op jit(solution)/shard_map/reduce_scatter | solution.py:174
  211.0 128.8 %reduce-scatter.5.cloned.1.call-start = ((), (), s32[]{:S(2)}) async-start(), calls=%async_computation.10 | async-start | bytes 4718592 | tf_op jit(solution)/shard_map/reduce_scatter | solution.py:199
  268.6 4.6 %copy-start.11 = (bf16[2,176,2048]{2,1,0:T(8,128)(2,1)S(1)}, bf16[2,176,2048]{2,1,0:T(8,128)(2,1)}, u32[]{:S(2)}) copy-start(bf16[2,176,2048]{2,1,0:T(8,128)(2,1)} %param.27) | copy-start | bytes 4325380
  341.7 24.4 %copy-start.4 = (f32[128,256]{1,0:T(8,128)S(1)}, f32[128,256]{1,0:T(8,128)}, u32[]{:S(2)}) copy-start(f32[128,256]{1,0:T(8,128)} %copy-done.3) | copy-start | bytes 393220
  341.7 17.4 %all-to-all-start.5 = ((bf16[32,2,16,256]{3,2,1,0:T(8,128)(2,1)}), bf16[32,2,16,256]{3,2,1,0:T(8,128)(2,1)S(1)}, u32[]{:S(2)}, u32[]{:S(2)}) async-start(bf16[32,2,16,256]{3,2,1,0:T(8,128)(2,1)} %copy.162), calls=%async_computation.7 | async-start | bytes 1048576 | tf_op jit(solution)/shard_map/all_to_all | solution.py:202
Sparse Core Ops, SparseCore 0:
  160.0 28.5 all-gather.1
  213.6 40.4 reduce-scatter.2
  276.6 63.1 reduce-scatter.4

commit v10 on v9

--- a/solution.py
+++ b/solution.py
@@ -147,15 +147,15 @@
     )
     attn_out = jnp.sum(attn_parts.astype(jnp.float32), 0)
     stream = residual.astype(jnp.float32) + attn_out
-    gathered = lax.all_gather(
-        jnp.concatenate([stream, norm_gain[None], router.astype(jnp.float32).T], 0),
+    weights_full = lax.all_gather(
+        jnp.concatenate([norm_gain[None], router.astype(jnp.float32).T], 0),
         "tensor",
         axis=1,
         tiled=True,
     )
-    stream_full = gathered[:tok_dev]
-    gain_full = gathered[tok_dev]
-    router_full = gathered[tok_dev + 1 :].T.astype(jnp.bfloat16)
+    stream_full = lax.all_gather(stream, "tensor", axis=1, tiled=True)
+    gain_full = weights_full[0]
+    router_full = weights_full[1:].T.astype(jnp.bfloat16)
     inverse_rms = lax.rsqrt(jnp.sum(stream_full * stream_full, 1) / D + epsilon)
     normed_full = (stream_full * inverse_rms[:, None] * gain_full).astype(jnp.bfloat16)
     logits = jnp.dot(normed_full, router_full, preferred_element_type=jnp.float32)

time: 376 us -> 369 us (0.981)
  blocking collectives: 0 us -> 46 us
  waiting for transfers between devices: 220 us -> 184 us
  starting transfers between devices: 45.4 us -> 32.4 us
    all_to_all x0 -> x1, blocking collectives: none -> 26.3 us  [shards(): lax.all_to_all(jnp.transpose(projected.astype(jnp.bfloat16).reshape(tok_d...]
    all_gather x1, waiting for transfers between devices: 22.3 us -> 0.02 us  [shards(): stream_full = lax.all_gather(stream, 'tensor', axis=1, tiled=True)]
    all_gather x0 -> x1, blocking collectives: none -> 19.7 us  [shards(): lax.all_gather(jnp.concatenate([norm_gain[None], router.astype(jnp.float3...]
    all_to_all x1 -> x0, waiting for transfers between devices: 13.9 us -> none  [shards(): lax.all_to_all(jnp.transpose(projected.astype(jnp.bfloat16).reshape(tok_d...]
    all_to_all x1 -> x0, starting transfers between devices: 11.2 us -> none  [shards(): lax.all_to_all(jnp.transpose(projected.astype(jnp.bfloat16).reshape(tok_d...]
  transfers between devices with their start and end apart: 9 -> 8, of which waited for: 8 -> 6; matrix products, arithmetic and copies ran while one was open for 6% -> 6% of each run, Pallas kernels for 0% -> 0%
where the time goes in v10:
time: 369 us; the launch traced here: 368 us
  waiting for transfers between devices  184 us (50%)
  blocking collectives  46 us (12%)
  local copies, waits for them, and re-layouts  42.5 us (12%)
  matrix products  33.2 us (9%)
  starting transfers between devices  32.4 us (9%)
  other arithmetic  16.9 us (5%)
  between operations  13.6 us (4%)
    reduce_scatter x1, waiting for transfers between devices, shards(): lax.psum_scatter(expert_term.astype(jnp.bfloat16), 'tensor', scatter_dime...  63.6 us
    reduce_scatter x1, waiting for transfers between devices, shards(): lax.psum_scatter(shared_term, 'tensor', scatter_dimension=1, tiled=True)  43.6 us
    all_to_all x1, waiting for transfers between devices, shards(): lax.all_to_all(spread, 'seq', 0, 0, tiled=True).reshape(tokens, width_local)  28 us
    all_to_all x1, blocking collectives, shards(): lax.all_to_all(jnp.transpose(projected.astype(jnp.bfloat16).reshape(tok_d...  26.3 us
    all_to_all x1, waiting for transfers between devices, shards(): lax.all_to_all(local_out.reshape(seq_count, tok_dev, heads_local, HD).ast...  25.4 us
    all_gather x1, blocking collectives, shards(): lax.all_gather(jnp.concatenate([norm_gain[None], router.astype(jnp.float3...  19.7 us
    all_to_all x1, waiting for transfers between devices, shards(): lax.all_to_all(outgoing, 'seq', split_axis=0, concat_axis=0, tiled=True)  13.8 us
    dot_general x1, matrix products, shards(): jnp.einsum('rhqk,rkhd->rqhd', cached_weights.astype(jnp.bfloat16), cache_...  9.95 us
  transfers between devices with their start and end apart: 8, of which 6 were waited for; matrix products, arithmetic and copies ran while one was open for 6% of the time, Pallas kernels for 0%

profile of v10, /device:TPU:65, one launch (start us, length us, event | category | flops | bytes accessed | tf_op | source)
XLA Modules:
  0.0 368.1 jit_solution(11455973162677981198)
XLA Ops:
  6.5 1.1 copy.133
  7.7 1.8 broadcast_in_dim.157
  9.4 8.5 %all-to-all-start = ((bf16[32,128,256]{1,2,0:T(8,128)(2,1)}), bf16[32,128,256]{1,2,0:T(8,128)(2,1)}, u32[]{:S(2)}, u32[]{:S(2)}) async-start(bf16[32,128,256]{1,2,0:T(8,128)(2,1)} %broadcast_in_dim.157), calls=%async_computation | async-start | bytes 4194304 | tf_op jit(solution)/shard_map/all_to_all | solution.py:60
  18.2 28.0 %all-to-all-done = bf16[32,128,256]{1,2,0:T(8,128)(2,1)} async-done(((bf16[32,128,256]{1,2,0:T(8,128)(2,1)}), bf16[32,128,256]{1,2,0:T(8,128)(2,1)}, u32[]{:S(2)}, u32[]{:S(2)}) %all-to-all-start) | async-done | bytes 2097184 | tf_op jit(solution)/shard_map/all_to_all | solution.py:60
  46.2 4.2 %copy.134 = bf16[32,128,256]{1,0,2:T(8,128)(2,1)} copy(bf16[32,128,256]{1,2,0:T(8,128)(2,1)} %all-to-all-done) | data formatting | bytes 4194304 | tf_op jit(solution)/shard_map/all_to_all | solution.py:60
  50.5 4.3 %reshape_reshape.3 = bf16[8,512,2,128]{1,0,3,2:T(8,128)(2,1)} reshape(bf16[32,128,256]{1,0,2:T(8,128)(2,1)} %copy.134) | data formatting | bytes 4194304 | tf_op jit(solution)/shard_map/reshape;reshape | solution.py:61
  54.8 2.1 constant_dynamic-slice_fusion
  56.9 1.0 copy.140
  57.9 1.2 select_reduce_fusion.1
  59.3 6.9 %select_reduce_fusion = (f32[8,2,512]{2,1,0:T(2,128)S(1)}, f32[8,2,512,512]{2,3,1,0:T(8,128)S(1)}) fusion(pred[8,512]{1,0:T(8,128)(4,1)S(1)} %broadcast_compare_fusion, bf16[8,512,2,128]{1,0,3,2:T(8,128)(2,1)} %reshape_reshape.3, bf16[8,512,256]{2,1,0:T(8,128)(2,1)} %param.19), kind=kOutput, calls=%fused_computation.4 | convolution fusion | flops 1086316544 | bytes 21008384 | tf_op jit(solution)/shard_map/rqhd,rkhd->rhqk/dot_general | solution.py:65
  66.2 3.6 fusion
  69.8 2.1 copy-done.1
  74.7 3.9 %all-to-all-start.2 = ((f32[32,128,2,2]{1,2,3,0:T(2,128)}), f32[32,128,2,2]{1,2,3,0:T(2,128)S(1)}, u32[]{:S(2)}, u32[]{:S(2)}) async-start(f32[32,128,2,2]{1,2,3,0:T(2,128)} %copy.149), calls=%async_computation.2 | async-start | bytes 131072 | tf_op jit(solution)/shard_map/all_to_all | solution.py:120
  78.6 0.8 copy.142
  79.4 0.8 copy.145
  80.2 1.2 convolution_bitcast_fusion
  81.4 10.0 %fusion.11 = bf16[8,512,2,128]{3,1,2,0:T(8,128)(2,1)S(1)} fusion(f32[8,2,512,512]{2,3,1,0:T(8,128)} %copy-done.1, f32[8,2,512]{2,1,0:T(2,128)} %copy-done.6, pred[8,512]{1,0:T(8,128)(4,1)S(1)} %broadcast_compare_fusion, f32[8,512,2]{1,2,0:T(2,128)S(1)} %copy.145, f32[512,2,128]{2,0,1:T(8,128)S(1)} %convolution_bitcast_fusion, f32[8,512,2]{1,2,0:T(2,128)S(1)} %copy.142, ...), kind=kOutput, calls=%fused_computation.16 | convolution fusion | flops 1095761920 | bytes 21598216 | tf_op jit(solution)/shard_map/rhqk,rkhd->rqhd/dot_general | solution.py:82
  91.5 1.4 copy.147
  92.9 8.0 %all-to-all-start.1 = ((bf16[32,128,2,128]{3,1,2,0:T(8,128)(2,1)}), bf16[32,128,2,128]{3,1,2,0:T(8,128)(2,1)}, u32[]{:S(2)}, u32[]{:S(2)}) async-start(bf16[32,128,2,128]{3,1,2,0:T(8,128)(2,1)} %copy.147), calls=%async_computation.1 | async-start | bytes 4194304 | tf_op jit(solution)/shard_map/all_to_all | solution.py:123
  101.2 25.4 %all-to-all-done.1 = bf16[32,128,2,128]{3,1,2,0:T(8,128)(2,1)} async-done(((bf16[32,128,2,128]{3,1,2,0:T(8,128)(2,1)}), bf16[32,128,2,128]{3,1,2,0:T(8,128)(2,1)}, u32[]{:S(2)}, u32[]{:S(2)}) %all-to-all-start.1) | async-done | bytes 2097184 | tf_op jit(solution)/shard_map/all_to_all | solution.py:123
  126.5 2.5 multiply_reduce_fusion
  129.3 1.6 convolution_convert_fusion.1
  130.9 26.3 %all_to_all.30 = bf16[8,128,256]{2,1,0:T(8,128)(2,1)S(1)} all-to-all(bf16[8,128,256]{2,1,0:T(8,128)(2,1)S(1)} %bitcast.183), channel_id=1, replica_groups=mesh['seq'=32,'tensor'=8] {'tensor'}, dimensions={0} | all-to-all | bytes 1048576 | tf_op jit(solution)/shard_map/all_to_all | solution.py:139
  158.4 19.7 %all_gather.7 = f32[65,2048]{1,0:T(8,128)S(1)} all-gather(f32[65,256]{1,0:T(8,128)S(1)} %pad_maximum_fusion), channel_id=1, replica_groups=mesh['seq'=32,'tensor'=8] {'tensor'}, dimensions={1}, use_global_device_ids=true | all-gather | bytes 599040 | tf_op jit(solution)/shard_map/all_gather | solution.py:150
  178.1 0.9 copy-done.3
  179.0 1.8 reduce-window.6
  181.6 3.4 scatter_custom_fusion
  185.0 1.4 multiply_reduce_fusion.2
  186.5 1.4 multiply_convert_fusion
  187.9 0.8 copy-done.2
  188.7 1.9 fusion.73
  190.6 1.1 convolution_convert_fusion
  191.8 1.1 concatenate.7
  192.8 6.0 %gather_fusion = bf16[1024,2048]{1,0:T(8,128)(2,1)} fusion(bf16[129,2048]{1,0:T(8,128)(2,1)S(1)} %concatenate.7, s32[1024]{0:T(1024)S(1)} %fusion.61), kind=kCustom, calls=%fused_computation | custom fusion | bytes 8392704 | tf_op jit(solution)/shard_map/gather | solution.py:189
  198.9 5.2 %all-to-all-start.4 = ((bf16[32,2,16,2048]{3,2,1,0:T(8,128)(2,1)}), bf16[32,2,16,2048]{3,2,1,0:T(8,128)(2,1)}, u32[]{:S(2)}, u32[]{:S(2)}) async-start(bf16[32,2,16,2048]{3,2,1,0:T(8,128)(2,1)} %bitcast.180), calls=%async_computation.4 | async-start | bytes 8388608 | tf_op jit(solution)/shard_map/all_to_all | solution.py:190
  204.8 43.6 %reduce-scatter.3.cloned.1.call-done = bf16[128,256]{1,0:T(8,128)(2,1)} async-done(((bf16[128,2048]{1,0:T(8,128)(2,1)}), bf16[128,256]{1,0:T(8,128)(2,1)}) %reduce-scatter.3.cloned.1.call-update) | async-done | bytes 65552 | tf_op jit(solution)/shard_map/reduce_scatter | solution.py:174
  248.5 13.8 %all-to-all-done.4 = bf16[32,2,16,2048]{3,2,1,0:T(8,128)(2,1)} async-done(((bf16[32,2,16,2048]{3,2,1,0:T(8,128)(2,1)}), bf16[32,2,16,2048]{3,2,1,0:T(8,128)(2,1)}, u32[]{:S(2)}, u32[]{:S(2)}) %all-to-all-start.4) | async-done | bytes 4194336 | tf_op jit(solution)/shard_map/all_to_all | solution.py:190
  262.3 4.6 %fusion.21 = f32[32,2,16,2,176]{4,2,3,0,1:T(8,128)S(1)} fusion(bf16[2,2048,2,176]{1,3,2,0:T(8,128)(2,1)S(1)} %copy-done, bf16[32,2,16,2048]{3,2,1,0:T(8,128)(2,1)} %all-to-all-done.4), kind=kOutput, calls=%fused_computation.28 | convolution fusion | flops 1476395008 | bytes 8519680 | tf_op jit(solution)/shard_map/secd,edjf->secjf/dot_general | solution.py:192
  266.9 3.2 convert_bitcast_fusion
  270.2 63.6 %reduce-scatter.5.cloned.1.call-done = bf16[32,2,16,256]{3,2,0,1:T(8,128)(2,1)} async-done(((bf16[32,2,16,2048]{3,2,0,1:T(8,128)(2,1)}), bf16[32,2,16,256]{3,2,0,1:T(8,128)(2,1)}) %reduce-scatter.5.cloned.1.call-update) | async-done | bytes 524304 | tf_op jit(solution)/shard_map/reduce_scatter | solution.py:199
  333.8 1.9 copy.162
  335.7 6.6 %all-to-all-start.5 = ((bf16[32,2,16,256]{3,2,1,0:T(8,128)(2,1)}), bf16[32,2,16,256]{3,2,1,0:T(8,128)(2,1)S(1)}, u32[]{:S(2)}, u32[]{:S(2)}) async-start(bf16[32,2,16,256]{3,2,1,0:T(8,128)(2,1)} %copy.162), calls=%async_computation.7 | async-start | bytes 1048576 | tf_op jit(solution)/shard_map/all_to_all | solution.py:202
  342.3 1.5 fusion.34
  344.7 8.4 %all-to-all-done.5 = bf16[32,2,16,256]{3,2,1,0:T(8,128)(2,1)S(1)} async-done(((bf16[32,2,16,256]{3,2,1,0:T(8,128)(2,1)}), bf16[32,2,16,256]{3,2,1,0:T(8,128)(2,1)S(1)}, u32[]{:S(2)}, u32[]{:S(2)}) %all-to-all-start.5) | async-done | bytes 524320 | tf_op jit(solution)/shard_map/all_to_all | solution.py:202
  353.1 3.3 gather_fusion.1
  356.3 2.1 reshape.185
  358.4 1.6 multiply_reduce_fusion.1
  360.0 1.5 add_convert_fusion
  (75 shorter events, 7.3 us)
Async XLA Ops:
  6.5 255.7 %copy-start = (bf16[2,2048,2,176]{1,3,2,0:T(8,128)(2,1)S(1)}, bf16[2,2048,2,176]{1,3,2,0:T(8,128)(2,1)}, u32[]{:S(2)}) copy-start(bf16[2,2048,2,176]{1,3,2,0:T(8,128)(2,1)} %param.26) | copy-start | bytes 8650756
  6.5 11.5 %copy-start.12 = (s32[8]{0:T(128)S(1)}, s32[8]{0:T(128)}, u32[]{:S(2)}) copy-start(s32[8]{0:T(128)} %param.21) | copy-start | bytes 100
  9.4 36.8 %all-to-all-start = ((bf16[32,128,256]{1,2,0:T(8,128)(2,1)}), bf16[32,128,256]{1,2,0:T(8,128)(2,1)}, u32[]{:S(2)}, u32[]{:S(2)}) async-start(bf16[32,128,256]{1,2,0:T(8,128)(2,1)} %broadcast_in_dim.157), calls=%async_computation | async-start | bytes 4194304 | tf_op jit(solution)/shard_map/all_to_all | solution.py:60
  18.2 39.7 %copy-start.7 = (bf16[128,256]{1,0:T(8,128)(2,1)S(1)}, bf16[128,256]{1,0:T(8,128)(2,1)}, u32[]{:S(2)}) copy-start(bf16[128,256]{1,0:T(8,128)(2,1)} %param.17) | copy-start | bytes 196612
  66.2 5.7 %copy-start.1 = (f32[8,2,512,512]{2,3,1,0:T(8,128)}, f32[8,2,512,512]{2,3,1,0:T(8,128)S(1)}, u32[]{:S(2)}) copy-start(f32[8,2,512,512]{2,3,1,0:T(8,128)S(1)} %get-tuple-element.18) | copy-start | bytes 50331652
  66.2 5.7 %copy-start.6 = (f32[8,2,512]{2,1,0:T(2,128)}, f32[8,2,512]{2,1,0:T(2,128)S(1)}, u32[]{:S(2)}) copy-start(f32[8,2,512]{2,1,0:T(2,128)S(1)} %get-tuple-element.17) | copy-start | bytes 98308
  74.7 18.2 %all-to-all-start.2 = ((f32[32,128,2,2]{1,2,3,0:T(2,128)}), f32[32,128,2,2]{1,2,3,0:T(2,128)S(1)}, u32[]{:S(2)}, u32[]{:S(2)}) async-start(f32[32,128,2,2]{1,2,3,0:T(2,128)} %copy.149), calls=%async_computation.2 | async-start | bytes 131072 | tf_op jit(solution)/shard_map/all_to_all | solution.py:120
  92.9 33.6 %all-to-all-start.1 = ((bf16[32,128,2,128]{3,1,2,0:T(8,128)(2,1)}), bf16[32,128,2,128]{3,1,2,0:T(8,128)(2,1)}, u32[]{:S(2)}, u32[]{:S(2)}) async-start(bf16[32,128,2,128]{3,1,2,0:T(8,128)(2,1)} %copy.147), calls=%async_computation.1 | async-start | bytes 4194304 | tf_op jit(solution)/shard_map/all_to_all | solution.py:123
  100.9 56.3 %copy-start.8 = (bf16[128,256]{1,0:T(8,128)(2,1)S(1)}, bf16[128,256]{1,0:T(8,128)(2,1)}, u32[]{:S(2)}) copy-start(bf16[128,256]{1,0:T(8,128)(2,1)} %param.15) | copy-start | bytes 196612
  101.0 57.0 %copy-start.9 = (s32[128,6]{0,1:T(8,128)S(1)}, s32[128,6]{0,1:T(8,128)}, u32[]{:S(2)}) copy-start(s32[128,6]{0,1:T(8,128)} %param.25) | copy-start | bytes 9220
  101.0 57.4 %copy-start.10 = (bf16[256,64]{0,1:T(8,128)(2,1)S(1)}, bf16[256,64]{0,1:T(8,128)(2,1)}, u32[]{:S(2)}) copy-start(bf16[256,64]{0,1:T(8,128)(2,1)} %param.24) | copy-start | bytes 98308
  101.0 57.4 %copy-start.11 = (f32[256]{0:T(256)S(1)}, f32[256]{0:T(256)}, u32[]{:S(2)}) copy-start(f32[256]{0:T(256)} %param.23) | copy-start | bytes 3076
  101.0 84.0 %all-gather.2.cloned.1.call-start = ((), (), s32[]{:S(2)}) async-start(), calls=%async_computation.8 | async-start | bytes 1179648 | tf_op jit(solution)/shard_map/all_gather | solution.py:156
  178.1 0.9 copy-start.3
  185.0 5.6 %copy-start.5 = (bf16[176,2048]{1,0:T(8,128)(2,1)S(1)}, bf16[176,2048]{1,0:T(8,128)(2,1)}, u32[]{:S(2)}) copy-start(bf16[176,2048]{1,0:T(8,128)(2,1)} %param.29) | copy-start | bytes 2162692
  187.9 0.8 copy-start.2
  198.9 63.4 %all-to-all-start.4 = ((bf16[32,2,16,2048]{3,2,1,0:T(8,128)(2,1)}), bf16[32,2,16,2048]{3,2,1,0:T(8,128)(2,1)}, u32[]{:S(2)}, u32[]{:S(2)}) async-start(bf16[32,2,16,2048]{3,2,1,0:T(8,128)(2,1)} %bitcast.180), calls=%async_computation.4 | async-start | bytes 8388608 | tf_op jit(solution)/shard_map/all_to_all | solution.py:190
  204.0 44.4 %reduce-scatter.3.cloned.1.call-start = ((), (), s32[]{:S(2)}) async-start(), calls=%async_computation.9 | async-start | bytes 589824 | tf_op jit(solution)/shard_map/reduce_scatter | solution.py:174
  204.8 129.0 %reduce-scatter.5.cloned.1.call-start = ((), (), s32[]{:S(2)}) async-start(), calls=%async_computation.10 | async-start | bytes 4718592 | tf_op jit(solution)/shard_map/reduce_scatter | solution.py:199
  262.3 4.7 %copy-start.13 = (bf16[2,176,2048]{2,1,0:T(8,128)(2,1)S(1)}, bf16[2,176,2048]{2,1,0:T(8,128)(2,1)}, u32[]{:S(2)}) copy-start(bf16[2,176,2048]{2,1,0:T(8,128)(2,1)} %param.27) | copy-start | bytes 4325380
  335.7 24.4 %copy-start.4 = (f32[128,256]{1,0:T(8,128)S(1)}, f32[128,256]{1,0:T(8,128)}, u32[]{:S(2)}) copy-start(f32[128,256]{1,0:T(8,128)} %convert_add_fusion) | copy-start | bytes 393220
  335.7 17.4 %all-to-all-start.5 = ((bf16[32,2,16,256]{3,2,1,0:T(8,128)(2,1)}), bf16[32,2,16,256]{3,2,1,0:T(8,128)(2,1)S(1)}, u32[]{:S(2)}, u32[]{:S(2)}) async-start(bf16[32,2,16,256]{3,2,1,0:T(8,128)(2,1)} %copy.162), calls=%async_computation.7 | async-start | bytes 1048576 | tf_op jit(solution)/shard_map/all_to_all | solution.py:202
Sparse Core Ops, SparseCore 0:
  158.1 25.6 all-gather.1
  207.4 41.0 reduce-scatter.2
  270.3 63.4 reduce-scatter.4
